TPU v7x, 128 devices: a whole 4x4x4 slice. The times are simulated.
128 devices in a mesh: line: 16 (over z, x_lo, core), col: 8 (over x_hi, y).
Axes of the slice: x: 4 (x_hi: 2, x_lo: 2; x = x_hi * 2 + x_lo), y: 4, z: 4, core: 2. Of those that a mesh axis runs over, the one named last changes fastest.
Arguments:
- ptdf: bfloat16 [12288, 36864], P('line', 'col'), may hold values from -0.03125 to 0.03125
- lodf: bfloat16 [12288, 12288], P('line', 'col'), may hold values from -3.296875 to 3.296875
- injection: float32 [512, 36864], P('line', 'col'), may hold values from 0 to 1
- injection_prev: float32 [512, 36864], P('line', 'col'), may hold values from 0 to 1
- bus_cost: float32 [36864], P('col'), may hold values from -1 to 1
- bus_cap: float32 [36864], P('col'), may hold values from 0.5 to 2
- demand: float32 [512], P('line'), may hold values from 12902.4 to 23961.6
- balance_dual: float32 [512], P('line'), may hold values from -3 to 3
- base_dual: float32 [512, 12288], P(None, 'line'), may hold values from -3 to 3
- post_dual: float32 [512, 12288], P(None, 'line'), may hold values from -3 to 3
- flow_limit: float32 [12288], P('line'), may hold values from 0.3 to 2
- emergency_limit: float32 [12288], P('line'), may hold values from 0.4 to 2.5
- outage_line: int32 [12288], P('col'), may hold values from 0 to 12287, each once
- outage_weight: float32 [12288], P('col'), may hold values from 0.004961604 to 0.059539247
Outputs:
- new_injection: float32 [512, 36864], P('line', 'col')
- balance_new: float32 [512], P('line')
- base_new: float32 [512, 12288], P(None, 'line')
- post_new: float32 [512, 12288], P(None, 'line')
Inputs may be any that keep to these rules, and one draw needn't show every extreme that they name: `outage_line`: a permutation: every line is the outage of exactly one contingency.
All inputs are finite; a program needn't handle non-finite values.
Results may differ from a plain program's by a relative error of at most 0.0075.
Values may be sent and summed in bfloat16 or wider, within the bound.
No kernel may reach another device: no remote copies, remote signals or barrier semaphores. Data moves between devices by JAX's collectives and lax.ppermute only.
A program may use at most 192 MiB of HBM per device.

v0:
```python
import jax
import jax.numpy as jnp
from jax import lax
from jax.sharding import PartitionSpec as P

BUSES = 36864


dual_step = 0.5
primal_step = 0.5


def dual_update(dual, flow, limit):
    shifted = dual + dual_step * flow
    return shifted - dual_step * jnp.clip(shifted / dual_step, -limit, limit)


def on_device(
    ptdf,
    lodf,
    injection,
    injection_prev,
    bus_cost,
    bus_cap,
    demand,
    balance_dual,
    base_dual,
    post_dual,
    flow_limit,
    emergency_limit,
    outage_line,
    outage_weight,
):
    extrapolated = 2.0 * injection - injection_prev
    extra_high = extrapolated.astype(jnp.bfloat16)
    extra_low = (extrapolated - extra_high.astype(jnp.float32)).astype(jnp.bfloat16)
    stacked = jnp.stack([extra_high, extra_low], axis=0)
    lines_dev = ptdf.shape[0]
    ptdf_turned = ptdf.T
    portion = lax.all_gather(stacked, "line", axis=1, tiled=True)
    count = portion.shape[1]
    flat = portion.reshape(2 * count, portion.shape[2])
    product = jnp.dot(flat, ptdf_turned, preferred_element_type=jnp.float32)
    flow_part = product[:count] + product[count:]
    local_total = jnp.sum(extra_high.astype(jnp.float32) + extra_low.astype(jnp.float32), axis=1)
    bus_total = lax.psum(local_total, "col")
    base_flow = lax.psum(flow_part, "col")
    balance_new = balance_dual + (bus_total - demand) / BUSES
    base_new = dual_update(base_dual, base_flow, flow_limit[None, :])
    first_line = lax.axis_index("line") * lines_dev
    local_line = outage_line - first_line
    inside = (local_line >= 0) & (local_line < lines_dev)
    all_flows = lax.all_gather(base_flow, "line", axis=1, tiled=True)
    picked = jnp.take(all_flows, outage_line, axis=1)
    outage_flow = (picked * outage_weight[None, :]).astype(jnp.bfloat16)
    shift_part = jnp.dot(outage_flow, lodf.T, preferred_element_type=jnp.float32)
    post_shift = lax.psum(shift_part, "col")
    post_flow = base_flow + post_shift
    post_new = dual_update(post_dual, post_flow, emergency_limit[None, :])
    back_part = jnp.dot(post_new.astype(jnp.bfloat16), lodf, preferred_element_type=jnp.float32)
    back_flow = lax.psum(back_part, "line")
    target = jnp.where(inside, local_line, lines_dev)
    returned_part = (
        jnp.zeros(base_new.shape, jnp.float32)
        .at[:, target]
        .add(back_flow * outage_weight[None, :], mode="drop")
    )
    returned = lax.psum(returned_part, "col")
    line_total = (base_new + post_new + returned).astype(jnp.bfloat16)
    prices = lax.psum_scatter(
        jnp.dot(line_total, ptdf, preferred_element_type=jnp.float32),
        "line",
        scatter_dimension=0,
        tiled=True,
    )
    moved = injection - primal_step * (bus_cost[None, :] + prices + balance_new[:, None])
    new_injection = jnp.clip(moved, 0.0, bus_cap[None, :])
    return (new_injection, balance_new, base_new, post_new)


def solution(mesh):
    in_specs = (
        P("line", "col"),
        P("line", "col"),
        P("line", "col"),
        P("line", "col"),
        P("col"),
        P("col"),
        P("line"),
        P("line"),
        P(None, "line"),
        P(None, "line"),
        P("line"),
        P("line"),
        P("col"),
        P("col"),
    )
    out_specs = (P("line", "col"), P("line"), P(None, "line"), P(None, "line"))
    return jax.shard_map(
        on_device, mesh=mesh, in_specs=in_specs, out_specs=out_specs, check_vma=False
    )
```

profile of v0, /device:TPU:1, one launch (start us, length us, event | category | flops | bytes accessed | tf_op | source)
XLA Modules:
  0.0 810.0 jit_solution(6875233746082250814)
XLA Ops:
  7.2 0.0 copy-start
  7.2 0.0 all-gather.3.cloned.1.call-start
  7.2 1.6 fusion.13
  8.8 0.9 pad_maximum_fusion
  9.7 0.0 all-gather.3.cloned.1.call-update
  9.7 0.0 all-reduce.5.cloned.1.call-start
  9.8 61.1 %all-gather.3.cloned.1.call-done = bf16[2,512,4608]{2,1,0:T(8,128)(2,1)} async-done(((bf16[2,32,4608]{2,1,0:T(8,128)(2,1)}), bf16[2,512,4608]{2,1,0:T(8,128)(2,1)}) %all-gather.3.cloned.1.call-update) | async-done | bytes 9437200 | tf_op jit(solution)/shard_map/all_gather | solution.py:40
  70.9 12.1 %fusion.16 = f32[1024,768]{1,0:T(8,128)S(1)} fusion(bf16[1024,4608]{1,0:T(8,128)(2,1)} %bitcast.13, bf16[768,4608]{1,0:T(8,128)(2,1)} %param.14), kind=kOutput, calls=%fused_computation.34 | convolution fusion | flops 7247757312 | bytes 19660800 | tf_op jit(solution)/shard_map/dot_general | solution.py:43
  83.0 1.3 slice_add_fusion
  84.4 0.0 all-reduce.5.cloned.1.call-update
  84.4 0.0 all-gather.5.cloned.1.call-start
  84.5 85.5 %all-reduce.5.cloned.1.call-done = f32[512,768]{1,0:T(8,128)} async-done(((f32[512,768]{1,0:T(8,128)}), f32[512,768]{1,0:T(8,128)}) %all-reduce.5.cloned.1.call-update) | async-done | bytes 1572880 | tf_op jit(solution)/shard_map/psum | solution.py:47
  170.0 0.0 all-gather.5.cloned.1.call-update
  170.0 0.0 all-reduce.7.cloned.1.call-start
  170.0 0.0 copy-done.3
  170.1 136.5 %all-gather.5.cloned.1.call-done = f32[512,12288]{1,0:T(8,128)} async-done(((f32[512,768]{1,0:T(8,128)}), f32[512,12288]{1,0:T(8,128)}) %all-gather.5.cloned.1.call-update) | async-done | bytes 25165840 | tf_op jit(solution)/shard_map/all_gather | solution.py:53
  306.6 24.7 %copy.18 = f32[512,12288]{0,1:T(8,128)} copy(f32[512,12288]{1,0:T(8,128)} %all-gather.5.cloned.1.call-done) | data formatting | bytes 50331648 | tf_op jit(solution)/shard_map/all_gather | solution.py:53
  331.3 13.9 %gather_fusion = f32[1536,512]{1,0:T(8,128)} fusion(f32[512,12288]{0,1:T(8,128)} %copy.18, s32[2048]{0:T(1024)S(1)} %pad_clamp_fusion), kind=kCustom, calls=%fused_computation | custom fusion | bytes 6297600 | tf_op jit(solution)/shard_map/jit(_take)/gather | solution.py:54
  345.2 0.0 copy-done
  345.2 0.0 copy-done.8
  345.2 4.9 fusion.3
  350.1 0.0 all-reduce.7.cloned.1.call-update
  350.1 0.0 all-reduce.9.cloned.1.call-start
  350.2 0.6 copy-done.6
  350.8 0.0 copy-done.7
  350.8 84.8 %all-reduce.7.cloned.1.call-done = f32[512,768]{1,0:T(8,128)} async-done(((f32[512,768]{1,0:T(8,128)}), f32[512,768]{1,0:T(8,128)}) %all-reduce.7.cloned.1.call-update) | async-done | bytes 1572880 | tf_op jit(solution)/shard_map/psum | solution.py:57
  435.6 4.7 multiply_subtract_fusion.1
  440.3 1.1 copy-done.1
  441.5 3.1 fusion.9
  444.6 0.0 all-reduce.9.cloned.1.call-update
  444.6 0.0 all-reduce.11.cloned.1.call-start
  444.7 132.7 %all-reduce.9.cloned.1.call-done = f32[512,1536]{0,1:T(8,128)} async-done(((f32[512,1536]{0,1:T(8,128)}), f32[512,1536]{0,1:T(8,128)}) %all-reduce.9.cloned.1.call-update) | async-done | bytes 3145744 | tf_op jit(solution)/shard_map/psum | solution.py:61
  577.4 12.2 %scatter_custom_fusion = f32[512,768]{0,1:T(8,128)} fusion(s32[1536]{0:T(1024)S(1)} %get-tuple-element.10, f32[512,1536]{0,1:T(8,128)} %all-reduce.9.cloned.1.call-done, f32[1536]{0:T(1024)S(1)} %copy-done.8, f32[]{:T(128)} %constant.11.clone.1), kind=kCustom, calls=%fused_computation.2 | custom fusion | flops 1572864 | bytes 4726788 | tf_op jit(solution)/shard_map/scatter-add | solution.py:66
  589.6 3.0 copy.19
  592.6 0.0 all-reduce.11.cloned.1.call-update
  592.7 0.2 reduce-scatter.2.cloned.1.call-start
  592.9 85.9 %all-reduce.11.cloned.1.call-done = f32[512,768]{1,0:T(8,128)} async-done(((f32[512,768]{1,0:T(8,128)}), f32[512,768]{1,0:T(8,128)}) %all-reduce.11.cloned.1.call-update) | async-done | bytes 1572880 | tf_op jit(solution)/shard_map/psum | solution.py:68
  678.8 11.9 %fusion.8 = f32[512,4608]{1,0:T(8,128)} fusion(bf16[768,4608]{1,0:T(8,128)(2,1)} %param.14, f32[512,768]{1,0:T(8,128)} %all-reduce.11.cloned.1.call-done, f32[512,768]{1,0:T(8,128)} %get-tuple-element.4, f32[512,768]{1,0:T(8,128)} %copy-done.1), kind=kOutput, calls=%fused_computation.15 | convolution fusion | flops 3625058304 | bytes 21233664 | tf_op jit(solution)/shard_map/dot_general | solution.py:71
  690.7 0.0 copy-start.5
  690.7 0.0 reduce-scatter.2.cloned.1.call-update
  690.7 18.1 %psum.39 = f32[32]{0:T(128)S(1)} all-reduce(f32[32]{0:T(128)S(1)} %get-tuple-element.6), channel_id=1, replica_groups=mesh['line'=16,'col'=8] {'col'}, use_global_device_ids=true, to_apply=%region_7.8 | all-reduce | flops 32 | bytes 256 | tf_op jit(solution)/shard_map/psum | solution.py:46
  708.9 0.0 copy-done.10
  708.9 0.0 copy-done.11
  708.9 0.0 copy-start.9
  708.9 92.2 %reduce-scatter.2.cloned.1.call-done = f32[32,4608]{1,0:T(8,128)} async-done(((f32[512,4608]{1,0:T(8,128)}), f32[32,4608]{1,0:T(8,128)}) %reduce-scatter.2.cloned.1.call-update) | async-done | bytes 589840 | tf_op jit(solution)/shard_map/reduce_scatter | solution.py:70
  801.1 0.0 copy-done.2
  801.1 0.0 copy-done.4
  801.1 2.1 maximum_minimum_fusion
  (17 shorter events, 0.1 us)
Async XLA Ops:
  7.2 338.0 %copy-start = (bf16[768,1536]{1,0:T(8,128)(2,1)S(1)}, bf16[768,1536]{1,0:T(8,128)(2,1)}, u32[]{:S(2)}) copy-start(bf16[768,1536]{1,0:T(8,128)(2,1)} %param.15) | copy-start | bytes 7077892
  7.2 63.7 %all-gather.3.cloned.1.call-start = ((), (), s32[]{:S(2)}) async-start(), calls=%async_computation.1 | async-start | bytes 10027008 | tf_op jit(solution)/shard_map/all_gather | solution.py:40
  9.7 160.2 %all-reduce.5.cloned.1.call-start = ((), (), s32[]{:S(2)}) async-start(), calls=%async_computation.2 | async-start | bytes 3145728 | tf_op jit(solution)/shard_map/psum | solution.py:47
  84.4 85.7 %copy-start.3 = (s32[1536]{0:T(1024)S(1)}, s32[1536]{0:T(1024)}, u32[]{:S(2)}) copy-start(s32[1536]{0:T(1024)} %param.26) | copy-start | bytes 18436
  84.4 222.2 %all-gather.5.cloned.1.call-start = ((), (), s32[]{:S(2)}) async-start(), calls=%async_computation.3 | async-start | bytes 26738688 | tf_op jit(solution)/shard_map/all_gather | solution.py:53
  170.0 265.6 %all-reduce.7.cloned.1.call-start = ((), (), s32[]{:S(2)}) async-start(), calls=%async_computation.4 | async-start | bytes 3145728 | tf_op jit(solution)/shard_map/psum | solution.py:57
  331.3 13.9 %copy-start.8 = (f32[1536]{0:T(1024)S(1)}, f32[1536]{0:T(1024)}, u32[]{:S(2)}) copy-start(f32[1536]{0:T(1024)} %param.27) | copy-start | bytes 18436
  350.1 0.7 copy-start.6
  350.1 0.7 copy-start.7
  350.1 227.3 %all-reduce.9.cloned.1.call-start = ((), (), s32[]{:S(2)}) async-start(), calls=%async_computation.5 | async-start | bytes 6291456 | tf_op jit(solution)/shard_map/psum | solution.py:61
  440.3 1.1 copy-start.1
  444.6 234.2 %all-reduce.11.cloned.1.call-start = ((), (), s32[]{:S(2)}) async-start(), calls=%async_computation.6 | async-start | bytes 3145728 | tf_op jit(solution)/shard_map/psum | solution.py:68
  592.7 208.4 %reduce-scatter.2.cloned.1.call-start = ((), (), s32[]{:S(2)}) async-start(), calls=%async_computation.7 | async-start | bytes 10027008 | tf_op jit(solution)/shard_map/reduce_scatter | solution.py:70
  690.7 18.2 %copy-start.10 = (f32[32]{0:T(128)S(1)}, f32[32]{0:T(128)}, u32[]{:S(2)}) copy-start(f32[32]{0:T(128)} %param.21) | copy-start | bytes 388
  690.7 18.2 %copy-start.11 = (f32[32]{0:T(128)S(1)}, f32[32]{0:T(128)}, u32[]{:S(2)}) copy-start(f32[32]{0:T(128)} %param.20) | copy-start | bytes 388
  690.7 110.4 %copy-start.2 = (f32[32,4608]{1,0:T(8,128)S(1)}, f32[32,4608]{1,0:T(8,128)}, u32[]{:S(2)}) copy-start(f32[32,4608]{1,0:T(8,128)} %param.16) | copy-start | bytes 1769476
  690.7 110.4 %copy-start.4 = (f32[4608]{0:T(1024)S(1)}, f32[4608]{0:T(1024)}, u32[]{:S(2)}) copy-start(f32[4608]{0:T(1024)} %param.18) | copy-start | bytes 55300
  690.7 110.4 %copy-start.5 = (f32[4608]{0:T(1024)S(1)}, f32[4608]{0:T(1024)}, u32[]{:S(2)}) copy-start(f32[4608]{0:T(1024)} %param.19) | copy-start | bytes 55300
  708.9 94.3 %copy-start.9 = (f32[32]{0:T(128)}, f32[32]{0:T(128)S(1)}, u32[]{:S(2)}) copy-start(f32[32]{0:T(128)S(1)} %multiply_add_fusion) | copy-start | bytes 388
Sparse Core Ops, SparseCore 0:
  10.2 60.6 all-gather.2
  84.5 85.3 all-reduce.4
  171.6 134.9 all-gather.4
  350.2 85.3 all-reduce.6
  444.7 132.5 all-reduce.8
  592.8 85.9 all-reduce.10
  690.9 110.1 reduce-scatter.1
where the time goes:
time: 812 us; the launch traced here: 810 us
  waiting for transfers between devices  679 us (84%)
  local copies, waits for them, and re-layouts  43.4 us (5%)
  matrix products  32.1 us (4%)
  other arithmetic  22.9 us (3%)
  blocking collectives  18.1 us (2%)
  between operations  14.2 us (2%)
    all_gather x1, waiting for transfers between devices, on_device(): all_flows = lax.all_gather(base_flow, 'line', axis=1, tiled=True)  136 us
    psum x1, waiting for transfers between devices, on_device(): back_flow = lax.psum(back_part, 'line')  133 us
    reduce_scatter x1, waiting for transfers between devices, on_device(): lax.psum_scatter(jnp.dot(line_total, ptdf, preferred_element_type=jnp.flo...  92.2 us
    psum x1, waiting for transfers between devices, on_device(): returned = lax.psum(returned_part, 'col')  85.9 us
    psum x1, waiting for transfers between devices, on_device(): base_flow = lax.psum(flow_part, 'col')  85.5 us
    psum x1, waiting for transfers between devices, on_device(): post_shift = lax.psum(shift_part, 'col')  84.8 us
    all_gather x1, waiting for transfers between devices, on_device(): portion = lax.all_gather(stacked, 'line', axis=1, tiled=True)  61.1 us
    all_gather x1, local copies, waits for them, and re-layouts, on_device(): all_flows = lax.all_gather(base_flow, 'line', axis=1, tiled=True)  24.7 us
  transfers between devices with their start and end apart: 7, of which 7 were waited for; matrix products, arithmetic and copies ran while one was open for 0% of the time, Pallas kernels for 0%

commit v1 on v0

--- a/solution.py
+++ b/solution.py
@@ -50,9 +50,11 @@
     first_line = lax.axis_index("line") * lines_dev
     local_line = outage_line - first_line
     inside = (local_line >= 0) & (local_line < lines_dev)
-    all_flows = lax.all_gather(base_flow, "line", axis=1, tiled=True)
-    picked = jnp.take(all_flows, outage_line, axis=1)
-    outage_flow = (picked * outage_weight[None, :]).astype(jnp.bfloat16)
+    safe_line = jnp.where(inside, local_line, 0)
+    picked = jnp.take(base_flow, safe_line, axis=1)
+    weighted = jnp.where(inside[None, :], picked * outage_weight[None, :], 0.0)
+    pieces = lax.psum_scatter(weighted.astype(jnp.bfloat16), "line", scatter_dimension=0, tiled=True)
+    outage_flow = lax.all_gather(pieces, "line", axis=0, tiled=True)
     shift_part = jnp.dot(outage_flow, lodf.T, preferred_element_type=jnp.float32)
     post_shift = lax.psum(shift_part, "col")
     post_flow = base_flow + post_shift

time: 812 us -> 751 us (0.925)
  waiting for transfers between devices: 679 us -> 640 us
  local copies, waits for them, and re-layouts: 43.4 us -> 18.2 us
    all_gather x1, waiting for transfers between devices: 136 us -> 36.8 us  [on_device(): outage_flow = lax.all_gather(pieces, 'line', axis=0, tiled=True)]
    reduce_scatter x0 -> x1, waiting for transfers between devices: none -> 63.8 us  [on_device(): lax.psum_scatter(weighted.astype(jnp.bfloat16), 'line', scatter_dimension...]
    all_gather x1 -> x0, local copies, waits for them, and re-layouts: 24.7 us -> none  [on_device(): all_flows = lax.all_gather(base_flow, 'line', axis=1, tiled=True)]
  transfers between devices with their start and end apart: 7 -> 8, of which waited for: 7 -> 8; matrix products, arithmetic and copies ran while one was open for 0% -> 0% of each run, Pallas kernels for 0% -> 0%
where the time goes in v1:
time: 751 us; the launch traced here: 749 us
  waiting for transfers between devices  640 us (85%)
  matrix products  31.3 us (4%)
  other arithmetic  26.4 us (4%)
  local copies, waits for them, and re-layouts  18.2 us (2%)
  blocking collectives  18.1 us (2%)
  between operations  14.2 us (2%)
    psum x1, waiting for transfers between devices, on_device(): back_flow = lax.psum(back_part, 'line')  132 us
    reduce_scatter x1, waiting for transfers between devices, on_device(): lax.psum_scatter(jnp.dot(line_total, ptdf, preferred_element_type=jnp.flo...  92.2 us
    psum x1, waiting for transfers between devices, on_device(): returned = lax.psum(returned_part, 'col')  85.9 us
    psum x1, waiting for transfers between devices, on_device(): base_flow = lax.psum(flow_part, 'col')  84.9 us
    psum x1, waiting for transfers between devices, on_device(): post_shift = lax.psum(shift_part, 'col')  83.5 us
    reduce_scatter x1, waiting for transfers between devices, on_device(): lax.psum_scatter(weighted.astype(jnp.bfloat16), 'line', scatter_dimension...  63.8 us
    all_gather x1, waiting for transfers between devices, on_device(): portion = lax.all_gather(stacked, 'line', axis=1, tiled=True)  61.1 us
    all_gather x1, waiting for transfers between devices, on_device(): outage_flow = lax.all_gather(pieces, 'line', axis=0, tiled=True)  36.8 us
  transfers between devices with their start and end apart: 8, of which 8 were waited for; matrix products, arithmetic and copies ran while one was open for 0% of the time, Pallas kernels for 0%

profile of v1, /device:TPU:1, one launch (start us, length us, event | category | flops | bytes accessed | tf_op | source)
XLA Modules:
  0.0 749.1 jit_solution(5636638106736619497)
XLA Ops:
  7.2 0.0 copy-start
  7.2 0.0 all-gather.3.cloned.1.call-start
  7.2 1.6 fusion.10
  8.8 0.9 pad_maximum_fusion
  9.7 0.0 all-gather.3.cloned.1.call-update
  9.7 0.0 all-reduce.5.cloned.1.call-start
  9.8 61.1 %all-gather.3.cloned.1.call-done = bf16[2,512,4608]{2,1,0:T(8,128)(2,1)} async-done(((bf16[2,32,4608]{2,1,0:T(8,128)(2,1)}), bf16[2,512,4608]{2,1,0:T(8,128)(2,1)}) %all-gather.3.cloned.1.call-update) | async-done | bytes 9437200 | tf_op jit(solution)/shard_map/all_gather | solution.py:40
  70.9 12.1 %fusion.12 = f32[1024,768]{1,0:T(8,128)S(1)} fusion(bf16[1024,4608]{1,0:T(8,128)(2,1)} %bitcast.17, bf16[768,4608]{1,0:T(8,128)(2,1)} %param.14), kind=kOutput, calls=%fused_computation.31 | convolution fusion | flops 7247757312 | bytes 19660800 | tf_op jit(solution)/shard_map/dot_general | solution.py:43
  83.0 1.3 slice_add_fusion
  84.4 0.0 all-reduce.5.cloned.1.call-update
  84.4 0.0 reduce-scatter.7.cloned.1.call-start
  84.5 0.6 copy-done.4
  85.1 84.9 %all-reduce.5.cloned.1.call-done = f32[512,768]{1,0:T(8,128)} async-done(((f32[512,768]{1,0:T(8,128)}), f32[512,768]{1,0:T(8,128)}) %all-reduce.5.cloned.1.call-update) | async-done | bytes 1572880 | tf_op jit(solution)/shard_map/psum | solution.py:47
  170.0 3.0 copy.20
  173.0 7.1 gather_fusion
  180.1 3.5 fusion.3
  183.6 2.6 copy.23
  186.2 0.0 reduce-scatter.7.cloned.1.call-update
  186.2 0.0 all-gather.5.cloned.1.call-start
  186.3 63.8 %reduce-scatter.7.cloned.1.call-done = bf16[32,1536]{1,0:T(8,128)(2,1)} async-done(((bf16[512,1536]{1,0:T(8,128)(2,1)}), bf16[32,1536]{1,0:T(8,128)(2,1)}) %reduce-scatter.7.cloned.1.call-update) | async-done | bytes 98320 | tf_op jit(solution)/shard_map/reduce_scatter | solution.py:56
  250.1 0.0 all-gather.5.cloned.1.call-update
  250.1 0.0 all-reduce.7.cloned.1.call-start
  250.1 36.8 %all-gather.5.cloned.1.call-done = bf16[512,1536]{1,0:T(8,128)(2,1)} async-done(((bf16[32,1536]{1,0:T(8,128)(2,1)}), bf16[512,1536]{1,0:T(8,128)(2,1)}) %all-gather.5.cloned.1.call-update) | async-done | bytes 1572880 | tf_op jit(solution)/shard_map/all_gather | solution.py:57
  286.9 4.0 fusion.13
  290.9 0.0 all-reduce.7.cloned.1.call-update
  290.9 0.0 all-reduce.9.cloned.1.call-start
  290.9 0.6 copy-done.7
  291.6 0.0 copy-done.8
  291.6 83.5 %all-reduce.7.cloned.1.call-done = f32[512,768]{1,0:T(8,128)} async-done(((f32[512,768]{1,0:T(8,128)}), f32[512,768]{1,0:T(8,128)}) %all-reduce.7.cloned.1.call-update) | async-done | bytes 1572880 | tf_op jit(solution)/shard_map/psum | solution.py:59
  375.1 4.7 multiply_subtract_fusion.1
  379.8 1.1 copy-done.1
  381.0 3.1 fusion.6
  384.1 0.0 all-reduce.9.cloned.1.call-update
  384.1 0.0 all-reduce.11.cloned.1.call-start
  384.2 132.1 %all-reduce.9.cloned.1.call-done = f32[512,1536]{0,1:T(8,128)} async-done(((f32[512,1536]{0,1:T(8,128)}), f32[512,1536]{0,1:T(8,128)}) %all-reduce.9.cloned.1.call-update) | async-done | bytes 3145744 | tf_op jit(solution)/shard_map/psum | solution.py:63
  516.3 12.2 %scatter_custom_fusion = f32[512,768]{0,1:T(8,128)} fusion(s32[1536]{0:T(1024)S(1)} %compare_select_fusion, f32[512,1536]{0,1:T(8,128)} %all-reduce.9.cloned.1.call-done, f32[1536]{0:T(1024)S(1)} %copy-done.3, f32[]{:T(128)} %constant.11.clone.1), kind=kCustom, calls=%fused_computation.2 | custom fusion | flops 1572864 | bytes 4726788 | tf_op jit(solution)/shard_map/scatter-add | solution.py:68
  528.5 3.0 copy.22
  531.6 0.0 all-reduce.11.cloned.1.call-update
  531.6 0.2 reduce-scatter.5.cloned.1.call-start
  531.8 85.9 %all-reduce.11.cloned.1.call-done = f32[512,768]{1,0:T(8,128)} async-done(((f32[512,768]{1,0:T(8,128)}), f32[512,768]{1,0:T(8,128)}) %all-reduce.11.cloned.1.call-update) | async-done | bytes 1572880 | tf_op jit(solution)/shard_map/psum | solution.py:70
  617.7 12.0 %fusion.5 = f32[512,4608]{1,0:T(8,128)} fusion(bf16[768,4608]{1,0:T(8,128)(2,1)} %param.14, f32[512,768]{1,0:T(8,128)} %all-reduce.11.cloned.1.call-done, f32[512,768]{1,0:T(8,128)} %get-tuple-element.6, f32[512,768]{1,0:T(8,128)} %copy-done.1), kind=kOutput, calls=%fused_computation.12 | convolution fusion | flops 3625058304 | bytes 21233664 | tf_op jit(solution)/shard_map/dot_general | solution.py:73
  629.8 0.0 copy-start.6
  629.8 0.0 reduce-scatter.5.cloned.1.call-update
  629.8 18.1 %psum.39 = f32[32]{0:T(128)S(1)} all-reduce(f32[32]{0:T(128)S(1)} %get-tuple-element.8), channel_id=1, replica_groups=mesh['line'=16,'col'=8] {'col'}, use_global_device_ids=true, to_apply=%region_8.9 | all-reduce | flops 32 | bytes 256 | tf_op jit(solution)/shard_map/psum | solution.py:46
  647.9 0.0 copy-done.11
  647.9 0.0 copy-start.9
  648.0 92.2 %reduce-scatter.5.cloned.1.call-done = f32[32,4608]{1,0:T(8,128)} async-done(((f32[512,4608]{1,0:T(8,128)}), f32[32,4608]{1,0:T(8,128)}) %reduce-scatter.5.cloned.1.call-update) | async-done | bytes 589840 | tf_op jit(solution)/shard_map/reduce_scatter | solution.py:72
  740.2 2.1 maximum_minimum_fusion
  (22 shorter events, 0.1 us)
Async XLA Ops:
  7.2 279.7 %copy-start = (bf16[768,1536]{1,0:T(8,128)(2,1)S(1)}, bf16[768,1536]{1,0:T(8,128)(2,1)}, u32[]{:S(2)}) copy-start(bf16[768,1536]{1,0:T(8,128)(2,1)} %param.15) | copy-start | bytes 7077892
  7.2 63.7 %all-gather.3.cloned.1.call-start = ((), (), s32[]{:S(2)}) async-start(), calls=%async_computation.2 | async-start | bytes 10027008 | tf_op jit(solution)/shard_map/all_gather | solution.py:40
  9.7 160.2 %all-reduce.5.cloned.1.call-start = ((), (), s32[]{:S(2)}) async-start(), calls=%async_computation.3 | async-start | bytes 3145728 | tf_op jit(solution)/shard_map/psum | solution.py:47
  84.4 0.7 copy-start.4
  84.4 165.7 %reduce-scatter.7.cloned.1.call-start = ((), (), s32[]{:S(2)}) async-start(), calls=%async_computation.9 | async-start | bytes 1671168 | tf_op jit(solution)/shard_map/reduce_scatter | solution.py:56
  173.0 7.2 copy-start.3
  186.2 100.7 %all-gather.5.cloned.1.call-start = ((), (), s32[]{:S(2)}) async-start(), calls=%async_computation.4 | async-start | bytes 1671168 | tf_op jit(solution)/shard_map/all_gather | solution.py:57
  250.1 125.0 %all-reduce.7.cloned.1.call-start = ((), (), s32[]{:S(2)}) async-start(), calls=%async_computation.5 | async-start | bytes 3145728 | tf_op jit(solution)/shard_map/psum | solution.py:59
  290.9 0.7 copy-start.7
  290.9 0.7 copy-start.8
  290.9 225.4 %all-reduce.9.cloned.1.call-start = ((), (), s32[]{:S(2)}) async-start(), calls=%async_computation.6 | async-start | bytes 6291456 | tf_op jit(solution)/shard_map/psum | solution.py:63
  379.8 1.1 copy-start.1
  384.1 233.6 %all-reduce.11.cloned.1.call-start = ((), (), s32[]{:S(2)}) async-start(), calls=%async_computation.7 | async-start | bytes 3145728 | tf_op jit(solution)/shard_map/psum | solution.py:70
  531.6 208.6 %reduce-scatter.5.cloned.1.call-start = ((), (), s32[]{:S(2)}) async-start(), calls=%async_computation.8 | async-start | bytes 10027008 | tf_op jit(solution)/shard_map/reduce_scatter | solution.py:72
  629.7 18.2 %copy-start.10 = (f32[32]{0:T(128)S(1)}, f32[32]{0:T(128)}, u32[]{:S(2)}) copy-start(f32[32]{0:T(128)} %param.21) | copy-start | bytes 388
  629.7 18.2 %copy-start.11 = (f32[32]{0:T(128)S(1)}, f32[32]{0:T(128)}, u32[]{:S(2)}) copy-start(f32[32]{0:T(128)} %param.20) | copy-start | bytes 388
  629.8 110.4 %copy-start.2 = (f32[32,4608]{1,0:T(8,128)S(1)}, f32[32,4608]{1,0:T(8,128)}, u32[]{:S(2)}) copy-start(f32[32,4608]{1,0:T(8,128)} %param.16) | copy-start | bytes 1769476
  629.8 110.4 %copy-start.5 = (f32[4608]{0:T(1024)S(1)}, f32[4608]{0:T(1024)}, u32[]{:S(2)}) copy-start(f32[4608]{0:T(1024)} %param.18) | copy-start | bytes 55300
  629.8 110.4 %copy-start.6 = (f32[4608]{0:T(1024)S(1)}, f32[4608]{0:T(1024)}, u32[]{:S(2)}) copy-start(f32[4608]{0:T(1024)} %param.19) | copy-start | bytes 55300
  647.9 94.3 %copy-start.9 = (f32[32]{0:T(128)}, f32[32]{0:T(128)S(1)}, u32[]{:S(2)}) copy-start(f32[32]{0:T(128)S(1)} %multiply_add_fusion) | copy-start | bytes 388
Sparse Core Ops, SparseCore 0:
  10.2 60.6 all-gather.2
  84.5 85.3 all-reduce.4
  186.3 63.6 reduce-scatter.6
  251.6 35.2 all-gather.4
  291.0 84.0 all-reduce.6
  384.2 132.0 all-reduce.8
  531.7 85.9 all-reduce.10
  629.9 110.1 reduce-scatter.4

commit v2 on v1

v2 whole, which is shorter than its diff:
```python
import jax
import jax.numpy as jnp
from jax import lax
from jax.sharding import PartitionSpec as P

BUSES = 36864
CHUNKS = 2


dual_step = 0.5
primal_step = 0.5


def dual_update(dual, flow, limit):
    shifted = dual + dual_step * flow
    return shifted - dual_step * jnp.clip(shifted / dual_step, -limit, limit)


def tie(value, previous):
    if previous is None:
        return value
    value, _ = lax.optimization_barrier((value, previous))
    return value


def pipeline(
    extra_high,
    extra_low,
    injection,
    bus_cost,
    bus_cap,
    balance_new,
    base_dual,
    post_dual,
    flow_limit,
    emergency_limit,
    ptdf,
    lodf,
    inside,
    safe_line,
    target,
    outage_weight,
):
    chunks = range(len(extra_high))
    base_flow, outage_flow, post_new, base_new, back_flow, returned = [], [], [], [], [], []
    last_col = None
    for c in chunks:
        stacked = jnp.stack([extra_high[c], extra_low[c]], axis=0)
        portion = lax.all_gather(stacked, "line", axis=1, tiled=True)
        count = portion.shape[1]
        flat = portion.reshape(2 * count, portion.shape[2])
        product = jnp.dot(flat, ptdf.T, preferred_element_type=jnp.float32)
        flow_part = product[:count] + product[count:]
        last_col = lax.psum(tie(flow_part, last_col), "col")
        base_flow.append(last_col)
    for c in chunks:
        base_new.append(dual_update(base_dual[c], base_flow[c], flow_limit[None, :]))
        picked = jnp.take(base_flow[c], safe_line, axis=1)
        weighted = jnp.where(inside[None, :], picked * outage_weight[None, :], 0.0)
        pieces = lax.psum_scatter(weighted.astype(jnp.bfloat16), "line", scatter_dimension=0, tiled=True)
        outage_flow.append(lax.all_gather(pieces, "line", axis=0, tiled=True))
    for c in chunks:
        shift_part = jnp.dot(outage_flow[c], lodf.T, preferred_element_type=jnp.float32)
        post_shift = lax.psum(tie(shift_part, last_col), "col")
        last_col = post_shift
        post_flow = base_flow[c] + post_shift
        post_new.append(dual_update(post_dual[c], post_flow, emergency_limit[None, :]))
    for c in chunks:
        back_part = jnp.dot(post_new[c].astype(jnp.bfloat16), lodf, preferred_element_type=jnp.float32)
        back_flow.append(lax.psum(tie(back_part, back_flow[c - 1] if c else None), "line"))
    for c in chunks:
        returned_part = (
            jnp.zeros(base_new[c].shape, jnp.float32)
            .at[:, target]
            .add(back_flow[c] * outage_weight[None, :], mode="drop")
        )
        last_col = lax.psum(tie(returned_part, last_col), "col")
        returned.append(last_col)
    new_injection = []
    for c in chunks:
        line_total = (base_new[c] + post_new[c] + returned[c]).astype(jnp.bfloat16)
        prices = lax.psum_scatter(
            jnp.dot(line_total, ptdf, preferred_element_type=jnp.float32),
            "line",
            scatter_dimension=0,
            tiled=True,
        )
        moved = injection[c] - primal_step * (bus_cost[None, :] + prices + balance_new[c][:, None])
        new_injection.append(jnp.clip(moved, 0.0, bus_cap[None, :]))
    return new_injection, base_new, post_new


def on_device(
    ptdf,
    lodf,
    injection,
    injection_prev,
    bus_cost,
    bus_cap,
    demand,
    balance_dual,
    base_dual,
    post_dual,
    flow_limit,
    emergency_limit,
    outage_line,
    outage_weight,
):
    extrapolated = 2.0 * injection - injection_prev
    extra_high = extrapolated.astype(jnp.bfloat16)
    extra_low = (extrapolated - extra_high.astype(jnp.float32)).astype(jnp.bfloat16)
    local_total = jnp.sum(extra_high.astype(jnp.float32) + extra_low.astype(jnp.float32), axis=1)
    bus_total = lax.psum(local_total, "col")
    balance_new = balance_dual + (bus_total - demand) / BUSES

    lines_dev = ptdf.shape[0]
    line_devs = lax.axis_size("line")
    first_line = lax.axis_index("line") * lines_dev
    local_line = outage_line - first_line
    inside = (local_line >= 0) & (local_line < lines_dev)
    safe_line = jnp.where(inside, local_line, 0)
    target = jnp.where(inside, local_line, lines_dev)

    rows = injection.shape[0]
    step = rows // CHUNKS
    snapshots = base_dual.shape[0]
    base_rows = base_dual.reshape(line_devs, rows, lines_dev)
    post_rows = post_dual.reshape(line_devs, rows, lines_dev)
    parts = [slice(c * step, (c + 1) * step) for c in range(CHUNKS)]
    new_parts, base_parts, post_parts = pipeline(
        [extra_high[p] for p in parts],
        [extra_low[p] for p in parts],
        [injection[p] for p in parts],
        bus_cost,
        bus_cap,
        [balance_new[p] for p in parts],
        [base_rows[:, p].reshape(line_devs * step, lines_dev) for p in parts],
        [post_rows[:, p].reshape(line_devs * step, lines_dev) for p in parts],
        flow_limit,
        emergency_limit,
        ptdf,
        lodf,
        inside,
        safe_line,
        target,
        outage_weight,
    )
    new_injection = jnp.concatenate(new_parts, axis=0)
    base_new = jnp.stack([b.reshape(line_devs, step, lines_dev) for b in base_parts], axis=1).reshape(snapshots, lines_dev)
    post_new = jnp.stack([b.reshape(line_devs, step, lines_dev) for b in post_parts], axis=1).reshape(snapshots, lines_dev)
    return (new_injection, balance_new, base_new, post_new)


def solution(mesh):
    in_specs = (
        P("line", "col"),
        P("line", "col"),
        P("line", "col"),
        P("line", "col"),
        P("col"),
        P("col"),
        P("line"),
        P("line"),
        P(None, "line"),
        P(None, "line"),
        P("line"),
        P("line"),
        P("col"),
        P("col"),
    )
    out_specs = (P("line", "col"), P("line"), P(None, "line"), P(None, "line"))
    return jax.shard_map(
        on_device, mesh=mesh, in_specs=in_specs, out_specs=out_specs, check_vma=False
    )
```

time: 751 us -> 1180 us (1.57)
  waiting for transfers between devices: 640 us -> 983 us
  blocking collectives: 18.1 us -> 68.2 us
  local copies, waits for them, and re-layouts: 18.2 us -> 36.1 us
  other arithmetic: 26.4 us -> 41.1 us
    psum x4 -> x8, waiting for transfers between devices: 386 us -> 692 us  [the longest x2 251 us: pipeline(): lax.psum(tie(back_part, back_flow[c - 1] if c else None), 'line')]
    reduce_scatter x2 -> x4, waiting for transfers between devices: 156 us -> 218 us  [the longest x2 120 us: pipeline(): lax.psum_scatter(jnp.dot(line_total, ptdf, preferred_element_type=jnp.flo...]
    all_gather x0 -> x2, blocking collectives: none -> 50.7 us  [pipeline(): outage_flow.append(lax.all_gather(pieces, 'line', axis=0, tiled=True))]
    all_gather x2, waiting for transfers between devices: 97.9 us -> 72.9 us  [pipeline(): portion = lax.all_gather(stacked, 'line', axis=1, tiled=True)]
    dot_general x4 -> x8, matrix products: 31.3 us -> 38.5 us  [the longest x2 15.6 us: pipeline(): jnp.dot(line_total, ptdf, preferred_element_type=jnp.float32)]
  transfers between devices with their start and end apart: 8 -> 14, of which waited for: 8 -> 14; matrix products, arithmetic and copies ran while one was open for 0% -> 6% of each run, Pallas kernels for 0% -> 0%
where the time goes in v2:
time: 1180 us
  waiting for transfers between devices  983 us (83%)
  blocking collectives  68.2 us (6%)
  other arithmetic  41.1 us (3%)
  matrix products  38.5 us (3%)
  local copies, waits for them, and re-layouts  36.1 us (3%)
  between operations  14.1 us (1%)
    psum x2, waiting for transfers between devices, pipeline(): lax.psum(tie(back_part, back_flow[c - 1] if c else None), 'line')  251 us
    psum x2, waiting for transfers between devices, pipeline(): last_col = lax.psum(tie(flow_part, last_col), 'col')  153 us
    psum x2, waiting for transfers between devices, pipeline(): last_col = lax.psum(tie(returned_part, last_col), 'col')  146 us
    psum x2, waiting for transfers between devices, pipeline(): post_shift = lax.psum(tie(shift_part, last_col), 'col')  142 us
    reduce_scatter x2, waiting for transfers between devices, pipeline(): lax.psum_scatter(jnp.dot(line_total, ptdf, preferred_element_type=jnp.flo...  120 us
    reduce_scatter x2, waiting for transfers between devices, pipeline(): lax.psum_scatter(weighted.astype(jnp.bfloat16), 'line', scatter_dimension...  97.5 us
    all_gather x2, waiting for transfers between devices, pipeline(): portion = lax.all_gather(stacked, 'line', axis=1, tiled=True)  72.9 us
    all_gather x2, blocking collectives, pipeline(): outage_flow.append(lax.all_gather(pieces, 'line', axis=0, tiled=True))  50.7 us
  transfers between devices with their start and end apart: 14, of which 14 were waited for; matrix products, arithmetic and copies ran while one was open for 6% of the time, Pallas kernels for 0%

profile of v2, /device:TPU:1, one launch (start us, length us, event | category | flops | bytes accessed | tf_op | source)
XLA Modules:
  0.0 1181.9 jit_solution(13825952645487158330)
XLA Ops:
  7.2 1.6 fusion.5
  10.5 41.3 %all-gather.3.cloned.1.call-done = bf16[2,256,4608]{2,1,0:T(8,128)(2,1)} async-done(((bf16[2,16,4608]{2,1,0:T(8,128)(2,1)}), bf16[2,256,4608]{2,1,0:T(8,128)(2,1)}) %all-gather.3.cloned.1.call-update) | async-done | bytes 4718608 | tf_op jit(solution)/shard_map/all_gather | solution.py:49
  51.8 7.8 fusion.22
  59.6 1.0 slice_add_fusion.1
  60.6 31.6 %all-gather.5.cloned.1.call-done = bf16[2,256,4608]{2,1,0:T(8,128)(2,1)} async-done(((bf16[2,16,4608]{2,1,0:T(8,128)(2,1)}), bf16[2,256,4608]{2,1,0:T(8,128)(2,1)}) %all-gather.5.cloned.1.call-update) | async-done | bytes 4718608 | tf_op jit(solution)/shard_map/all_gather | solution.py:49
  92.2 7.8 fusion.24
  100.0 1.0 slice_add_fusion
  101.0 75.0 %all-reduce.9.cloned.1.call-done = f32[256,768]{1,0:T(8,128)} async-done(((f32[256,768]{1,0:T(8,128)}), f32[256,768]{1,0:T(8,128)}) %all-reduce.9.cloned.1.call-update) | async-done | bytes 786448 | tf_op jit(solution)/shard_map/psum | solution.py:54
  176.2 1.4 copy.18
  177.6 4.6 gather_fusion
  182.2 3.0 copy.19
  185.2 77.9 %all-reduce.11.cloned.1.call-done = f32[256,768]{1,0:T(8,128)} async-done(((f32[256,768]{1,0:T(8,128)}), f32[256,768]{1,0:T(8,128)}) %all-reduce.11.cloned.1.call-update) | async-done | bytes 786448 | tf_op jit(solution)/shard_map/psum | solution.py:54
  263.1 1.4 copy.21
  264.5 4.6 gather_fusion.1
  269.2 3.1 copy.22
  272.2 3.4 fusion.3
  276.3 61.7 %reduce-scatter.5.cloned.1.call-done = bf16[16,1536]{1,0:T(8,128)(2,1)} async-done(((bf16[256,1536]{1,0:T(8,128)(2,1)}), bf16[16,1536]{1,0:T(8,128)(2,1)}) %reduce-scatter.5.cloned.1.call-update) | async-done | bytes 49168 | tf_op jit(solution)/shard_map/reduce_scatter | solution.py:60
  338.1 25.5 %all_gather.13 = bf16[256,1536]{1,0:T(8,128)(2,1)S(1)} all-gather(bf16[16,1536]{1,0:T(8,128)(2,1)} %reduce-scatter.5.cloned.1.call-done), channel_id=1, replica_groups=mesh['line'=16,'col'=8] {'line'}, dimensions={0}, use_global_device_ids=true | all-gather | bytes 835584 | tf_op jit(solution)/shard_map/all_gather | solution.py:61
  363.6 1.7 fusion.23
  365.4 35.8 %reduce-scatter.7.cloned.1.call-done = bf16[16,1536]{1,0:T(8,128)(2,1)} async-done(((bf16[256,1536]{1,0:T(8,128)(2,1)}), bf16[16,1536]{1,0:T(8,128)(2,1)}) %reduce-scatter.7.cloned.1.call-update) | async-done | bytes 49168 | tf_op jit(solution)/shard_map/reduce_scatter | solution.py:60
  401.2 25.2 %all_gather.15 = bf16[256,1536]{1,0:T(8,128)(2,1)S(1)} all-gather(bf16[16,1536]{1,0:T(8,128)(2,1)} %reduce-scatter.7.cloned.1.call-done), channel_id=1, replica_groups=mesh['line'=16,'col'=8] {'line'}, dimensions={0}, use_global_device_ids=true | all-gather | bytes 835584 | tf_op jit(solution)/shard_map/all_gather | solution.py:61
  426.3 1.7 fusion.25
  428.1 58.9 %all-reduce.13.cloned.1.call-done = f32[256,768]{1,0:T(8,128)} async-done(((f32[256,768]{1,0:T(8,128)}), f32[256,768]{1,0:T(8,128)}) %all-reduce.13.cloned.1.call-update) | async-done | bytes 786448 | tf_op jit(solution)/shard_map/psum | solution.py:64
  487.1 3.6 fusion.19
  490.7 83.5 %all-reduce.17.cloned.1.call-done = f32[256,768]{1,0:T(8,128)} async-done(((f32[256,768]{1,0:T(8,128)}), f32[256,768]{1,0:T(8,128)}) %all-reduce.17.cloned.1.call-update) | async-done | bytes 786448 | tf_op jit(solution)/shard_map/psum | solution.py:64
  574.2 4.7 multiply_subtract_fusion.1
  579.8 1.9 fusion.10
  581.8 1.9 fusion.8
  583.7 124.5 %all-reduce.15.cloned.1.call-done = f32[256,1536]{1,0:T(8,128)} async-done(((f32[256,1536]{1,0:T(8,128)}), f32[256,1536]{1,0:T(8,128)}) %all-reduce.15.cloned.1.call-update) | async-done | bytes 1572880 | tf_op jit(solution)/shard_map/psum | solution.py:70
  708.5 126.1 %all-reduce.21.cloned.1.call-done = f32[256,1536]{1,0:T(8,128)} async-done(((f32[256,1536]{1,0:T(8,128)}), f32[256,1536]{1,0:T(8,128)}) %all-reduce.21.cloned.1.call-update) | async-done | bytes 1572880 | tf_op jit(solution)/shard_map/psum | solution.py:70
  834.6 3.9 multiply_bitcast_fusion.1
  838.5 3.1 copy.20
  841.5 10.1 scatter_custom_fusion
  851.6 2.3 copy.23
  854.0 3.0 copy.24
  857.0 10.1 scatter_custom_fusion.1
  867.2 68.7 %all-reduce.19.cloned.1.call-done = f32[256,768]{1,0:T(8,128)} async-done(((f32[256,768]{1,0:T(8,128)}), f32[256,768]{1,0:T(8,128)}) %all-reduce.19.cloned.1.call-update) | async-done | bytes 786448 | tf_op jit(solution)/shard_map/psum | solution.py:77
  935.9 2.3 copy.25
  938.2 7.9 fusion.6
  946.2 77.3 %all-reduce.23.cloned.1.call-done = f32[256,768]{1,0:T(8,128)} async-done(((f32[256,768]{1,0:T(8,128)}), f32[256,768]{1,0:T(8,128)}) %all-reduce.23.cloned.1.call-update) | async-done | bytes 786448 | tf_op jit(solution)/shard_map/psum | solution.py:77
  1023.5 7.8 fusion.7
  1031.3 17.5 %psum.69 = f32[32]{0:T(128)S(1)} all-reduce(f32[32]{0:T(128)S(1)} %get-tuple-element.17), channel_id=1, replica_groups=mesh['line'=16,'col'=8] {'col'}, use_global_device_ids=true, to_apply=%region_11.13 | all-reduce | flops 32 | bytes 256 | tf_op jit(solution)/shard_map/psum | solution.py:113
  1048.9 1.5 pad_maximum_fusion
  1050.4 1.3 copy.26
  1051.9 1.3 copy.27
  1053.2 46.6 %reduce-scatter.9.cloned.1.call-done = f32[16,4608]{1,0:T(8,128)} async-done(((f32[256,4608]{1,0:T(8,128)}), f32[16,4608]{1,0:T(8,128)}) %reduce-scatter.9.cloned.1.call-update) | async-done | bytes 294928 | tf_op jit(solution)/shard_map/reduce_scatter | solution.py:82
  1099.8 73.5 %reduce-scatter.11.cloned.1.call-done = f32[16,4608]{1,0:T(8,128)} async-done(((f32[256,4608]{1,0:T(8,128)}), f32[16,4608]{1,0:T(8,128)}) %reduce-scatter.11.cloned.1.call-update) | async-done | bytes 294928 | tf_op jit(solution)/shard_map/reduce_scatter | solution.py:82
  1173.3 1.2 maximum_minimum_fusion.1
  (66 shorter events, 5.1 us)
Async XLA Ops:
  7.2 356.4 %copy-start = (bf16[768,1536]{1,0:T(8,128)(2,1)S(1)}, bf16[768,1536]{1,0:T(8,128)(2,1)}, u32[]{:S(2)}) copy-start(bf16[768,1536]{1,0:T(8,128)(2,1)} %param.17) | copy-start | bytes 7077892
  7.2 44.6 %all-gather.3.cloned.1.call-start = ((), (), s32[]{:S(2)}) async-start(), calls=%async_computation.4 | async-start | bytes 5013504 | tf_op jit(solution)/shard_map/all_gather | solution.py:49
  9.7 82.6 %all-gather.5.cloned.1.call-start = ((), (), s32[]{:S(2)}) async-start(), calls=%async_computation.7 | async-start | bytes 5013504 | tf_op jit(solution)/shard_map/all_gather | solution.py:49
  10.5 165.6 %all-reduce.9.cloned.1.call-start = ((), (), s32[]{:S(2)}) async-start(), calls=%async_computation.5 | async-start | bytes 1572864 | tf_op jit(solution)/shard_map/psum | solution.py:54
  60.6 202.5 %all-reduce.11.cloned.1.call-start = ((), (), s32[]{:S(2)}) async-start(), calls=%async_computation.8 | async-start | bytes 1572864 | tf_op jit(solution)/shard_map/psum | solution.py:54
  100.0 76.1 %copy-start.5 = (s32[1536]{0:T(1024)S(1)}, s32[1536]{0:T(1024)}, u32[]{:S(2)}) copy-start(s32[1536]{0:T(1024)} %param.28) | copy-start | bytes 18436
  176.1 162.0 %reduce-scatter.5.cloned.1.call-start = ((), (), s32[]{:S(2)}) async-start(), calls=%async_computation.6 | async-start | bytes 835584 | tf_op jit(solution)/shard_map/reduce_scatter | solution.py:60
  269.2 3.1 copy-start.4
  275.7 125.5 %reduce-scatter.7.cloned.1.call-start = ((), (), s32[]{:S(2)}) async-start(), calls=%async_computation.11 | async-start | bytes 835584 | tf_op jit(solution)/shard_map/reduce_scatter | solution.py:60
  276.3 210.7 %all-reduce.13.cloned.1.call-start = ((), (), s32[]{:S(2)}) async-start(), calls=%async_computation.9 | async-start | bytes 1572864 | tf_op jit(solution)/shard_map/psum | solution.py:64
  365.3 208.9 %all-reduce.17.cloned.1.call-start = ((), (), s32[]{:S(2)}) async-start(), calls=%async_computation.12 | async-start | bytes 1572864 | tf_op jit(solution)/shard_map/psum | solution.py:64
  426.3 60.7 %copy-start.8 = (f32[768]{0:T(1024)S(1)}, f32[768]{0:T(1024)}, u32[]{:S(2)}) copy-start(f32[768]{0:T(1024)} %param.26) | copy-start | bytes 9220
  426.3 60.8 %copy-start.9 = (f32[768]{0:T(1024)S(1)}, f32[768]{0:T(1024)}, u32[]{:S(2)}) copy-start(f32[768]{0:T(1024)} %param.27) | copy-start | bytes 9220
  487.0 221.2 %all-reduce.15.cloned.1.call-start = ((), (), s32[]{:S(2)}) async-start(), calls=%async_computation.10 | async-start | bytes 3145728 | tf_op jit(solution)/shard_map/psum | solution.py:70
  578.9 0.9 copy-start.1
  581.7 252.9 %all-reduce.21.cloned.1.call-start = ((), (), s32[]{:S(2)}) async-start(), calls=%async_computation.15 | async-start | bytes 3145728 | tf_op jit(solution)/shard_map/psum | solution.py:70
  708.2 227.6 %all-reduce.19.cloned.1.call-start = ((), (), s32[]{:S(2)}) async-start(), calls=%async_computation.13 | async-start | bytes 1572864 | tf_op jit(solution)/shard_map/psum | solution.py:77
  854.0 169.5 %all-reduce.23.cloned.1.call-start = ((), (), s32[]{:S(2)}) async-start(), calls=%async_computation.16 | async-start | bytes 1572864 | tf_op jit(solution)/shard_map/psum | solution.py:77
  938.2 161.6 %reduce-scatter.9.cloned.1.call-start = ((), (), s32[]{:S(2)}) async-start(), calls=%async_computation.14 | async-start | bytes 5013504 | tf_op jit(solution)/shard_map/reduce_scatter | solution.py:82
  946.1 227.2 %reduce-scatter.11.cloned.1.call-start = ((), (), s32[]{:S(2)}) async-start(), calls=%async_computation.17 | async-start | bytes 5013504 | tf_op jit(solution)/shard_map/reduce_scatter | solution.py:82
  1031.3 17.5 %copy-start.11 = (f32[32]{0:T(128)S(1)}, f32[32]{0:T(128)}, u32[]{:S(2)}) copy-start(f32[32]{0:T(128)} %param.23) | copy-start | bytes 388
  1031.3 17.5 %copy-start.12 = (f32[32]{0:T(128)S(1)}, f32[32]{0:T(128)}, u32[]{:S(2)}) copy-start(f32[32]{0:T(128)} %param.22) | copy-start | bytes 388
  1048.8 1.6 copy-start.10
  1050.4 1.4 copy-start.2
  1051.9 121.4 %copy-start.3 = (f32[32,4608]{1,0:T(8,128)S(1)}, f32[32,4608]{1,0:T(8,128)}, u32[]{:S(2)}) copy-start(f32[32,4608]{1,0:T(8,128)} %param.18) | copy-start | bytes 1769476
  1051.9 121.4 %copy-start.6 = (f32[4608]{0:T(1024)S(1)}, f32[4608]{0:T(1024)}, u32[]{:S(2)}) copy-start(f32[4608]{0:T(1024)} %param.20) | copy-start | bytes 55300
  1051.9 121.4 %copy-start.7 = (f32[4608]{0:T(1024)S(1)}, f32[4608]{0:T(1024)}, u32[]{:S(2)}) copy-start(f32[4608]{0:T(1024)} %param.21) | copy-start | bytes 55300
Sparse Core Ops, SparseCore 0:
  10.2 41.5 all-gather.2
  54.0 38.1 all-gather.4
  95.3 80.6 all-reduce.8
  178.4 84.6 all-reduce.10
  275.8 62.1 reduce-scatter.4
  340.3 60.8 reduce-scatter.6
  404.2 82.7 all-reduce.12
  489.5 84.6 all-reduce.16
  581.8 126.3 all-reduce.14
  711.1 123.3 all-reduce.20
  854.1 81.7 all-reduce.18
  938.8 84.6 all-reduce.22
  1025.9 73.7 reduce-scatter.8
  1102.0 71.1 reduce-scatter.10

commit v3 on v1

--- a/solution.py
+++ b/solution.py
@@ -8,6 +8,24 @@
 
 dual_step = 0.5
 primal_step = 0.5
+
+
+def summed_block(value, axis):
+    n = lax.axis_size(axis)
+    rows = value.shape[0] // n
+    parts = lax.all_to_all(value.reshape(n, rows, *value.shape[1:]), axis, 0, 0, tiled=True)
+    return parts.sum(axis=0, dtype=value.dtype)
+
+
+def gathered_rows(block, axis):
+    n = lax.axis_size(axis)
+    copies = jnp.broadcast_to(block[None], (n, *block.shape))
+    whole = lax.all_to_all(copies, axis, 0, 0, tiled=True)
+    return whole.reshape(n * block.shape[0], *block.shape[1:])
+
+
+def full_sum(value, axis):
+    return gathered_rows(summed_block(value, axis), axis)
 
 
 def dual_update(dual, flow, limit):
@@ -44,7 +62,7 @@
     flow_part = product[:count] + product[count:]
     local_total = jnp.sum(extra_high.astype(jnp.float32) + extra_low.astype(jnp.float32), axis=1)
     bus_total = lax.psum(local_total, "col")
-    base_flow = lax.psum(flow_part, "col")
+    base_flow = full_sum(flow_part, "col")
     balance_new = balance_dual + (bus_total - demand) / BUSES
     base_new = dual_update(base_dual, base_flow, flow_limit[None, :])
     first_line = lax.axis_index("line") * lines_dev
@@ -53,21 +71,20 @@
     safe_line = jnp.where(inside, local_line, 0)
     picked = jnp.take(base_flow, safe_line, axis=1)
     weighted = jnp.where(inside[None, :], picked * outage_weight[None, :], 0.0)
-    pieces = lax.psum_scatter(weighted.astype(jnp.bfloat16), "line", scatter_dimension=0, tiled=True)
-    outage_flow = lax.all_gather(pieces, "line", axis=0, tiled=True)
+    outage_flow = full_sum(weighted.astype(jnp.bfloat16), "line")
     shift_part = jnp.dot(outage_flow, lodf.T, preferred_element_type=jnp.float32)
-    post_shift = lax.psum(shift_part, "col")
+    post_shift = full_sum(shift_part, "col")
     post_flow = base_flow + post_shift
     post_new = dual_update(post_dual, post_flow, emergency_limit[None, :])
     back_part = jnp.dot(post_new.astype(jnp.bfloat16), lodf, preferred_element_type=jnp.float32)
-    back_flow = lax.psum(back_part, "line")
+    back_flow = full_sum(back_part, "line")
     target = jnp.where(inside, local_line, lines_dev)
     returned_part = (
         jnp.zeros(base_new.shape, jnp.float32)
         .at[:, target]
         .add(back_flow * outage_weight[None, :], mode="drop")
     )
-    returned = lax.psum(returned_part, "col")
+    returned = full_sum(returned_part, "col")
     line_total = (base_new + post_new + returned).astype(jnp.bfloat16)
     prices = lax.psum_scatter(
         jnp.dot(line_total, ptdf, preferred_element_type=jnp.float32),

time: 751 us -> 563 us (0.75)
  waiting for transfers between devices: 640 us -> 239 us
  blocking collectives: 18.1 us -> 200 us
  starting transfers between devices: 0.51 us -> 18.8 us
  other arithmetic: 26.4 us -> 37.9 us
  local copies, waits for them, and re-layouts: 18.2 us -> 26.4 us
    psum x4 -> x0, waiting for transfers between devices: 386 us -> none  [the longest x1 132 us: on_device(): back_flow = lax.psum(back_part, 'line')]
    all_to_all x0 -> x6, blocking collectives: none -> 178 us  [the longest x5 153 us: summed_block(): lax.all_to_all(value.reshape(n, rows, *value.shape[1:]), axis, 0, 0, tile...]
    all_to_all x0 -> x4, waiting for transfers between devices: none -> 92.3 us  [gathered_rows(): whole = lax.all_to_all(copies, axis, 0, 0, tiled=True)]
    reduce_scatter x1 -> x0, waiting for transfers between devices: 63.8 us -> none  [on_device(): lax.psum_scatter(weighted.astype(jnp.bfloat16), 'line', scatter_dimension...]
    all_gather x1 -> x0, waiting for transfers between devices: 36.8 us -> none  [on_device(): outage_flow = lax.all_gather(pieces, 'line', axis=0, tiled=True)]
    all_to_all x0 -> x4, starting transfers between devices: none -> 18.7 us  [gathered_rows(): whole = lax.all_to_all(copies, axis, 0, 0, tiled=True)]
    reduce_sum x0 -> x5, other arithmetic: none -> 8.22 us  [summed_block(): return parts.sum(axis=0, dtype=value.dtype)]
  transfers between devices with their start and end apart: 8 -> 6, of which waited for: 8 -> 6; matrix products, arithmetic and copies ran while one was open for 0% -> 0% of each run, Pallas kernels for 0% -> 0%
where the time goes in v3:
time: 563 us; the launch traced here: 561 us
  waiting for transfers between devices  239 us (42%)
  blocking collectives  200 us (36%)
  other arithmetic  37.9 us (7%)
  local copies, waits for them, and re-layouts  26.4 us (5%)
  matrix products  24.1 us (4%)
  starting transfers between devices  18.8 us (3%)
  between operations  14.3 us (3%)
    all_to_all x5, blocking collectives, summed_block(): lax.all_to_all(value.reshape(n, rows, *value.shape[1:]), axis, 0, 0, tile...  153 us
    all_to_all x4, waiting for transfers between devices, gathered_rows(): whole = lax.all_to_all(copies, axis, 0, 0, tiled=True)  92.3 us
    reduce_scatter x1, waiting for transfers between devices, on_device(): lax.psum_scatter(jnp.dot(line_total, ptdf, preferred_element_type=jnp.flo...  85.5 us
    all_gather x1, waiting for transfers between devices, on_device(): portion = lax.all_gather(stacked, 'line', axis=1, tiled=True)  61.2 us
    all_to_all x1, blocking collectives, gathered_rows(): whole = lax.all_to_all(copies, axis, 0, 0, tiled=True)  24.7 us
    psum x1, blocking collectives, on_device(): bus_total = lax.psum(local_total, 'col')  22.4 us
    all_to_all x4, starting transfers between devices, gathered_rows(): whole = lax.all_to_all(copies, axis, 0, 0, tiled=True)  18.7 us
    dot_general x1, matrix products, on_device(): product = jnp.dot(flat, ptdf_turned, preferred_element_type=jnp.float32)  12.1 us
  transfers between devices with their start and end apart: 6, of which 6 were waited for; matrix products, arithmetic and copies ran while one was open for 0% of the time, Pallas kernels for 0%

profile of v3, /device:TPU:1, one launch (start us, length us, event | category | flops | bytes accessed | tf_op | source)
XLA Modules:
  0.0 560.8 jit_solution(15334212271270037050)
XLA Ops:
  7.2 0.0 all-gather.2.cloned.1.call-start
  7.2 1.6 fusion.10
  8.8 0.9 pad_maximum_fusion
  9.7 61.2 %all-gather.2.cloned.1.call-done = bf16[2,512,4608]{2,1,0:T(8,128)(2,1)} async-done(((bf16[2,32,4608]{2,1,0:T(8,128)(2,1)}), bf16[2,512,4608]{2,1,0:T(8,128)(2,1)}) %all-gather.2.cloned.1.call-update) | async-done | bytes 9437200 | tf_op jit(solution)/shard_map/all_gather | solution.py:58
  70.9 12.1 %fusion.12 = f32[1024,768]{1,0:T(8,128)S(1)} fusion(bf16[1024,4608]{1,0:T(8,128)(2,1)} %bitcast.46, bf16[768,4608]{1,0:T(8,128)(2,1)} %param.14), kind=kOutput, calls=%fused_computation.33 | convolution fusion | flops 7247757312 | bytes 19660800 | tf_op jit(solution)/shard_map/dot_general | solution.py:61
  83.0 0.2 slice_add_fusion
  83.2 27.7 %all_to_all.50 = f32[8,64,768]{2,1,0:T(8,128)} all-to-all(f32[8,64,768]{2,1,0:T(8,128)S(1)} %bitcast.43), channel_id=1, replica_groups=mesh['line'=16,'col'=8] {'col'}, dimensions={0} | all-to-all | bytes 3145728 | tf_op jit(solution)/shard_map/all_to_all | solution.py:16
  111.0 1.5 reduce_sum.54
  112.5 1.3 broadcast_in_dim.41
  113.8 4.4 all-to-all-start.1
  118.2 18.5 %all-to-all-done.1 = f32[8,64,768]{2,1,0:T(8,128)} async-done(((f32[8,64,768]{2,1,0:T(8,128)}), f32[8,64,768]{2,1,0:T(8,128)}, u32[]{:S(2)}, u32[]{:S(2)}) %all-to-all-start.1) | async-done | bytes 1572896 | tf_op jit(solution)/shard_map/all_to_all | solution.py:23
  136.7 3.0 copy.22
  139.8 7.1 %gather_fusion = f32[1536,512]{1,0:T(8,128)} fusion(f32[512,768]{0,1:T(8,128)} %copy.22, s32[2048]{0:T(1024)S(1)} %pad_clamp_fusion), kind=kCustom, calls=%fused_computation | custom fusion | bytes 6297600 | tf_op jit(solution)/shard_map/jit(_take)/gather | solution.py:72
  146.9 3.6 copy.23
  150.4 2.3 select_convert_fusion
  152.8 28.4 %all_to_all.51 = bf16[16,32,1536]{2,1,0:T(8,128)(2,1)} all-to-all(bf16[16,32,1536]{2,1,0:T(8,128)(2,1)S(1)} %select_convert_fusion), channel_id=1, replica_groups=mesh['line'=16,'col'=8] {'line'}, dimensions={0} | all-to-all | bytes 3145728 | tf_op jit(solution)/shard_map/all_to_all | solution.py:16
  181.2 1.6 reduce_sum.55
  182.8 0.1 broadcast_in_dim.77
  183.0 24.7 %all_to_all.52 = bf16[16,32,1536]{2,1,0:T(8,128)(2,1)S(1)} all-to-all(bf16[16,32,1536]{2,1,0:T(8,128)(2,1)S(1)} %broadcast_in_dim.77), channel_id=1, replica_groups=mesh['line'=16,'col'=8] {'line'}, dimensions={0} | all-to-all | bytes 3145728 | tf_op jit(solution)/shard_map/all_to_all | solution.py:23
  207.7 1.4 fusion
  209.1 24.9 %all_to_all.53 = f32[8,64,768]{2,1,0:T(8,128)} all-to-all(f32[8,64,768]{2,1,0:T(8,128)S(1)} %fusion), channel_id=1, replica_groups=mesh['line'=16,'col'=8] {'col'}, dimensions={0} | all-to-all | bytes 3145728 | tf_op jit(solution)/shard_map/all_to_all | solution.py:16
  234.1 1.5 reduce_sum.56
  235.6 1.3 broadcast_in_dim.78
  236.8 4.4 all-to-all-start.5
  241.3 17.4 %all-to-all-done.5 = f32[8,64,768]{2,1,0:T(8,128)} async-done(((f32[8,64,768]{2,1,0:T(8,128)}), f32[8,64,768]{2,1,0:T(8,128)}, u32[]{:S(2)}, u32[]{:S(2)}) %all-to-all-start.5) | async-done | bytes 1572896 | tf_op jit(solution)/shard_map/all_to_all | solution.py:23
  258.7 2.8 multiply_subtract_fusion
  261.5 1.4 fusion.5
  262.9 46.2 %all_to_all.54 = f32[16,32,1536]{2,1,0:T(8,128)} all-to-all(f32[16,32,1536]{2,1,0:T(8,128)S(1)} %bitcast.44), channel_id=1, replica_groups=mesh['line'=16,'col'=8] {'line'}, dimensions={0} | all-to-all | bytes 6291456 | tf_op jit(solution)/shard_map/all_to_all | solution.py:16
  309.1 2.1 reduce_sum.57
  311.2 2.1 broadcast_in_dim.81
  313.3 5.5 all-to-all-start.7
  318.8 38.4 %all-to-all-done.7 = f32[16,32,1536]{2,1,0:T(8,128)} async-done(((f32[16,32,1536]{2,1,0:T(8,128)}), f32[16,32,1536]{2,1,0:T(8,128)}, u32[]{:S(2)}, u32[]{:S(2)}) %all-to-all-start.7) | async-done | bytes 3145760 | tf_op jit(solution)/shard_map/all_to_all | solution.py:23
  357.1 3.9 bitcast_multiply_fusion
  361.1 3.5 copy.24
  364.6 11.4 %scatter_custom_fusion = f32[512,768]{0,1:T(8,128)} fusion(s32[1536]{0:T(1024)S(1)} %compare_select_fusion, f32[1536,512]{1,0:T(8,128)} %copy.24, f32[]{:T(128)} %constant.11.clone.1), kind=kCustom, calls=%fused_computation.16 | custom fusion | flops 786432 | bytes 1573376 | tf_op jit(solution)/shard_map/scatter-add | solution.py:85
  376.0 3.1 copy.25
  379.1 25.9 %all_to_all.55 = f32[8,64,768]{2,1,0:T(8,128)} all-to-all(f32[8,64,768]{2,1,0:T(8,128)} %bitcast.42), channel_id=1, replica_groups=mesh['line'=16,'col'=8] {'col'}, dimensions={0} | all-to-all | bytes 3145728 | tf_op jit(solution)/shard_map/all_to_all | solution.py:16
  405.0 1.5 reduce_sum.58
  406.5 1.3 broadcast_in_dim.82
  407.7 4.4 all-to-all-start.9
  412.2 0.0 reduce-scatter.2.cloned.1.call-start
  412.2 18.0 %all-to-all-done.9 = f32[8,64,768]{2,1,0:T(8,128)} async-done(((f32[8,64,768]{2,1,0:T(8,128)}), f32[8,64,768]{2,1,0:T(8,128)}, u32[]{:S(2)}, u32[]{:S(2)}) %all-to-all-start.9) | async-done | bytes 1572896 | tf_op jit(solution)/shard_map/all_to_all | solution.py:23
  430.2 4.5 fusion.2
  434.7 9.2 %fusion.13 = f32[512,4608]{1,0:T(8,128)} fusion(bf16[512,768]{1,0:T(8,128)(2,1)S(1)} %get-tuple-element.8, bf16[768,4608]{1,0:T(8,128)(2,1)} %param.14), kind=kOutput, calls=%fused_computation.34 | convolution fusion | flops 3623878656 | bytes 17301504 | tf_op jit(solution)/shard_map/dot_general | solution.py:90
  443.9 0.0 reduce-scatter.2.cloned.1.call-update
  443.9 22.4 %psum.7 = f32[32]{0:T(128)S(1)} all-reduce(f32[32]{0:T(128)S(1)} %get-tuple-element.12), channel_id=1, replica_groups=mesh['line'=16,'col'=8] {'col'}, use_global_device_ids=true, to_apply=%region_8.9 | all-reduce | flops 32 | bytes 256 | tf_op jit(solution)/shard_map/psum | solution.py:64
  466.4 85.5 %reduce-scatter.2.cloned.1.call-done = f32[32,4608]{1,0:T(8,128)} async-done(((f32[512,4608]{1,0:T(8,128)}), f32[32,4608]{1,0:T(8,128)}) %reduce-scatter.2.cloned.1.call-update) | async-done | bytes 589840 | tf_op jit(solution)/shard_map/reduce_scatter | solution.py:89
  551.9 2.1 maximum_minimum_fusion
  (31 shorter events, 0.1 us)
Async XLA Ops:
  7.2 200.5 %copy-start = (bf16[768,1536]{1,0:T(8,128)(2,1)S(1)}, bf16[768,1536]{1,0:T(8,128)(2,1)}, u32[]{:S(2)}) copy-start(bf16[768,1536]{1,0:T(8,128)(2,1)} %param.15) | copy-start | bytes 7077892
  7.2 63.7 %all-gather.2.cloned.1.call-start = ((), (), s32[]{:S(2)}) async-start(), calls=%async_computation.11 | async-start | bytes 10027008 | tf_op jit(solution)/shard_map/all_gather | solution.py:58
  113.7 4.5 copy-start.4
  113.8 23.0 %all-to-all-start.1 = ((f32[8,64,768]{2,1,0:T(8,128)}), f32[8,64,768]{2,1,0:T(8,128)}, u32[]{:S(2)}, u32[]{:S(2)}) async-start(f32[8,64,768]{2,1,0:T(8,128)} %broadcast_in_dim.41), calls=%async_computation.1 | async-start | bytes 3145728 | tf_op jit(solution)/shard_map/all_to_all | solution.py:23
  146.9 3.6 copy-start.3
  236.8 4.4 copy-start.8
  236.8 21.9 %all-to-all-start.5 = ((f32[8,64,768]{2,1,0:T(8,128)}), f32[8,64,768]{2,1,0:T(8,128)}, u32[]{:S(2)}, u32[]{:S(2)}) async-start(f32[8,64,768]{2,1,0:T(8,128)} %broadcast_in_dim.78), calls=%async_computation.5 | async-start | bytes 3145728 | tf_op jit(solution)/shard_map/all_to_all | solution.py:23
  261.5 1.4 copy-start.1
  313.3 43.9 %all-to-all-start.7 = ((f32[16,32,1536]{2,1,0:T(8,128)}), f32[16,32,1536]{2,1,0:T(8,128)}, u32[]{:S(2)}, u32[]{:S(2)}) async-start(f32[16,32,1536]{2,1,0:T(8,128)} %broadcast_in_dim.81), calls=%async_computation.7 | async-start | bytes 6291456 | tf_op jit(solution)/shard_map/all_to_all | solution.py:23
  407.7 4.5 copy-start.7
  407.7 22.5 %all-to-all-start.9 = ((f32[8,64,768]{2,1,0:T(8,128)}), f32[8,64,768]{2,1,0:T(8,128)}, u32[]{:S(2)}, u32[]{:S(2)}) async-start(f32[8,64,768]{2,1,0:T(8,128)} %broadcast_in_dim.82), calls=%async_computation.9 | async-start | bytes 3145728 | tf_op jit(solution)/shard_map/all_to_all | solution.py:23
  412.2 139.7 %reduce-scatter.2.cloned.1.call-start = ((), (), s32[]{:S(2)}) async-start(), calls=%async_computation.12 | async-start | bytes 10027008 | tf_op jit(solution)/shard_map/reduce_scatter | solution.py:89
  443.9 22.5 %copy-start.10 = (f32[32]{0:T(128)S(1)}, f32[32]{0:T(128)}, u32[]{:S(2)}) copy-start(f32[32]{0:T(128)} %param.21) | copy-start | bytes 388
  443.9 22.5 %copy-start.11 = (f32[32]{0:T(128)S(1)}, f32[32]{0:T(128)}, u32[]{:S(2)}) copy-start(f32[32]{0:T(128)} %param.20) | copy-start | bytes 388
  443.9 108.0 %copy-start.2 = (f32[32,4608]{1,0:T(8,128)S(1)}, f32[32,4608]{1,0:T(8,128)}, u32[]{:S(2)}) copy-start(f32[32,4608]{1,0:T(8,128)} %param.16) | copy-start | bytes 1769476
  443.9 108.0 %copy-start.5 = (f32[4608]{0:T(1024)S(1)}, f32[4608]{0:T(1024)}, u32[]{:S(2)}) copy-start(f32[4608]{0:T(1024)} %param.18) | copy-start | bytes 55300
  443.9 108.0 %copy-start.6 = (f32[4608]{0:T(1024)S(1)}, f32[4608]{0:T(1024)}, u32[]{:S(2)}) copy-start(f32[4608]{0:T(1024)} %param.19) | copy-start | bytes 55300
  466.4 87.6 %copy-start.9 = (f32[32]{0:T(128)}, f32[32]{0:T(128)S(1)}, u32[]{:S(2)}) copy-start(f32[32]{0:T(128)S(1)} %multiply_add_fusion) | copy-start | bytes 388
Sparse Core Ops, SparseCore 0:
  10.2 60.6 all-gather.1
  444.0 107.7 reduce-scatter.1

commit v4 on v3

--- a/solution.py
+++ b/solution.py
@@ -86,11 +86,14 @@
     )
     returned = full_sum(returned_part, "col")
     line_total = (base_new + post_new + returned).astype(jnp.bfloat16)
-    prices = lax.psum_scatter(
-        jnp.dot(line_total, ptdf, preferred_element_type=jnp.float32),
-        "line",
-        scatter_dimension=0,
-        tiled=True,
+    split = ptdf.shape[1] // 2
+    price_part = jnp.dot(line_total, ptdf, preferred_element_type=jnp.float32)
+    prices = jnp.concatenate(
+        [
+            lax.psum_scatter(price_part[:, :split], "line", scatter_dimension=0, tiled=True),
+            summed_block(price_part[:, split:], "line"),
+        ],
+        axis=1,
     )
     moved = injection - primal_step * (bus_cost[None, :] + prices + balance_new[:, None])
     new_injection = jnp.clip(moved, 0.0, bus_cap[None, :])

time: 563 us -> 576 us (1.023)
  blocking collectives: 200 us -> 290 us
  waiting for transfers between devices: 239 us -> 153 us
  starting transfers between devices: 18.8 us -> 26.8 us
    psum x1, blocking collectives: 22.4 us -> 112 us  [on_device(): bus_total = lax.psum(local_total, 'col')]
    reduce_scatter x1, waiting for transfers between devices: 85.5 us -> 0.02 us  [on_device(): lax.psum_scatter(price_part[:, :split], 'line', scatter_dimension=0, tile...]
    all_to_all x0 -> x1, starting transfers between devices: none -> 7.97 us  [summed_block(): lax.all_to_all(value.reshape(n, rows, *value.shape[1:]), axis, 0, 0, tile...]
  transfers between devices with their start and end apart: 6 -> 7, of which waited for: 6 -> 5; matrix products, arithmetic and copies ran while one was open for 0% -> 0% of each run, Pallas kernels for 0% -> 0%
where the time goes in v4:
time: 576 us; the launch traced here: 573 us
  blocking collectives  290 us (50%)
  waiting for transfers between devices  153 us (27%)
  other arithmetic  37.8 us (7%)
  local copies, waits for them, and re-layouts  29.3 us (5%)
  starting transfers between devices  26.8 us (5%)
  matrix products  21 us (4%)
  between operations  14.3 us (2%)
    all_to_all x5, blocking collectives, summed_block(): lax.all_to_all(value.reshape(n, rows, *value.shape[1:]), axis, 0, 0, tile...  153 us
    psum x1, blocking collectives, on_device(): bus_total = lax.psum(local_total, 'col')  112 us
    all_to_all x4, waiting for transfers between devices, gathered_rows(): whole = lax.all_to_all(copies, axis, 0, 0, tiled=True)  92.3 us
    all_gather x1, waiting for transfers between devices, on_device(): portion = lax.all_gather(stacked, 'line', axis=1, tiled=True)  61.2 us
    all_to_all x1, blocking collectives, gathered_rows(): whole = lax.all_to_all(copies, axis, 0, 0, tiled=True)  24.7 us
    all_to_all x4, starting transfers between devices, gathered_rows(): whole = lax.all_to_all(copies, axis, 0, 0, tiled=True)  18.8 us
    dot_general x1, matrix products, on_device(): product = jnp.dot(flat, ptdf_turned, preferred_element_type=jnp.float32)  12.1 us
  transfers between devices with their start and end apart: 7, of which 5 were waited for; matrix products, arithmetic and copies ran while one was open for 0% of the time, Pallas kernels for 0%

profile of v4, /device:TPU:1, one launch (start us, length us, event | category | flops | bytes accessed | tf_op | source)
XLA Modules:
  0.0 572.6 jit_solution(15802820290882644909)
XLA Ops:
  7.2 1.6 fusion.10
  8.8 0.9 pad_maximum_fusion
  9.7 61.2 %all-gather.2.cloned.1.call-done = bf16[2,512,4608]{2,1,0:T(8,128)(2,1)} async-done(((bf16[2,32,4608]{2,1,0:T(8,128)(2,1)}), bf16[2,512,4608]{2,1,0:T(8,128)(2,1)}) %all-gather.2.cloned.1.call-update) | async-done | bytes 9437200 | tf_op jit(solution)/shard_map/all_gather | solution.py:58
  70.9 12.1 %fusion.18 = f32[1024,768]{1,0:T(8,128)S(1)} fusion(bf16[1024,4608]{1,0:T(8,128)(2,1)} %bitcast.48, bf16[768,4608]{1,0:T(8,128)(2,1)} %param.14), kind=kOutput, calls=%fused_computation.39 | convolution fusion | flops 7247757312 | bytes 19660800 | tf_op jit(solution)/shard_map/dot_general | solution.py:61
  83.1 0.2 slice_add_fusion
  83.2 27.7 %all_to_all.55 = f32[8,64,768]{2,1,0:T(8,128)} all-to-all(f32[8,64,768]{2,1,0:T(8,128)S(1)} %bitcast.45), channel_id=1, replica_groups=mesh['line'=16,'col'=8] {'col'}, dimensions={0} | all-to-all | bytes 3145728 | tf_op jit(solution)/shard_map/all_to_all | solution.py:16
  110.9 1.5 reduce_sum.63
  112.4 1.3 broadcast_in_dim.41
  113.7 4.4 all-to-all-start.1
  118.2 18.5 %all-to-all-done.1 = f32[8,64,768]{2,1,0:T(8,128)} async-done(((f32[8,64,768]{2,1,0:T(8,128)}), f32[8,64,768]{2,1,0:T(8,128)}, u32[]{:S(2)}, u32[]{:S(2)}) %all-to-all-start.1) | async-done | bytes 1572896 | tf_op jit(solution)/shard_map/all_to_all | solution.py:23
  136.7 3.0 copy.22
  139.7 7.1 %gather_fusion = f32[1536,512]{1,0:T(8,128)} fusion(f32[512,768]{0,1:T(8,128)} %copy.22, s32[2048]{0:T(1024)S(1)} %pad_clamp_fusion), kind=kCustom, calls=%fused_computation | custom fusion | bytes 6297600 | tf_op jit(solution)/shard_map/jit(_take)/gather | solution.py:72
  146.8 3.6 copy.23
  150.4 2.3 select_convert_fusion
  152.7 28.5 %all_to_all.56 = bf16[16,32,1536]{2,1,0:T(8,128)(2,1)} all-to-all(bf16[16,32,1536]{2,1,0:T(8,128)(2,1)S(1)} %select_convert_fusion), channel_id=1, replica_groups=mesh['line'=16,'col'=8] {'line'}, dimensions={0} | all-to-all | bytes 3145728 | tf_op jit(solution)/shard_map/all_to_all | solution.py:16
  181.2 1.6 reduce_sum.64
  182.8 0.1 broadcast_in_dim.77
  183.0 24.7 %all_to_all.57 = bf16[16,32,1536]{2,1,0:T(8,128)(2,1)S(1)} all-to-all(bf16[16,32,1536]{2,1,0:T(8,128)(2,1)S(1)} %broadcast_in_dim.77), channel_id=1, replica_groups=mesh['line'=16,'col'=8] {'line'}, dimensions={0} | all-to-all | bytes 3145728 | tf_op jit(solution)/shard_map/all_to_all | solution.py:23
  207.7 1.4 fusion
  209.1 24.9 %all_to_all.58 = f32[8,64,768]{2,1,0:T(8,128)} all-to-all(f32[8,64,768]{2,1,0:T(8,128)S(1)} %fusion), channel_id=1, replica_groups=mesh['line'=16,'col'=8] {'col'}, dimensions={0} | all-to-all | bytes 3145728 | tf_op jit(solution)/shard_map/all_to_all | solution.py:16
  234.0 1.5 reduce_sum.65
  235.5 1.3 broadcast_in_dim.78
  236.8 4.4 all-to-all-start.5
  241.3 17.4 %all-to-all-done.5 = f32[8,64,768]{2,1,0:T(8,128)} async-done(((f32[8,64,768]{2,1,0:T(8,128)}), f32[8,64,768]{2,1,0:T(8,128)}, u32[]{:S(2)}, u32[]{:S(2)}) %all-to-all-start.5) | async-done | bytes 1572896 | tf_op jit(solution)/shard_map/all_to_all | solution.py:23
  258.7 2.8 multiply_subtract_fusion
  261.5 1.4 fusion.5
  262.9 46.2 %all_to_all.59 = f32[16,32,1536]{2,1,0:T(8,128)} all-to-all(f32[16,32,1536]{2,1,0:T(8,128)S(1)} %bitcast.46), channel_id=1, replica_groups=mesh['line'=16,'col'=8] {'line'}, dimensions={0} | all-to-all | bytes 6291456 | tf_op jit(solution)/shard_map/all_to_all | solution.py:16
  309.1 2.1 reduce_sum.66
  311.2 2.1 broadcast_in_dim.81
  313.3 5.5 all-to-all-start.7
  318.7 38.4 %all-to-all-done.7 = f32[16,32,1536]{2,1,0:T(8,128)} async-done(((f32[16,32,1536]{2,1,0:T(8,128)}), f32[16,32,1536]{2,1,0:T(8,128)}, u32[]{:S(2)}, u32[]{:S(2)}) %all-to-all-start.7) | async-done | bytes 3145760 | tf_op jit(solution)/shard_map/all_to_all | solution.py:23
  357.1 3.9 bitcast_multiply_fusion
  361.0 3.5 copy.24
  364.6 10.6 %scatter_custom_fusion = f32[512,768]{0,1:T(8,128)S(1)} fusion(s32[1536]{0:T(1024)S(1)} %compare_select_fusion, f32[1536,512]{1,0:T(8,128)} %copy.24, f32[]{:T(128)} %constant.11.clone.1), kind=kCustom, calls=%fused_computation.16 | custom fusion | flops 786432 | bytes 1573376 | tf_op jit(solution)/shard_map/scatter-add | solution.py:85
  375.2 1.6 copy.25
  376.8 25.8 %all_to_all.60 = f32[8,64,768]{2,1,0:T(8,128)S(1)} all-to-all(f32[8,64,768]{2,1,0:T(8,128)} %bitcast.44), channel_id=1, replica_groups=mesh['line'=16,'col'=8] {'col'}, dimensions={0} | all-to-all | bytes 3145728 | tf_op jit(solution)/shard_map/all_to_all | solution.py:16
  402.6 0.1 reduce_sum.67
  402.7 1.3 broadcast_in_dim.82
  404.0 4.4 all-to-all-start.9
  408.4 0.0 reduce-scatter.2.cloned.1.call-start
  408.5 18.0 %all-to-all-done.9 = f32[8,64,768]{2,1,0:T(8,128)} async-done(((f32[8,64,768]{2,1,0:T(8,128)}), f32[8,64,768]{2,1,0:T(8,128)}, u32[]{:S(2)}, u32[]{:S(2)}) %all-to-all-start.9) | async-done | bytes 1572896 | tf_op jit(solution)/shard_map/all_to_all | solution.py:23
  426.5 4.0 fusion.2
  430.4 6.0 %fusion.19 = f32[512,4608]{1,0:T(8,128)S(1)} fusion(bf16[512,768]{1,0:T(8,128)(2,1)S(1)} %get-tuple-element.8, bf16[768,4608]{1,0:T(8,128)(2,1)} %param.14), kind=kOutput, calls=%fused_computation.40 | convolution fusion | flops 3623878656 | bytes 17301504 | tf_op jit(solution)/shard_map/dot_general | solution.py:90
  436.5 4.3 fusion.17
  440.9 8.0 %all-to-all-start.10 = ((f32[16,32,2304]{2,1,0:T(8,128)}), f32[16,32,2304]{2,1,0:T(8,128)}, u32[]{:S(2)}, u32[]{:S(2)}) async-start(f32[16,32,2304]{2,1,0:T(8,128)} %bitcast.40), calls=%async_computation.11 | async-start | bytes 9437184 | tf_op jit(solution)/shard_map/all_to_all | solution.py:16
  448.8 112.1 %psum.7 = f32[32]{0:T(128)S(1)} all-reduce(f32[32]{0:T(128)S(1)} %get-tuple-element.14), channel_id=1, replica_groups=mesh['line'=16,'col'=8] {'col'}, use_global_device_ids=true, to_apply=%region_9.10 | all-reduce | flops 32 | bytes 256 | tf_op jit(solution)/shard_map/psum | solution.py:64
  561.0 2.7 reduce_sum.68
  563.8 2.0 fusion.15
  (39 shorter events, 0.2 us)
Async XLA Ops:
  7.2 200.5 %copy-start = (bf16[768,1536]{1,0:T(8,128)(2,1)S(1)}, bf16[768,1536]{1,0:T(8,128)(2,1)}, u32[]{:S(2)}) copy-start(bf16[768,1536]{1,0:T(8,128)(2,1)} %param.15) | copy-start | bytes 7077892
  7.2 63.7 %all-gather.2.cloned.1.call-start = ((), (), s32[]{:S(2)}) async-start(), calls=%async_computation.12 | async-start | bytes 10027008 | tf_op jit(solution)/shard_map/all_gather | solution.py:58
  113.7 4.5 copy-start.6
  113.7 23.0 %all-to-all-start.1 = ((f32[8,64,768]{2,1,0:T(8,128)}), f32[8,64,768]{2,1,0:T(8,128)}, u32[]{:S(2)}, u32[]{:S(2)}) async-start(f32[8,64,768]{2,1,0:T(8,128)} %broadcast_in_dim.41), calls=%async_computation.1 | async-start | bytes 3145728 | tf_op jit(solution)/shard_map/all_to_all | solution.py:23
  146.8 3.6 copy-start.5
  236.8 4.4 copy-start.10
  236.8 21.9 %all-to-all-start.5 = ((f32[8,64,768]{2,1,0:T(8,128)}), f32[8,64,768]{2,1,0:T(8,128)}, u32[]{:S(2)}, u32[]{:S(2)}) async-start(f32[8,64,768]{2,1,0:T(8,128)} %broadcast_in_dim.78), calls=%async_computation.5 | async-start | bytes 3145728 | tf_op jit(solution)/shard_map/all_to_all | solution.py:23
  261.5 1.4 copy-start.2
  313.3 43.9 %all-to-all-start.7 = ((f32[16,32,1536]{2,1,0:T(8,128)}), f32[16,32,1536]{2,1,0:T(8,128)}, u32[]{:S(2)}, u32[]{:S(2)}) async-start(f32[16,32,1536]{2,1,0:T(8,128)} %broadcast_in_dim.81), calls=%async_computation.7 | async-start | bytes 6291456 | tf_op jit(solution)/shard_map/all_to_all | solution.py:23
  404.0 4.5 copy-start.9
  404.0 22.5 %copy-start.3 = (f32[512,768]{1,0:T(8,128)S(1)}, f32[512,768]{1,0:T(8,128)}, u32[]{:S(2)}) copy-start(f32[512,768]{1,0:T(8,128)} %copy-done.2) | copy-start | bytes 4718596
  404.0 22.5 %all-to-all-start.9 = ((f32[8,64,768]{2,1,0:T(8,128)}), f32[8,64,768]{2,1,0:T(8,128)}, u32[]{:S(2)}, u32[]{:S(2)}) async-start(f32[8,64,768]{2,1,0:T(8,128)} %broadcast_in_dim.82), calls=%async_computation.9 | async-start | bytes 3145728 | tf_op jit(solution)/shard_map/all_to_all | solution.py:23
  408.4 155.4 %reduce-scatter.2.cloned.1.call-start = ((), (), s32[]{:S(2)}) async-start(), calls=%async_computation.13 | async-start | bytes 5013504 | tf_op jit(solution)/shard_map/reduce_scatter | solution.py:93
  440.8 120.1 %copy-start.12 = (f32[32]{0:T(128)S(1)}, f32[32]{0:T(128)}, u32[]{:S(2)}) copy-start(f32[32]{0:T(128)} %param.21) | copy-start | bytes 388
  440.9 120.1 %copy-start.13 = (f32[32]{0:T(128)S(1)}, f32[32]{0:T(128)}, u32[]{:S(2)}) copy-start(f32[32]{0:T(128)} %param.20) | copy-start | bytes 388
  440.9 120.1 %all-to-all-start.10 = ((f32[16,32,2304]{2,1,0:T(8,128)}), f32[16,32,2304]{2,1,0:T(8,128)}, u32[]{:S(2)}, u32[]{:S(2)}) async-start(f32[16,32,2304]{2,1,0:T(8,128)} %bitcast.40), calls=%async_computation.11 | async-start | bytes 9437184 | tf_op jit(solution)/shard_map/all_to_all | solution.py:16
  560.9 2.8 copy-start.11
  560.9 2.8 copy-start.4
  561.0 2.8 copy-start.7
  561.0 2.8 copy-start.8
  561.0 4.8 copy-start.1
Sparse Core Ops, SparseCore 0:
  10.2 60.6 all-gather.1
  441.0 107.5 reduce-scatter.1

commit v5 on v3

--- a/solution.py
+++ b/solution.py
@@ -1,7 +1,7 @@
 import jax
 import jax.numpy as jnp
 from jax import lax
-from jax.sharding import PartitionSpec as P
+from jax.sharding import Mesh, PartitionSpec as P
 
 BUSES = 36864
 
@@ -26,6 +26,42 @@
 
 def full_sum(value, axis):
     return gathered_rows(summed_block(value, axis), axis)
+
+
+LINE_OUTER = "line_outer"
+LINE_CORE = "line_core"
+LINE = (LINE_OUTER, LINE_CORE)
+
+
+def swap_cores(value):
+    return lax.ppermute(value, LINE_CORE, [(0, 1), (1, 0)])
+
+
+def line_summed_block(value):
+    outer = lax.axis_size(LINE_OUTER)
+    core = lax.axis_index(LINE_CORE)
+    rows = value.shape[0] // (2 * outer)
+    split = value.reshape(outer, 2, rows, *value.shape[1:])
+    first, second = split[:, 0], split[:, 1]
+    keep = jnp.where(core == 0, first, second)
+    give = jnp.where(core == 0, second, first)
+    pair_sum = keep + swap_cores(give)
+    parts = lax.all_to_all(pair_sum, LINE_OUTER, 0, 0, tiled=True)
+    return parts.sum(axis=0, dtype=value.dtype)
+
+
+def line_gathered_rows(block):
+    outer = lax.axis_size(LINE_OUTER)
+    core = lax.axis_index(LINE_CORE)
+    copies = jnp.broadcast_to(block[None], (outer, *block.shape))
+    mine = lax.all_to_all(copies, LINE_OUTER, 0, 0, tiled=True)
+    other = swap_cores(mine)
+    whole = jnp.where(core == 0, jnp.stack([mine, other], axis=1), jnp.stack([other, mine], axis=1))
+    return whole.reshape(2 * outer * block.shape[0], *block.shape[1:])
+
+
+def line_full_sum(value):
+    return line_gathered_rows(line_summed_block(value))
 
 
 def dual_update(dual, flow, limit):
@@ -55,7 +91,7 @@
     stacked = jnp.stack([extra_high, extra_low], axis=0)
     lines_dev = ptdf.shape[0]
     ptdf_turned = ptdf.T
-    portion = lax.all_gather(stacked, "line", axis=1, tiled=True)
+    portion = lax.all_gather(stacked, LINE, axis=1, tiled=True)
     count = portion.shape[1]
     flat = portion.reshape(2 * count, portion.shape[2])
     product = jnp.dot(flat, ptdf_turned, preferred_element_type=jnp.float32)
@@ -65,19 +101,19 @@
     base_flow = full_sum(flow_part, "col")
     balance_new = balance_dual + (bus_total - demand) / BUSES
     base_new = dual_update(base_dual, base_flow, flow_limit[None, :])
-    first_line = lax.axis_index("line") * lines_dev
+    first_line = lax.axis_index(LINE) * lines_dev
     local_line = outage_line - first_line
     inside = (local_line >= 0) & (local_line < lines_dev)
     safe_line = jnp.where(inside, local_line, 0)
     picked = jnp.take(base_flow, safe_line, axis=1)
     weighted = jnp.where(inside[None, :], picked * outage_weight[None, :], 0.0)
-    outage_flow = full_sum(weighted.astype(jnp.bfloat16), "line")
+    outage_flow = line_full_sum(weighted.astype(jnp.bfloat16))
     shift_part = jnp.dot(outage_flow, lodf.T, preferred_element_type=jnp.float32)
     post_shift = full_sum(shift_part, "col")
     post_flow = base_flow + post_shift
     post_new = dual_update(post_dual, post_flow, emergency_limit[None, :])
     back_part = jnp.dot(post_new.astype(jnp.bfloat16), lodf, preferred_element_type=jnp.float32)
-    back_flow = full_sum(back_part, "line")
+    back_flow = line_full_sum(back_part)
     target = jnp.where(inside, local_line, lines_dev)
     returned_part = (
         jnp.zeros(base_new.shape, jnp.float32)
@@ -86,35 +122,34 @@
     )
     returned = full_sum(returned_part, "col")
     line_total = (base_new + post_new + returned).astype(jnp.bfloat16)
-    prices = lax.psum_scatter(
-        jnp.dot(line_total, ptdf, preferred_element_type=jnp.float32),
-        "line",
-        scatter_dimension=0,
-        tiled=True,
-    )
+    prices = line_summed_block(jnp.dot(line_total, ptdf, preferred_element_type=jnp.float32))
     moved = injection - primal_step * (bus_cost[None, :] + prices + balance_new[:, None])
     new_injection = jnp.clip(moved, 0.0, bus_cap[None, :])
     return (new_injection, balance_new, base_new, post_new)
 
 
 def solution(mesh):
+    outer = mesh.shape["line"] // 2
+    fine = Mesh(
+        mesh.devices.reshape(outer, 2, mesh.shape["col"]), (LINE_OUTER, LINE_CORE, "col")
+    )
     in_specs = (
-        P("line", "col"),
-        P("line", "col"),
-        P("line", "col"),
-        P("line", "col"),
+        P(LINE, "col"),
+        P(LINE, "col"),
+        P(LINE, "col"),
+        P(LINE, "col"),
         P("col"),
         P("col"),
-        P("line"),
-        P("line"),
-        P(None, "line"),
-        P(None, "line"),
-        P("line"),
-        P("line"),
+        P(LINE),
+        P(LINE),
+        P(None, LINE),
+        P(None, LINE),
+        P(LINE),
+        P(LINE),
         P("col"),
         P("col"),
     )
-    out_specs = (P("line", "col"), P("line"), P(None, "line"), P(None, "line"))
+    out_specs = (P(LINE, "col"), P(LINE), P(None, LINE), P(None, LINE))
     return jax.shard_map(
-        on_device, mesh=mesh, in_specs=in_specs, out_specs=out_specs, check_vma=False
+        on_device, mesh=fine, in_specs=in_specs, out_specs=out_specs, check_vma=False
     )

time: 563 us -> 487 us (0.87)
  waiting for transfers between devices: 239 us -> 134 us
  blocking collectives: 200 us -> 220 us
  starting transfers between devices: 18.8 us -> 32.8 us
    reduce_scatter x1 -> x0, waiting for transfers between devices: 85.5 us -> none  [on_device(): lax.psum_scatter(jnp.dot(line_total, ptdf, preferred_element_type=jnp.flo...]
    all_to_all x5 -> x3, blocking collectives: 153 us -> 79.2 us  [summed_block(): lax.all_to_all(value.reshape(n, rows, *value.shape[1:]), axis, 0, 0, tile...]
    all_to_all x1 -> x4, blocking collectives: 24.7 us -> 76.4 us  [the longest x2 39.5 us: line_summed_block(): parts = lax.all_to_all(pair_sum, LINE_OUTER, 0, 0, tiled=True)]
    psum x1, blocking collectives: 22.4 us -> 64.6 us  [on_device(): bus_total = lax.psum(local_total, 'col')]
    all_to_all x4 -> x3, waiting for transfers between devices: 92.3 us -> 55.1 us  [gathered_rows(): whole = lax.all_to_all(copies, axis, 0, 0, tiled=True)]
    ppermute x0 -> x5, waiting for transfers between devices: none -> 17.4 us  [swap_cores(): return lax.ppermute(value, LINE_CORE, [(0, 1), (1, 0)])]
    ppermute x0 -> x5, starting transfers between devices: none -> 14.8 us  [swap_cores(): return lax.ppermute(value, LINE_CORE, [(0, 1), (1, 0)])]
    all_to_all x4 -> x3, starting transfers between devices: 18.7 us -> 13.3 us  [gathered_rows(): whole = lax.all_to_all(copies, axis, 0, 0, tiled=True)]
  transfers between devices with their start and end apart: 6 -> 10, of which waited for: 6 -> 9; matrix products, arithmetic and copies ran while one was open for 0% -> 0% of each run, Pallas kernels for 0% -> 0%
where the time goes in v5:
time: 487 us; the launch traced here: 483 us
  blocking collectives  220 us (45%)
  waiting for transfers between devices  134 us (28%)
  other arithmetic  37.6 us (8%)
  starting transfers between devices  32.8 us (7%)
  local copies, waits for them, and re-layouts  23.3 us (5%)
  matrix products  21 us (4%)
  between operations  14.4 us (3%)
    all_to_all x3, blocking collectives, summed_block(): lax.all_to_all(value.reshape(n, rows, *value.shape[1:]), axis, 0, 0, tile...  79.2 us
    psum x1, blocking collectives, on_device(): bus_total = lax.psum(local_total, 'col')  64.6 us
    all_gather x1, waiting for transfers between devices, on_device(): portion = lax.all_gather(stacked, LINE, axis=1, tiled=True)  61.2 us
    all_to_all x3, waiting for transfers between devices, gathered_rows(): whole = lax.all_to_all(copies, axis, 0, 0, tiled=True)  55.1 us
    all_to_all x2, blocking collectives, line_summed_block(): parts = lax.all_to_all(pair_sum, LINE_OUTER, 0, 0, tiled=True)  39.5 us
    all_to_all x2, blocking collectives, line_gathered_rows(): mine = lax.all_to_all(copies, LINE_OUTER, 0, 0, tiled=True)  36.9 us
    ppermute x5, waiting for transfers between devices, swap_cores(): return lax.ppermute(value, LINE_CORE, [(0, 1), (1, 0)])  17.4 us
    ppermute x5, starting transfers between devices, swap_cores(): return lax.ppermute(value, LINE_CORE, [(0, 1), (1, 0)])  14.8 us
  transfers between devices with their start and end apart: 10, of which 9 were waited for; matrix products, arithmetic and copies ran while one was open for 0% of the time, Pallas kernels for 0%

profile of v5, /device:TPU:1, one launch (start us, length us, event | category | flops | bytes accessed | tf_op | source)
XLA Modules:
  0.0 483.0 jit_solution(11826154275775770024)
XLA Ops:
  7.2 1.6 fusion.15
  9.7 61.2 %all-gather.2.cloned.1.call-done = bf16[2,512,4608]{2,1,0:T(8,128)(2,1)} async-done(((bf16[2,32,4608]{2,1,0:T(8,128)(2,1)}), bf16[2,512,4608]{2,1,0:T(8,128)(2,1)}) %all-gather.2.cloned.1.call-update) | async-done | bytes 9437200 | tf_op jit(solution)/shard_map/all_gather | solution.py:94
  70.9 12.1 %fusion.17 = f32[1024,768]{1,0:T(8,128)S(1)} fusion(bf16[1024,4608]{1,0:T(8,128)(2,1)} %bitcast.112, bf16[768,4608]{1,0:T(8,128)(2,1)} %param.14), kind=kOutput, calls=%fused_computation.48 | convolution fusion | flops 7247757312 | bytes 19660800 | tf_op jit(solution)/shard_map/dot_general | solution.py:97
  83.2 27.7 %all_to_all.55 = f32[8,64,768]{2,1,0:T(8,128)} all-to-all(f32[8,64,768]{2,1,0:T(8,128)S(1)} %bitcast.107), channel_id=1, replica_groups=mesh['line_outer'=8,'line_core'=2,'col'=8] {'col'}, dimensions={0} | all-to-all | bytes 3145728 | tf_op jit(solution)/shard_map/all_to_all | solution.py:16
  110.9 1.5 reduce_sum.63
  112.4 1.3 broadcast_in_dim.41
  113.7 4.4 all-to-all-start.1
  118.2 18.5 %all-to-all-done.1 = f32[8,64,768]{2,1,0:T(8,128)} async-done(((f32[8,64,768]{2,1,0:T(8,128)}), f32[8,64,768]{2,1,0:T(8,128)}, u32[]{:S(2)}, u32[]{:S(2)}) %all-to-all-start.1) | async-done | bytes 1572896 | tf_op jit(solution)/shard_map/all_to_all | solution.py:23
  136.7 3.0 copy.47
  139.7 7.1 %gather_fusion = f32[1536,512]{1,0:T(8,128)} fusion(f32[512,768]{0,1:T(8,128)} %copy.47, s32[2048]{0:T(1024)S(1)} %pad_clamp_fusion), kind=kCustom, calls=%fused_computation | custom fusion | bytes 6297600 | tf_op jit(solution)/shard_map/jit(_take)/gather | solution.py:108
  146.8 3.6 copy.48
  150.4 2.3 select_convert_fusion
  152.8 3.3 collective-permute-start
  156.1 1.9 collective-permute-done
  158.2 16.0 %all_to_all.56 = bf16[8,32,1536]{2,1,0:T(8,128)(2,1)S(1)} all-to-all(bf16[8,32,1536]{2,1,0:T(8,128)(2,1)S(1)} %fusion.9), channel_id=1, replica_groups=mesh['line_outer'=8,'line_core'=2,'col'=8] {'line_outer'}, dimensions={0} | all-to-all | bytes 1572864 | tf_op jit(solution)/shard_map/all_to_all | solution.py:49
  174.4 14.4 %all_to_all.57 = bf16[8,32,1536]{2,1,0:T(8,128)(2,1)S(1)} all-to-all(bf16[8,32,1536]{2,1,0:T(8,128)(2,1)S(1)} %broadcast_in_dim.77), channel_id=1, replica_groups=mesh['line_outer'=8,'line_core'=2,'col'=8] {'line_outer'}, dimensions={0} | all-to-all | bytes 1572864 | tf_op jit(solution)/shard_map/all_to_all | solution.py:57
  188.8 2.3 collective-permute-start.1
  191.1 1.9 collective-permute-done.1
  193.4 1.4 fusion.2
  194.9 25.9 %all_to_all.58 = f32[8,64,768]{2,1,0:T(8,128)} all-to-all(f32[8,64,768]{2,1,0:T(8,128)S(1)} %fusion.2), channel_id=1, replica_groups=mesh['line_outer'=8,'line_core'=2,'col'=8] {'col'}, dimensions={0} | all-to-all | bytes 3145728 | tf_op jit(solution)/shard_map/all_to_all | solution.py:16
  220.7 1.5 reduce_sum.65
  222.2 1.3 broadcast_in_dim.78
  223.5 4.4 all-to-all-start.5
  227.9 18.3 %all-to-all-done.5 = f32[8,64,768]{2,1,0:T(8,128)} async-done(((f32[8,64,768]{2,1,0:T(8,128)}), f32[8,64,768]{2,1,0:T(8,128)}, u32[]{:S(2)}, u32[]{:S(2)}) %all-to-all-start.5) | async-done | bytes 1572896 | tf_op jit(solution)/shard_map/all_to_all | solution.py:23
  246.3 2.8 multiply_subtract_fusion
  249.1 1.4 fusion.10
  250.7 3.5 collective-permute-start.2
  254.1 3.0 collective-permute-done.2
  257.6 23.5 %all_to_all.59 = f32[8,32,1536]{2,1,0:T(8,128)S(1)} all-to-all(f32[8,32,1536]{2,1,0:T(8,128)S(1)} %bitcast_add_fusion.1), channel_id=1, replica_groups=mesh['line_outer'=8,'line_core'=2,'col'=8] {'line_outer'}, dimensions={0} | all-to-all | bytes 3145728 | tf_op jit(solution)/shard_map/all_to_all | solution.py:49
  281.3 22.5 %all_to_all.60 = f32[8,32,1536]{2,1,0:T(8,128)S(1)} all-to-all(f32[8,32,1536]{2,1,0:T(8,128)S(1)} %broadcast_in_dim.81), channel_id=1, replica_groups=mesh['line_outer'=8,'line_core'=2,'col'=8] {'line_outer'}, dimensions={0} | all-to-all | bytes 3145728 | tf_op jit(solution)/shard_map/all_to_all | solution.py:57
  303.8 2.2 collective-permute-start.3
  306.0 3.0 collective-permute-done.3
  309.6 2.0 bitcast_multiply_fusion
  311.6 3.6 copy.57
  315.1 10.6 %scatter_custom_fusion = f32[512,768]{0,1:T(8,128)S(1)} fusion(s32[1536]{0:T(1024)S(1)} %compare_select_fusion, f32[1536,512]{1,0:T(8,128)} %copy.57, f32[]{:T(128)} %constant.14.clone.1), kind=kCustom, calls=%fused_computation.31 | custom fusion | flops 786432 | bytes 1573376 | tf_op jit(solution)/shard_map/scatter-add | solution.py:121
  325.8 1.6 copy.58
  327.4 25.7 %all_to_all.61 = f32[8,64,768]{2,1,0:T(8,128)S(1)} all-to-all(f32[8,64,768]{2,1,0:T(8,128)} %bitcast.105), channel_id=1, replica_groups=mesh['line_outer'=8,'line_core'=2,'col'=8] {'col'}, dimensions={0} | all-to-all | bytes 3145728 | tf_op jit(solution)/shard_map/all_to_all | solution.py:16
  354.4 4.4 all-to-all-start.9
  358.9 18.3 %all-to-all-done.9 = f32[8,64,768]{2,1,0:T(8,128)} async-done(((f32[8,64,768]{2,1,0:T(8,128)}), f32[8,64,768]{2,1,0:T(8,128)}, u32[]{:S(2)}, u32[]{:S(2)}) %all-to-all-start.9) | async-done | bytes 1572896 | tf_op jit(solution)/shard_map/all_to_all | solution.py:23
  377.2 4.0 fusion.4
  381.2 6.0 %fusion.18 = f32[512,4608]{1,0:T(8,128)S(1)} fusion(bf16[512,768]{1,0:T(8,128)(2,1)S(1)} %get-tuple-element.8, bf16[768,4608]{1,0:T(8,128)(2,1)} %param.14), kind=kOutput, calls=%fused_computation.49 | convolution fusion | flops 3623878656 | bytes 17301504 | tf_op jit(solution)/shard_map/dot_general | solution.py:125
  387.8 3.5 collective-permute-start.4
  391.3 7.5 %collective-permute-done.4 = f32[8,32,4608]{2,1,0:T(8,128)S(1)} collective-permute-done((f32[8,32,4608]{2,1,0:T(8,128)S(1)}, f32[8,32,4608]{2,1,0:T(8,128)S(1)}, u32[]{:S(2)}, u32[]{:S(2)}) %collective-permute-start.4) | collective-permute-done | bytes 4718624 | tf_op jit(solution)/shard_map/ppermute | solution.py:37
  398.8 3.3 fusion.1
  402.2 4.7 all-to-all-start.10
  406.9 64.6 %psum.7 = f32[32]{0:T(128)S(1)} all-reduce(f32[32]{0:T(128)S(1)} %get-tuple-element.12), channel_id=1, replica_groups=mesh['line_outer'=8,'line_core'=2,'col'=8] {'col'}, use_global_device_ids=true, to_apply=%region_8.9 | all-reduce | flops 32 | bytes 256 | tf_op jit(solution)/shard_map/psum | solution.py:100
  471.6 2.8 reduce_sum.68
  474.4 1.7 maximum_minimum_fusion
  (50 shorter events, 5.4 us)
Async XLA Ops:
  7.2 186.3 %copy-start = (bf16[768,1536]{1,0:T(8,128)(2,1)S(1)}, bf16[768,1536]{1,0:T(8,128)(2,1)}, u32[]{:S(2)}) copy-start(bf16[768,1536]{1,0:T(8,128)(2,1)} %param.15) | copy-start | bytes 7077892
  7.2 63.7 %all-gather.2.cloned.1.call-start = ((), (), s32[]{:S(2)}) async-start(), calls=%async_computation.11 | async-start | bytes 10027008 | tf_op jit(solution)/shard_map/all_gather | solution.py:94
  113.7 4.5 copy-start.6
  113.7 23.0 %all-to-all-start.1 = ((f32[8,64,768]{2,1,0:T(8,128)}), f32[8,64,768]{2,1,0:T(8,128)}, u32[]{:S(2)}, u32[]{:S(2)}) async-start(f32[8,64,768]{2,1,0:T(8,128)} %broadcast_in_dim.41), calls=%async_computation.1 | async-start | bytes 3145728 | tf_op jit(solution)/shard_map/all_to_all | solution.py:23
  146.8 3.6 copy-start.5
  152.8 5.2 %collective-permute-start = (bf16[8,32,1536]{2,1,0:T(8,128)(2,1)S(1)}, bf16[8,32,1536]{2,1,0:T(8,128)(2,1)S(1)}, u32[]{:S(2)}, u32[]{:S(2)}) collective-permute-start(bf16[8,32,1536]{2,1,0:T(8,128)(2,1)S(1)} %fusion.7), channel_id=1, source_target_pairs={{0,8},{8,0},{1,9},{9,1},{2,10},{10,2},{3,11},{11,3},{4,12},{12,4},... | collective-permute-start | bytes 2359304 | tf_op jit(solution)/shard_map/ppermute | solution.py:37
  188.8 4.2 collective-permute-start.1
  223.5 4.4 copy-start.8
  223.5 22.8 %all-to-all-start.5 = ((f32[8,64,768]{2,1,0:T(8,128)}), f32[8,64,768]{2,1,0:T(8,128)}, u32[]{:S(2)}, u32[]{:S(2)}) async-start(f32[8,64,768]{2,1,0:T(8,128)} %broadcast_in_dim.78), calls=%async_computation.5 | async-start | bytes 3145728 | tf_op jit(solution)/shard_map/all_to_all | solution.py:23
  249.0 1.4 copy-start.2
  250.7 6.5 %collective-permute-start.2 = (f32[8,32,1536]{2,1,0:T(8,128)S(1)}, f32[8,32,1536]{2,1,0:T(8,128)S(1)}, u32[]{:S(2)}, u32[]{:S(2)}) collective-permute-start(f32[8,32,1536]{2,1,0:T(8,128)S(1)} %select_bitcast_fusion.1), channel_id=1, source_target_pairs={{0,8},{8,0},{1,9},{9,1},{2,10},{10,2},{3,11},{11,3},{4,12},{12,4},... | collective-permute-start | bytes 4718600 | tf_op jit(solution)/shard_map/ppermute | solution.py:37
  303.8 5.3 %collective-permute-start.3 = (f32[8,32,1536]{2,1,0:T(8,128)S(1)}, f32[8,32,1536]{2,1,0:T(8,128)S(1)}, u32[]{:S(2)}, u32[]{:S(2)}) collective-permute-start(f32[8,32,1536]{2,1,0:T(8,128)S(1)} %all_to_all.60), channel_id=1, source_target_pairs={{0,8},{8,0},{1,9},{9,1},{2,10},{10,2},{3,11},{11,3},{4,12},{12,4},... | collective-permute-start | bytes 4718600 | tf_op jit(solution)/shard_map/ppermute | solution.py:37
  354.4 4.4 copy-start.7
  354.4 22.8 %copy-start.3 = (f32[512,768]{1,0:T(8,128)S(1)}, f32[512,768]{1,0:T(8,128)}, u32[]{:S(2)}) copy-start(f32[512,768]{1,0:T(8,128)} %copy-done.2) | copy-start | bytes 4718596
  354.4 22.8 %all-to-all-start.9 = ((f32[8,64,768]{2,1,0:T(8,128)}), f32[8,64,768]{2,1,0:T(8,128)}, u32[]{:S(2)}, u32[]{:S(2)}) async-start(f32[8,64,768]{2,1,0:T(8,128)} %broadcast_in_dim.82), calls=%async_computation.9 | async-start | bytes 3145728 | tf_op jit(solution)/shard_map/all_to_all | solution.py:23
  387.8 11.0 %collective-permute-start.4 = (f32[8,32,4608]{2,1,0:T(8,128)S(1)}, f32[8,32,4608]{2,1,0:T(8,128)S(1)}, u32[]{:S(2)}, u32[]{:S(2)}) collective-permute-start(f32[8,32,4608]{2,1,0:T(8,128)S(1)} %select_bitcast_fusion), channel_id=1, source_target_pairs={{0,8},{8,0},{1,9},{9,1},{2,10},{10,2},{3,11},{11,3},{4,12},{12,4},... | collective-permute-start | bytes 14155784 | tf_op jit(solution)/shard_map/ppermute | solution.py:37
  402.2 69.4 %copy-start.10 = (f32[32]{0:T(128)S(1)}, f32[32]{0:T(128)}, u32[]{:S(2)}) copy-start(f32[32]{0:T(128)} %param.21) | copy-start | bytes 388
  402.2 69.4 %copy-start.11 = (f32[32]{0:T(128)S(1)}, f32[32]{0:T(128)}, u32[]{:S(2)}) copy-start(f32[32]{0:T(128)} %param.20) | copy-start | bytes 388
  402.2 69.4 %all-to-all-start.10 = ((f32[8,32,4608]{2,1,0:T(8,128)}), f32[8,32,4608]{2,1,0:T(8,128)}, u32[]{:S(2)}, u32[]{:S(2)}) async-start(f32[8,32,4608]{2,1,0:T(8,128)} %fusion.1), calls=%async_computation.10 | async-start | bytes 9437184 | tf_op jit(solution)/shard_map/all_to_all | solution.py:49
  471.5 2.8 copy-start.9
  471.5 2.8 copy-start.4
  471.6 4.6 copy-start.1
Sparse Core Ops, SparseCore 0:
  10.2 60.6 all-gather.1

commit v6 on v5

--- a/solution.py
+++ b/solution.py
@@ -91,13 +91,14 @@
     stacked = jnp.stack([extra_high, extra_low], axis=0)
     lines_dev = ptdf.shape[0]
     ptdf_turned = ptdf.T
+    local_total = jnp.sum(extra_high.astype(jnp.float32) + extra_low.astype(jnp.float32), axis=1)
+    bus_total = lax.psum(local_total, "col")
     portion = lax.all_gather(stacked, LINE, axis=1, tiled=True)
+    portion, bus_total = lax.optimization_barrier((portion, bus_total))
     count = portion.shape[1]
     flat = portion.reshape(2 * count, portion.shape[2])
     product = jnp.dot(flat, ptdf_turned, preferred_element_type=jnp.float32)
     flow_part = product[:count] + product[count:]
-    local_total = jnp.sum(extra_high.astype(jnp.float32) + extra_low.astype(jnp.float32), axis=1)
-    bus_total = lax.psum(local_total, "col")
     base_flow = full_sum(flow_part, "col")
     balance_new = balance_dual + (bus_total - demand) / BUSES
     base_new = dual_update(base_dual, base_flow, flow_limit[None, :])

time: 487 us -> 474 us (0.973)
  blocking collectives: 220 us -> 177 us
  waiting for transfers between devices: 134 us -> 167 us
    all_to_all x1, waiting for transfers between devices: 0.01 us -> 54.8 us  [line_summed_block(): parts = lax.all_to_all(pair_sum, LINE_OUTER, 0, 0, tiled=True)]
    psum x1, blocking collectives: 64.6 us -> 21.9 us  [on_device(): bus_total = lax.psum(local_total, 'col')]
    all_gather x1, waiting for transfers between devices: 61.2 us -> 39.2 us  [on_device(): portion = lax.all_gather(stacked, LINE, axis=1, tiled=True)]
  transfers between devices with their start and end apart: 10 -> 10, of which waited for: 9 -> 10; matrix products, arithmetic and copies ran while one was open for 0% -> 0% of each run, Pallas kernels for 0% -> 0%
where the time goes in v6:
time: 474 us; the launch traced here: 473 us
  blocking collectives  177 us (37%)
  waiting for transfers between devices  167 us (35%)
  other arithmetic  37.6 us (8%)
  starting transfers between devices  32.8 us (7%)
  local copies, waits for them, and re-layouts  23.3 us (5%)
  matrix products  21 us (4%)
  between operations  14.4 us (3%)
    all_to_all x3, blocking collectives, summed_block(): lax.all_to_all(value.reshape(n, rows, *value.shape[1:]), axis, 0, 0, tile...  79.2 us
    all_to_all x3, waiting for transfers between devices, gathered_rows(): whole = lax.all_to_all(copies, axis, 0, 0, tiled=True)  55.1 us
    all_to_all x1, waiting for transfers between devices, line_summed_block(): parts = lax.all_to_all(pair_sum, LINE_OUTER, 0, 0, tiled=True)  54.8 us
    all_to_all x2, blocking collectives, line_summed_block(): parts = lax.all_to_all(pair_sum, LINE_OUTER, 0, 0, tiled=True)  39.5 us
    all_gather x1, waiting for transfers between devices, on_device(): portion = lax.all_gather(stacked, LINE, axis=1, tiled=True)  39.2 us
    all_to_all x2, blocking collectives, line_gathered_rows(): mine = lax.all_to_all(copies, LINE_OUTER, 0, 0, tiled=True)  36.9 us
    psum x1, blocking collectives, on_device(): bus_total = lax.psum(local_total, 'col')  21.9 us
    ppermute x5, waiting for transfers between devices, swap_cores(): return lax.ppermute(value, LINE_CORE, [(0, 1), (1, 0)])  17.4 us
  transfers between devices with their start and end apart: 10, of which 10 were waited for; matrix products, arithmetic and copies ran while one was open for 0% of the time, Pallas kernels for 0%

profile of v6, /device:TPU:1, one launch (start us, length us, event | category | flops | bytes accessed | tf_op | source)
XLA Modules:
  0.0 473.1 jit_solution(2073628423927841574)
XLA Ops:
  7.2 1.6 fusion.15
  9.7 21.9 %psum.7 = f32[32]{0:T(128)S(1)} all-reduce(f32[32]{0:T(128)S(1)} %get-tuple-element.16), channel_id=1, replica_groups=mesh['line_outer'=8,'line_core'=2,'col'=8] {'col'}, use_global_device_ids=true, to_apply=%region_1.0 | all-reduce | flops 32 | bytes 256 | tf_op jit(solution)/shard_map/psum | solution.py:95
  31.7 39.2 %all-gather.2.cloned.1.call-done = bf16[2,512,4608]{2,1,0:T(8,128)(2,1)} async-done(((bf16[2,32,4608]{2,1,0:T(8,128)(2,1)}), bf16[2,512,4608]{2,1,0:T(8,128)(2,1)}) %all-gather.2.cloned.1.call-update) | async-done | bytes 9437200 | tf_op jit(solution)/shard_map/all_gather | solution.py:96
  70.9 12.1 %fusion.17 = f32[1024,768]{1,0:T(8,128)S(1)} fusion(bf16[1024,4608]{1,0:T(8,128)(2,1)} %bitcast.112, bf16[768,4608]{1,0:T(8,128)(2,1)} %param.14), kind=kOutput, calls=%fused_computation.48 | convolution fusion | flops 7247757312 | bytes 19660800 | tf_op jit(solution)/shard_map/dot_general | solution.py:100
  83.2 27.7 %all_to_all.55 = f32[8,64,768]{2,1,0:T(8,128)} all-to-all(f32[8,64,768]{2,1,0:T(8,128)S(1)} %bitcast.107), channel_id=1, replica_groups=mesh['line_outer'=8,'line_core'=2,'col'=8] {'col'}, dimensions={0} | all-to-all | bytes 3145728 | tf_op jit(solution)/shard_map/all_to_all | solution.py:16
  110.9 1.5 reduce_sum.64
  112.4 1.3 broadcast_in_dim.41
  113.7 4.4 all-to-all-start.1
  118.2 18.5 %all-to-all-done.1 = f32[8,64,768]{2,1,0:T(8,128)} async-done(((f32[8,64,768]{2,1,0:T(8,128)}), f32[8,64,768]{2,1,0:T(8,128)}, u32[]{:S(2)}, u32[]{:S(2)}) %all-to-all-start.1) | async-done | bytes 1572896 | tf_op jit(solution)/shard_map/all_to_all | solution.py:23
  136.7 3.0 copy.47
  139.7 7.1 %gather_fusion = f32[1536,512]{1,0:T(8,128)} fusion(f32[512,768]{0,1:T(8,128)} %copy.47, s32[2048]{0:T(1024)S(1)} %pad_clamp_fusion), kind=kCustom, calls=%fused_computation | custom fusion | bytes 6297600 | tf_op jit(solution)/shard_map/jit(_take)/gather | solution.py:109
  146.8 3.6 copy.48
  150.4 2.3 select_convert_fusion
  152.8 3.3 collective-permute-start
  156.1 1.9 collective-permute-done
  158.2 16.0 %all_to_all.56 = bf16[8,32,1536]{2,1,0:T(8,128)(2,1)S(1)} all-to-all(bf16[8,32,1536]{2,1,0:T(8,128)(2,1)S(1)} %fusion.9), channel_id=1, replica_groups=mesh['line_outer'=8,'line_core'=2,'col'=8] {'line_outer'}, dimensions={0} | all-to-all | bytes 1572864 | tf_op jit(solution)/shard_map/all_to_all | solution.py:49
  174.4 14.4 %all_to_all.57 = bf16[8,32,1536]{2,1,0:T(8,128)(2,1)S(1)} all-to-all(bf16[8,32,1536]{2,1,0:T(8,128)(2,1)S(1)} %broadcast_in_dim.77), channel_id=1, replica_groups=mesh['line_outer'=8,'line_core'=2,'col'=8] {'line_outer'}, dimensions={0} | all-to-all | bytes 1572864 | tf_op jit(solution)/shard_map/all_to_all | solution.py:57
  188.8 2.3 collective-permute-start.1
  191.1 1.9 collective-permute-done.1
  193.4 1.4 fusion.2
  194.9 25.9 %all_to_all.58 = f32[8,64,768]{2,1,0:T(8,128)} all-to-all(f32[8,64,768]{2,1,0:T(8,128)S(1)} %fusion.2), channel_id=1, replica_groups=mesh['line_outer'=8,'line_core'=2,'col'=8] {'col'}, dimensions={0} | all-to-all | bytes 3145728 | tf_op jit(solution)/shard_map/all_to_all | solution.py:16
  220.7 1.5 reduce_sum.66
  223.5 4.4 all-to-all-start.5
  227.9 18.3 %all-to-all-done.5 = f32[8,64,768]{2,1,0:T(8,128)} async-done(((f32[8,64,768]{2,1,0:T(8,128)}), f32[8,64,768]{2,1,0:T(8,128)}, u32[]{:S(2)}, u32[]{:S(2)}) %all-to-all-start.5) | async-done | bytes 1572896 | tf_op jit(solution)/shard_map/all_to_all | solution.py:23
  246.3 2.8 multiply_subtract_fusion
  249.1 1.4 fusion.10
  250.7 3.5 collective-permute-start.2
  254.1 3.0 collective-permute-done.2
  257.6 23.5 %all_to_all.59 = f32[8,32,1536]{2,1,0:T(8,128)S(1)} all-to-all(f32[8,32,1536]{2,1,0:T(8,128)S(1)} %bitcast_add_fusion.1), channel_id=1, replica_groups=mesh['line_outer'=8,'line_core'=2,'col'=8] {'line_outer'}, dimensions={0} | all-to-all | bytes 3145728 | tf_op jit(solution)/shard_map/all_to_all | solution.py:49
  281.3 22.5 %all_to_all.60 = f32[8,32,1536]{2,1,0:T(8,128)S(1)} all-to-all(f32[8,32,1536]{2,1,0:T(8,128)S(1)} %broadcast_in_dim.81), channel_id=1, replica_groups=mesh['line_outer'=8,'line_core'=2,'col'=8] {'line_outer'}, dimensions={0} | all-to-all | bytes 3145728 | tf_op jit(solution)/shard_map/all_to_all | solution.py:57
  303.8 2.2 collective-permute-start.3
  306.0 3.0 collective-permute-done.3
  309.6 2.0 bitcast_multiply_fusion
  311.6 3.6 copy.57
  315.1 10.6 %scatter_custom_fusion = f32[512,768]{0,1:T(8,128)S(1)} fusion(s32[1536]{0:T(1024)S(1)} %compare_select_fusion, f32[1536,512]{1,0:T(8,128)} %copy.57, f32[]{:T(128)} %constant.14.clone.1), kind=kCustom, calls=%fused_computation.31 | custom fusion | flops 786432 | bytes 1573376 | tf_op jit(solution)/shard_map/scatter-add | solution.py:122
  325.8 1.6 copy.58
  327.4 25.7 %all_to_all.61 = f32[8,64,768]{2,1,0:T(8,128)S(1)} all-to-all(f32[8,64,768]{2,1,0:T(8,128)} %bitcast.105), channel_id=1, replica_groups=mesh['line_outer'=8,'line_core'=2,'col'=8] {'col'}, dimensions={0} | all-to-all | bytes 3145728 | tf_op jit(solution)/shard_map/all_to_all | solution.py:16
  354.4 4.4 all-to-all-start.9
  358.9 18.3 %all-to-all-done.9 = f32[8,64,768]{2,1,0:T(8,128)} async-done(((f32[8,64,768]{2,1,0:T(8,128)}), f32[8,64,768]{2,1,0:T(8,128)}, u32[]{:S(2)}, u32[]{:S(2)}) %all-to-all-start.9) | async-done | bytes 1572896 | tf_op jit(solution)/shard_map/all_to_all | solution.py:23
  377.2 4.0 fusion.4
  381.2 6.0 %fusion.18 = f32[512,4608]{1,0:T(8,128)S(1)} fusion(bf16[512,768]{1,0:T(8,128)(2,1)S(1)} %get-tuple-element.12, bf16[768,4608]{1,0:T(8,128)(2,1)} %param.14), kind=kOutput, calls=%fused_computation.49 | convolution fusion | flops 3623878656 | bytes 17301504 | tf_op jit(solution)/shard_map/dot_general | solution.py:126
  387.8 3.5 collective-permute-start.4
  391.3 7.5 %collective-permute-done.4 = f32[8,32,4608]{2,1,0:T(8,128)S(1)} collective-permute-done((f32[8,32,4608]{2,1,0:T(8,128)S(1)}, f32[8,32,4608]{2,1,0:T(8,128)S(1)}, u32[]{:S(2)}, u32[]{:S(2)}) %collective-permute-start.4) | collective-permute-done | bytes 4718624 | tf_op jit(solution)/shard_map/ppermute | solution.py:37
  398.8 3.3 fusion.1
  402.2 4.7 %all-to-all-start.10 = ((f32[8,32,4608]{2,1,0:T(8,128)}), f32[8,32,4608]{2,1,0:T(8,128)}, u32[]{:S(2)}, u32[]{:S(2)}) async-start(f32[8,32,4608]{2,1,0:T(8,128)} %fusion.1), calls=%async_computation.10 | async-start | bytes 9437184 | tf_op jit(solution)/shard_map/all_to_all | solution.py:49
  407.0 54.8 %all-to-all-done.10 = f32[8,32,4608]{2,1,0:T(8,128)} async-done(((f32[8,32,4608]{2,1,0:T(8,128)}), f32[8,32,4608]{2,1,0:T(8,128)}, u32[]{:S(2)}, u32[]{:S(2)}) %all-to-all-start.10) | async-done | bytes 4718624 | tf_op jit(solution)/shard_map/all_to_all | solution.py:49
  461.7 2.8 reduce_sum.69
  464.5 1.7 maximum_minimum_fusion
  (50 shorter events, 6.6 us)
Async XLA Ops:
  7.2 186.3 %copy-start = (bf16[768,1536]{1,0:T(8,128)(2,1)S(1)}, bf16[768,1536]{1,0:T(8,128)(2,1)}, u32[]{:S(2)}) copy-start(bf16[768,1536]{1,0:T(8,128)(2,1)} %param.15) | copy-start | bytes 7077892
  7.2 63.7 %all-gather.2.cloned.1.call-start = ((), (), s32[]{:S(2)}) async-start(), calls=%async_computation.11 | async-start | bytes 10027008 | tf_op jit(solution)/shard_map/all_gather | solution.py:96
  113.7 4.5 copy-start.6
  113.7 23.0 %all-to-all-start.1 = ((f32[8,64,768]{2,1,0:T(8,128)}), f32[8,64,768]{2,1,0:T(8,128)}, u32[]{:S(2)}, u32[]{:S(2)}) async-start(f32[8,64,768]{2,1,0:T(8,128)} %broadcast_in_dim.41), calls=%async_computation.1 | async-start | bytes 3145728 | tf_op jit(solution)/shard_map/all_to_all | solution.py:23
  146.8 3.6 copy-start.5
  152.8 5.2 %collective-permute-start = (bf16[8,32,1536]{2,1,0:T(8,128)(2,1)S(1)}, bf16[8,32,1536]{2,1,0:T(8,128)(2,1)S(1)}, u32[]{:S(2)}, u32[]{:S(2)}) collective-permute-start(bf16[8,32,1536]{2,1,0:T(8,128)(2,1)S(1)} %fusion.7), channel_id=1, source_target_pairs={{0,8},{8,0},{1,9},{9,1},{2,10},{10,2},{3,11},{11,3},{4,12},{12,4},... | collective-permute-start | bytes 2359304 | tf_op jit(solution)/shard_map/ppermute | solution.py:37
  188.8 4.2 collective-permute-start.1
  223.5 4.4 copy-start.8
  223.5 22.8 %all-to-all-start.5 = ((f32[8,64,768]{2,1,0:T(8,128)}), f32[8,64,768]{2,1,0:T(8,128)}, u32[]{:S(2)}, u32[]{:S(2)}) async-start(f32[8,64,768]{2,1,0:T(8,128)} %broadcast_in_dim.78), calls=%async_computation.5 | async-start | bytes 3145728 | tf_op jit(solution)/shard_map/all_to_all | solution.py:23
  249.0 1.4 copy-start.2
  250.7 6.5 %collective-permute-start.2 = (f32[8,32,1536]{2,1,0:T(8,128)S(1)}, f32[8,32,1536]{2,1,0:T(8,128)S(1)}, u32[]{:S(2)}, u32[]{:S(2)}) collective-permute-start(f32[8,32,1536]{2,1,0:T(8,128)S(1)} %select_bitcast_fusion.1), channel_id=1, source_target_pairs={{0,8},{8,0},{1,9},{9,1},{2,10},{10,2},{3,11},{11,3},{4,12},{12,4},... | collective-permute-start | bytes 4718600 | tf_op jit(solution)/shard_map/ppermute | solution.py:37
  303.8 5.3 %collective-permute-start.3 = (f32[8,32,1536]{2,1,0:T(8,128)S(1)}, f32[8,32,1536]{2,1,0:T(8,128)S(1)}, u32[]{:S(2)}, u32[]{:S(2)}) collective-permute-start(f32[8,32,1536]{2,1,0:T(8,128)S(1)} %all_to_all.60), channel_id=1, source_target_pairs={{0,8},{8,0},{1,9},{9,1},{2,10},{10,2},{3,11},{11,3},{4,12},{12,4},... | collective-permute-start | bytes 4718600 | tf_op jit(solution)/shard_map/ppermute | solution.py:37
  354.4 4.4 copy-start.7
  354.4 22.8 %copy-start.3 = (f32[512,768]{1,0:T(8,128)S(1)}, f32[512,768]{1,0:T(8,128)}, u32[]{:S(2)}) copy-start(f32[512,768]{1,0:T(8,128)} %copy-done.2) | copy-start | bytes 4718596
  354.4 22.8 %all-to-all-start.9 = ((f32[8,64,768]{2,1,0:T(8,128)}), f32[8,64,768]{2,1,0:T(8,128)}, u32[]{:S(2)}, u32[]{:S(2)}) async-start(f32[8,64,768]{2,1,0:T(8,128)} %broadcast_in_dim.82), calls=%async_computation.9 | async-start | bytes 3145728 | tf_op jit(solution)/shard_map/all_to_all | solution.py:23
  387.8 11.0 %collective-permute-start.4 = (f32[8,32,4608]{2,1,0:T(8,128)S(1)}, f32[8,32,4608]{2,1,0:T(8,128)S(1)}, u32[]{:S(2)}, u32[]{:S(2)}) collective-permute-start(f32[8,32,4608]{2,1,0:T(8,128)S(1)} %select_bitcast_fusion), channel_id=1, source_target_pairs={{0,8},{8,0},{1,9},{9,1},{2,10},{10,2},{3,11},{11,3},{4,12},{12,4},... | collective-permute-start | bytes 14155784 | tf_op jit(solution)/shard_map/ppermute | solution.py:37
  402.2 4.8 %copy-start.10 = (f32[32]{0:T(128)S(1)}, f32[32]{0:T(128)}, u32[]{:S(2)}) copy-start(f32[32]{0:T(128)} %param.21) | copy-start | bytes 388
  402.2 4.8 %copy-start.11 = (f32[32]{0:T(128)S(1)}, f32[32]{0:T(128)}, u32[]{:S(2)}) copy-start(f32[32]{0:T(128)} %param.20) | copy-start | bytes 388
  402.2 59.6 %all-to-all-start.10 = ((f32[8,32,4608]{2,1,0:T(8,128)}), f32[8,32,4608]{2,1,0:T(8,128)}, u32[]{:S(2)}, u32[]{:S(2)}) async-start(f32[8,32,4608]{2,1,0:T(8,128)} %fusion.1), calls=%async_computation.10 | async-start | bytes 9437184 | tf_op jit(solution)/shard_map/all_to_all | solution.py:49
  406.9 57.6 %copy-start.9 = (f32[32]{0:T(128)}, f32[32]{0:T(128)S(1)}, u32[]{:S(2)}) copy-start(f32[32]{0:T(128)S(1)} %multiply_add_fusion) | copy-start | bytes 388
  407.0 57.6 %copy-start.4 = (f32[32,4608]{1,0:T(8,128)S(1)}, f32[32,4608]{1,0:T(8,128)}, u32[]{:S(2)}) copy-start(f32[32,4608]{1,0:T(8,128)} %param.16) | copy-start | bytes 1769476
  461.7 4.5 copy-start.1
Sparse Core Ops, SparseCore 0:
  10.2 60.6 all-gather.1

commit v7 on v6

--- a/solution.py
+++ b/solution.py
@@ -64,6 +64,19 @@
     return line_gathered_rows(line_summed_block(value))
 
 
+def split_three(value):
+    high = value.astype(jnp.bfloat16)
+    rest = value - high.astype(jnp.float32)
+    middle = rest.astype(jnp.bfloat16)
+    low = (rest - middle.astype(jnp.float32)).astype(jnp.bfloat16)
+    return jnp.concatenate([high, middle, low], axis=0)
+
+
+def add_three(value):
+    rows = value.shape[0] // 3
+    return value[:rows] + value[rows : 2 * rows] + value[2 * rows :]
+
+
 def dual_update(dual, flow, limit):
     shifted = dual + dual_step * flow
     return shifted - dual_step * jnp.clip(shifted / dual_step, -limit, limit)
@@ -105,8 +118,9 @@
     first_line = lax.axis_index(LINE) * lines_dev
     local_line = outage_line - first_line
     inside = (local_line >= 0) & (local_line < lines_dev)
-    safe_line = jnp.where(inside, local_line, 0)
-    picked = jnp.take(base_flow, safe_line, axis=1)
+    lines_seen = lax.broadcasted_iota(jnp.int32, (lines_dev, outage_line.shape[0]), 0)
+    chosen = (lines_seen == local_line[None, :]).astype(jnp.bfloat16)
+    picked = add_three(jnp.dot(split_three(base_flow), chosen, preferred_element_type=jnp.float32))
     weighted = jnp.where(inside[None, :], picked * outage_weight[None, :], 0.0)
     outage_flow = line_full_sum(weighted.astype(jnp.bfloat16))
     shift_part = jnp.dot(outage_flow, lodf.T, preferred_element_type=jnp.float32)
@@ -115,11 +129,13 @@
     post_new = dual_update(post_dual, post_flow, emergency_limit[None, :])
     back_part = jnp.dot(post_new.astype(jnp.bfloat16), lodf, preferred_element_type=jnp.float32)
     back_flow = line_full_sum(back_part)
-    target = jnp.where(inside, local_line, lines_dev)
-    returned_part = (
-        jnp.zeros(base_new.shape, jnp.float32)
-        .at[:, target]
-        .add(back_flow * outage_weight[None, :], mode="drop")
+    returned_part = add_three(
+        lax.dot_general(
+            split_three(back_flow * outage_weight[None, :]),
+            chosen,
+            (((1,), (1,)), ((), ())),
+            preferred_element_type=jnp.float32,
+        )
     )
     returned = full_sum(returned_part, "col")
     line_total = (base_new + post_new + returned).astype(jnp.bfloat16)

time: 474 us -> 453 us (0.956)
  local copies, waits for them, and re-layouts: 23.3 us -> 4.11 us
  other arithmetic: 37.6 us -> 27.6 us
  matrix products: 21 us -> 28.9 us
    gather x2 -> x0, local copies, waits for them, and re-layouts: 10.7 us -> none  [on_device(): picked = jnp.take(base_flow, safe_line, axis=1)]
    scatter-add x1 -> x0, other arithmetic: 10.6 us -> none  [on_device(): returned_part = jnp.zeros(base_new.shape, jnp.float32).at[:, target].add(...]
    dot_general x0 -> x2, matrix products: none -> 7.89 us  [the longest x1 3.97 us: on_device(): jnp.dot(split_three(base_flow), chosen, preferred_element_type=jnp.float32)]
where the time goes in v7:
time: 453 us; the launch traced here: 452 us
  blocking collectives  177 us (39%)
  waiting for transfers between devices  166 us (37%)
  starting transfers between devices  33 us (7%)
  matrix products  28.9 us (6%)
  other arithmetic  27.6 us (6%)
  between operations  14.4 us (3%)
    all_to_all x3, blocking collectives, summed_block(): lax.all_to_all(value.reshape(n, rows, *value.shape[1:]), axis, 0, 0, tile...  79 us
    all_to_all x3, waiting for transfers between devices, gathered_rows(): whole = lax.all_to_all(copies, axis, 0, 0, tiled=True)  55 us
    all_to_all x1, waiting for transfers between devices, line_summed_block(): parts = lax.all_to_all(pair_sum, LINE_OUTER, 0, 0, tiled=True)  54.8 us
    all_to_all x2, blocking collectives, line_summed_block(): parts = lax.all_to_all(pair_sum, LINE_OUTER, 0, 0, tiled=True)  39.5 us
    all_gather x1, waiting for transfers between devices, on_device(): portion = lax.all_gather(stacked, LINE, axis=1, tiled=True)  39.2 us
    all_to_all x2, blocking collectives, line_gathered_rows(): mine = lax.all_to_all(copies, LINE_OUTER, 0, 0, tiled=True)  36.9 us
    psum x1, blocking collectives, on_device(): bus_total = lax.psum(local_total, 'col')  21.9 us
    ppermute x5, waiting for transfers between devices, swap_cores(): return lax.ppermute(value, LINE_CORE, [(0, 1), (1, 0)])  17.4 us
  transfers between devices with their start and end apart: 10, of which 10 were waited for; matrix products, arithmetic and copies ran while one was open for 0% of the time, Pallas kernels for 0%

profile of v7, /device:TPU:1, one launch (start us, length us, event | category | flops | bytes accessed | tf_op | source)
XLA Modules:
  0.0 451.7 jit_solution(17375785098329306630)
XLA Ops:
  7.2 1.6 fusion.34
  8.8 0.9 pad_maximum_fusion
  9.7 21.9 %psum.7 = f32[32]{0:T(128)S(1)} all-reduce(f32[32]{0:T(128)S(1)} %get-tuple-element.17), channel_id=1, replica_groups=mesh['line_outer'=8,'line_core'=2,'col'=8] {'col'}, use_global_device_ids=true, to_apply=%region_1.0 | all-reduce | flops 32 | bytes 256 | tf_op jit(solution)/shard_map/psum | solution.py:108
  31.7 39.2 %all-gather.2.cloned.1.call-done = bf16[2,512,4608]{2,1,0:T(8,128)(2,1)} async-done(((bf16[2,32,4608]{2,1,0:T(8,128)(2,1)}), bf16[2,512,4608]{2,1,0:T(8,128)(2,1)}) %all-gather.2.cloned.1.call-update) | async-done | bytes 9437200 | tf_op jit(solution)/shard_map/all_gather | solution.py:109
  70.9 12.1 %fusion.38 = f32[1024,768]{1,0:T(8,128)S(1)} fusion(bf16[1024,4608]{1,0:T(8,128)(2,1)} %bitcast.141, bf16[768,4608]{1,0:T(8,128)(2,1)} %param.14), kind=kOutput, calls=%fused_computation.74 | convolution fusion | flops 7247757312 | bytes 19660800 | tf_op jit(solution)/shard_map/dot_general | solution.py:113
  83.2 27.7 %all_to_all.55 = f32[8,64,768]{2,1,0:T(8,128)} all-to-all(f32[8,64,768]{2,1,0:T(8,128)S(1)} %bitcast.135), channel_id=1, replica_groups=mesh['line_outer'=8,'line_core'=2,'col'=8] {'col'}, dimensions={0} | all-to-all | bytes 3145728 | tf_op jit(solution)/shard_map/all_to_all | solution.py:16
  110.9 1.5 reduce_sum.64
  112.4 1.3 broadcast_in_dim.22
  113.7 4.4 all-to-all-start.1
  118.2 18.5 %all-to-all-done.1 = f32[8,64,768]{2,1,0:T(8,128)} async-done(((f32[8,64,768]{2,1,0:T(8,128)}), f32[8,64,768]{2,1,0:T(8,128)}, u32[]{:S(2)}, u32[]{:S(2)}) %all-to-all-start.1) | async-done | bytes 1572896 | tf_op jit(solution)/shard_map/all_to_all | solution.py:23
  136.7 1.5 bitcast_convert_fusion
  138.1 1.6 fusion.27
  139.8 4.0 fusion.8
  143.7 1.2 fusion.11
  145.0 3.3 collective-permute-start
  148.3 1.9 collective-permute-done
  150.4 16.0 %all_to_all.56 = bf16[8,32,1536]{2,1,0:T(8,128)(2,1)S(1)} all-to-all(bf16[8,32,1536]{2,1,0:T(8,128)(2,1)S(1)} %fusion.30), channel_id=1, replica_groups=mesh['line_outer'=8,'line_core'=2,'col'=8] {'line_outer'}, dimensions={0} | all-to-all | bytes 1572864 | tf_op jit(solution)/shard_map/all_to_all | solution.py:49
  166.6 14.4 %all_to_all.57 = bf16[8,32,1536]{2,1,0:T(8,128)(2,1)S(1)} all-to-all(bf16[8,32,1536]{2,1,0:T(8,128)(2,1)S(1)} %broadcast_in_dim.25), channel_id=1, replica_groups=mesh['line_outer'=8,'line_core'=2,'col'=8] {'line_outer'}, dimensions={0} | all-to-all | bytes 1572864 | tf_op jit(solution)/shard_map/all_to_all | solution.py:57
  181.0 2.3 collective-permute-start.1
  183.3 1.9 collective-permute-done.1
  185.4 1.4 fusion.18
  186.8 25.8 %all_to_all.58 = f32[8,64,768]{2,1,0:T(8,128)} all-to-all(f32[8,64,768]{2,1,0:T(8,128)S(1)} %fusion.18), channel_id=1, replica_groups=mesh['line_outer'=8,'line_core'=2,'col'=8] {'col'}, dimensions={0} | all-to-all | bytes 3145728 | tf_op jit(solution)/shard_map/all_to_all | solution.py:16
  212.6 1.5 reduce_sum.66
  214.1 1.3 broadcast_in_dim.26
  215.4 4.6 %all-to-all-start.5 = ((f32[8,64,768]{2,1,0:T(8,128)}), f32[8,64,768]{2,1,0:T(8,128)}, u32[]{:S(2)}, u32[]{:S(2)}) async-start(f32[8,64,768]{2,1,0:T(8,128)} %broadcast_in_dim.26), calls=%async_computation.5 | async-start | bytes 3145728 | tf_op jit(solution)/shard_map/all_to_all | solution.py:23
  220.0 18.1 %all-to-all-done.5 = f32[8,64,768]{2,1,0:T(8,128)} async-done(((f32[8,64,768]{2,1,0:T(8,128)}), f32[8,64,768]{2,1,0:T(8,128)}, u32[]{:S(2)}, u32[]{:S(2)}) %all-to-all-start.5) | async-done | bytes 1572896 | tf_op jit(solution)/shard_map/all_to_all | solution.py:23
  238.2 2.8 multiply_subtract_fusion
  241.0 1.4 fusion.31
  242.6 3.5 collective-permute-start.2
  246.0 3.0 collective-permute-done.2
  249.5 23.5 %all_to_all.59 = f32[8,32,1536]{2,1,0:T(8,128)S(1)} all-to-all(f32[8,32,1536]{2,1,0:T(8,128)S(1)} %bitcast_add_fusion.1), channel_id=1, replica_groups=mesh['line_outer'=8,'line_core'=2,'col'=8] {'line_outer'}, dimensions={0} | all-to-all | bytes 3145728 | tf_op jit(solution)/shard_map/all_to_all | solution.py:49
  273.2 22.5 %all_to_all.60 = f32[8,32,1536]{2,1,0:T(8,128)S(1)} all-to-all(f32[8,32,1536]{2,1,0:T(8,128)S(1)} %broadcast_in_dim.27), channel_id=1, replica_groups=mesh['line_outer'=8,'line_core'=2,'col'=8] {'line_outer'}, dimensions={0} | all-to-all | bytes 3145728 | tf_op jit(solution)/shard_map/all_to_all | solution.py:57
  295.7 2.2 collective-permute-start.3
  297.9 3.0 collective-permute-done.3
  301.9 3.9 fusion
  306.1 25.5 %all_to_all.61 = f32[8,64,768]{2,1,0:T(8,128)S(1)} all-to-all(f32[8,64,768]{2,1,0:T(8,128)S(1)} %bitcast.136), channel_id=1, replica_groups=mesh['line_outer'=8,'line_core'=2,'col'=8] {'col'}, dimensions={0} | all-to-all | bytes 3145728 | tf_op jit(solution)/shard_map/all_to_all | solution.py:16
  331.7 1.3 broadcast_in_dim.28
  333.0 4.4 all-to-all-start.9
  337.4 18.3 %all-to-all-done.9 = f32[8,64,768]{2,1,0:T(8,128)} async-done(((f32[8,64,768]{2,1,0:T(8,128)}), f32[8,64,768]{2,1,0:T(8,128)}, u32[]{:S(2)}, u32[]{:S(2)}) %all-to-all-start.9) | async-done | bytes 1572896 | tf_op jit(solution)/shard_map/all_to_all | solution.py:23
  355.8 4.0 fusion.23
  359.8 6.0 %fusion.39 = f32[512,4608]{1,0:T(8,128)S(1)} fusion(bf16[512,768]{1,0:T(8,128)(2,1)S(1)} %get-tuple-element.8, bf16[768,4608]{1,0:T(8,128)(2,1)} %param.14), kind=kOutput, calls=%fused_computation.75 | convolution fusion | flops 3623878656 | bytes 17301504 | tf_op jit(solution)/shard_map/dot_general | solution.py:142
  366.4 3.5 collective-permute-start.4
  369.9 7.5 %collective-permute-done.4 = f32[8,32,4608]{2,1,0:T(8,128)S(1)} collective-permute-done((f32[8,32,4608]{2,1,0:T(8,128)S(1)}, f32[8,32,4608]{2,1,0:T(8,128)S(1)}, u32[]{:S(2)}, u32[]{:S(2)}) %collective-permute-start.4) | collective-permute-done | bytes 4718624 | tf_op jit(solution)/shard_map/ppermute | solution.py:37
  377.4 3.3 fusion.7
  380.7 4.7 %all-to-all-start.10 = ((f32[8,32,4608]{2,1,0:T(8,128)}), f32[8,32,4608]{2,1,0:T(8,128)}, u32[]{:S(2)}, u32[]{:S(2)}) async-start(f32[8,32,4608]{2,1,0:T(8,128)} %fusion.7), calls=%async_computation.10 | async-start | bytes 9437184 | tf_op jit(solution)/shard_map/all_to_all | solution.py:49
  385.5 54.8 %all-to-all-done.10 = f32[8,32,4608]{2,1,0:T(8,128)} async-done(((f32[8,32,4608]{2,1,0:T(8,128)}), f32[8,32,4608]{2,1,0:T(8,128)}, u32[]{:S(2)}, u32[]{:S(2)}) %all-to-all-start.10) | async-done | bytes 4718624 | tf_op jit(solution)/shard_map/all_to_all | solution.py:49
  440.3 2.8 reduce_sum.69
  443.1 1.7 maximum_minimum_fusion
  (45 shorter events, 3.6 us)
Async XLA Ops:
  7.2 178.2 %copy-start = (bf16[768,1536]{1,0:T(8,128)(2,1)S(1)}, bf16[768,1536]{1,0:T(8,128)(2,1)}, u32[]{:S(2)}) copy-start(bf16[768,1536]{1,0:T(8,128)(2,1)} %param.15) | copy-start | bytes 7077892
  7.2 63.7 %all-gather.2.cloned.1.call-start = ((), (), s32[]{:S(2)}) async-start(), calls=%async_computation.11 | async-start | bytes 10027008 | tf_op jit(solution)/shard_map/all_gather | solution.py:109
  113.7 4.4 copy-start.8
  113.7 22.9 %all-to-all-start.1 = ((f32[8,64,768]{2,1,0:T(8,128)}), f32[8,64,768]{2,1,0:T(8,128)}, u32[]{:S(2)}, u32[]{:S(2)}) async-start(f32[8,64,768]{2,1,0:T(8,128)} %broadcast_in_dim.22), calls=%async_computation.1 | async-start | bytes 3145728 | tf_op jit(solution)/shard_map/all_to_all | solution.py:23
  139.7 4.0 copy-start.5
  145.0 5.2 %collective-permute-start = (bf16[8,32,1536]{2,1,0:T(8,128)(2,1)S(1)}, bf16[8,32,1536]{2,1,0:T(8,128)(2,1)S(1)}, u32[]{:S(2)}, u32[]{:S(2)}) collective-permute-start(bf16[8,32,1536]{2,1,0:T(8,128)(2,1)S(1)} %fusion.28), channel_id=1, source_target_pairs={{0,8},{8,0},{1,9},{9,1},{2,10},{10,2},{3,11},{11,3},{4,12},{12,4},... | collective-permute-start | bytes 2359304 | tf_op jit(solution)/shard_map/ppermute | solution.py:37
  181.0 4.2 collective-permute-start.1
  215.4 4.6 %copy-start.7 = (f32[768]{0:T(1024)S(1)}, f32[768]{0:T(1024)}, u32[]{:S(2)}) copy-start(f32[768]{0:T(1024)} %param.25) | copy-start | bytes 9220
  215.4 22.8 %all-to-all-start.5 = ((f32[8,64,768]{2,1,0:T(8,128)}), f32[8,64,768]{2,1,0:T(8,128)}, u32[]{:S(2)}, u32[]{:S(2)}) async-start(f32[8,64,768]{2,1,0:T(8,128)} %broadcast_in_dim.26), calls=%async_computation.5 | async-start | bytes 3145728 | tf_op jit(solution)/shard_map/all_to_all | solution.py:23
  241.0 1.4 copy-start.2
  242.6 6.5 %collective-permute-start.2 = (f32[8,32,1536]{2,1,0:T(8,128)S(1)}, f32[8,32,1536]{2,1,0:T(8,128)S(1)}, u32[]{:S(2)}, u32[]{:S(2)}) collective-permute-start(f32[8,32,1536]{2,1,0:T(8,128)S(1)} %select_bitcast_fusion.1), channel_id=1, source_target_pairs={{0,8},{8,0},{1,9},{9,1},{2,10},{10,2},{3,11},{11,3},{4,12},{12,4},... | collective-permute-start | bytes 4718600 | tf_op jit(solution)/shard_map/ppermute | solution.py:37
  295.7 5.3 %collective-permute-start.3 = (f32[8,32,1536]{2,1,0:T(8,128)S(1)}, f32[8,32,1536]{2,1,0:T(8,128)S(1)}, u32[]{:S(2)}, u32[]{:S(2)}) collective-permute-start(f32[8,32,1536]{2,1,0:T(8,128)S(1)} %all_to_all.60), channel_id=1, source_target_pairs={{0,8},{8,0},{1,9},{9,1},{2,10},{10,2},{3,11},{11,3},{4,12},{12,4},... | collective-permute-start | bytes 4718600 | tf_op jit(solution)/shard_map/ppermute | solution.py:37
  333.0 4.4 copy-start.6
  333.0 22.8 %copy-start.3 = (f32[512,768]{1,0:T(8,128)S(1)}, f32[512,768]{1,0:T(8,128)}, u32[]{:S(2)}) copy-start(f32[512,768]{1,0:T(8,128)} %copy-done.2) | copy-start | bytes 4718596
  333.0 22.8 %all-to-all-start.9 = ((f32[8,64,768]{2,1,0:T(8,128)}), f32[8,64,768]{2,1,0:T(8,128)}, u32[]{:S(2)}, u32[]{:S(2)}) async-start(f32[8,64,768]{2,1,0:T(8,128)} %broadcast_in_dim.28), calls=%async_computation.9 | async-start | bytes 3145728 | tf_op jit(solution)/shard_map/all_to_all | solution.py:23
  366.4 11.0 %collective-permute-start.4 = (f32[8,32,4608]{2,1,0:T(8,128)S(1)}, f32[8,32,4608]{2,1,0:T(8,128)S(1)}, u32[]{:S(2)}, u32[]{:S(2)}) collective-permute-start(f32[8,32,4608]{2,1,0:T(8,128)S(1)} %select_bitcast_fusion), channel_id=1, source_target_pairs={{0,8},{8,0},{1,9},{9,1},{2,10},{10,2},{3,11},{11,3},{4,12},{12,4},... | collective-permute-start | bytes 14155784 | tf_op jit(solution)/shard_map/ppermute | solution.py:37
  380.7 4.7 %copy-start.10 = (f32[32]{0:T(128)S(1)}, f32[32]{0:T(128)}, u32[]{:S(2)}) copy-start(f32[32]{0:T(128)} %param.21) | copy-start | bytes 388
  380.7 4.8 %copy-start.11 = (f32[32]{0:T(128)S(1)}, f32[32]{0:T(128)}, u32[]{:S(2)}) copy-start(f32[32]{0:T(128)} %param.20) | copy-start | bytes 388
  380.7 59.5 %all-to-all-start.10 = ((f32[8,32,4608]{2,1,0:T(8,128)}), f32[8,32,4608]{2,1,0:T(8,128)}, u32[]{:S(2)}, u32[]{:S(2)}) async-start(f32[8,32,4608]{2,1,0:T(8,128)} %fusion.7), calls=%async_computation.10 | async-start | bytes 9437184 | tf_op jit(solution)/shard_map/all_to_all | solution.py:49
  385.5 57.6 %copy-start.9 = (f32[32]{0:T(128)}, f32[32]{0:T(128)S(1)}, u32[]{:S(2)}) copy-start(f32[32]{0:T(128)S(1)} %multiply_add_fusion) | copy-start | bytes 388
  385.5 57.6 %copy-start.4 = (f32[32,4608]{1,0:T(8,128)S(1)}, f32[32,4608]{1,0:T(8,128)}, u32[]{:S(2)}) copy-start(f32[32,4608]{1,0:T(8,128)} %param.16) | copy-start | bytes 1769476
  440.3 4.5 %copy-start.1 = (bf16[768,1536]{1,0:T(8,128)(2,1)S(1)}, bf16[768,1536]{1,0:T(8,128)(2,1)}, u32[]{:S(2)}) copy-start(bf16[768,1536]{1,0:T(8,128)(2,1)} %param.15) | copy-start | bytes 7077892
Sparse Core Ops, SparseCore 0:
  10.2 60.6 all-gather.1

commit v8 on v6

--- a/solution.py
+++ b/solution.py
@@ -105,8 +105,10 @@
     first_line = lax.axis_index(LINE) * lines_dev
     local_line = outage_line - first_line
     inside = (local_line >= 0) & (local_line < lines_dev)
-    safe_line = jnp.where(inside, local_line, 0)
-    picked = jnp.take(base_flow, safe_line, axis=1)
+    lines_seen = lax.broadcasted_iota(jnp.int32, (lines_dev, outage_line.shape[0]), 0)
+    chosen = (lines_seen == local_line[None, :]).astype(jnp.float32)
+    exact = lax.Precision.HIGHEST
+    picked = jnp.dot(base_flow, chosen, precision=exact, preferred_element_type=jnp.float32)
     weighted = jnp.where(inside[None, :], picked * outage_weight[None, :], 0.0)
     outage_flow = line_full_sum(weighted.astype(jnp.bfloat16))
     shift_part = jnp.dot(outage_flow, lodf.T, preferred_element_type=jnp.float32)
@@ -115,11 +117,12 @@
     post_new = dual_update(post_dual, post_flow, emergency_limit[None, :])
     back_part = jnp.dot(post_new.astype(jnp.bfloat16), lodf, preferred_element_type=jnp.float32)
     back_flow = line_full_sum(back_part)
-    target = jnp.where(inside, local_line, lines_dev)
-    returned_part = (
-        jnp.zeros(base_new.shape, jnp.float32)
-        .at[:, target]
-        .add(back_flow * outage_weight[None, :], mode="drop")
+    returned_part = lax.dot_general(
+        back_flow * outage_weight[None, :],
+        chosen,
+        (((1,), (1,)), ((), ())),
+        precision=exact,
+        preferred_element_type=jnp.float32,
     )
     returned = full_sum(returned_part, "col")
     line_total = (base_new + post_new + returned).astype(jnp.bfloat16)

time: 474 us -> 450 us (0.949)
  local copies, waits for them, and re-layouts: 23.3 us -> 4.1 us
  other arithmetic: 37.6 us -> 22.8 us
  matrix products: 21 us -> 30.7 us
    gather x2 -> x0, local copies, waits for them, and re-layouts: 10.7 us -> none  [on_device(): picked = jnp.take(base_flow, safe_line, axis=1)]
    scatter-add x1 -> x0, other arithmetic: 10.6 us -> none  [on_device(): returned_part = jnp.zeros(base_new.shape, jnp.float32).at[:, target].add(...]
    dot_general x0 -> x2, matrix products: none -> 9.75 us  [the longest x1 5.45 us: on_device(): jnp.dot(base_flow, chosen, precision=exact, preferred_element_type=jnp.fl...]
where the time goes in v8:
time: 450 us; the launch traced here: 449 us
  blocking collectives  177 us (39%)
  waiting for transfers between devices  167 us (37%)
  starting transfers between devices  32.6 us (7%)
  matrix products  30.7 us (7%)
  other arithmetic  22.8 us (5%)
  between operations  14.4 us (3%)
    all_to_all x3, blocking collectives, summed_block(): lax.all_to_all(value.reshape(n, rows, *value.shape[1:]), axis, 0, 0, tile...  78.8 us
    all_to_all x3, waiting for transfers between devices, gathered_rows(): whole = lax.all_to_all(copies, axis, 0, 0, tiled=True)  55.1 us
    all_to_all x1, waiting for transfers between devices, line_summed_block(): parts = lax.all_to_all(pair_sum, LINE_OUTER, 0, 0, tiled=True)  54.8 us
    all_to_all x2, blocking collectives, line_summed_block(): parts = lax.all_to_all(pair_sum, LINE_OUTER, 0, 0, tiled=True)  39.5 us
    all_gather x1, waiting for transfers between devices, on_device(): portion = lax.all_gather(stacked, LINE, axis=1, tiled=True)  39.2 us
    all_to_all x2, blocking collectives, line_gathered_rows(): mine = lax.all_to_all(copies, LINE_OUTER, 0, 0, tiled=True)  37.2 us
    psum x1, blocking collectives, on_device(): bus_total = lax.psum(local_total, 'col')  21.9 us
    ppermute x5, waiting for transfers between devices, swap_cores(): return lax.ppermute(value, LINE_CORE, [(0, 1), (1, 0)])  17.4 us
  transfers between devices with their start and end apart: 10, of which 10 were waited for; matrix products, arithmetic and copies ran while one was open for 0% of the time, Pallas kernels for 0%

profile of v8, /device:TPU:1, one launch (start us, length us, event | category | flops | bytes accessed | tf_op | source)
XLA Modules:
  0.0 448.6 jit_solution(4846267917833410468)
XLA Ops:
  7.2 1.6 fusion.22
  8.8 0.9 pad_maximum_fusion
  9.7 21.9 %psum.7 = f32[32]{0:T(128)S(1)} all-reduce(f32[32]{0:T(128)S(1)} %get-tuple-element.12), channel_id=1, replica_groups=mesh['line_outer'=8,'line_core'=2,'col'=8] {'col'}, use_global_device_ids=true, to_apply=%region_1.0 | all-reduce | flops 32 | bytes 256 | tf_op jit(solution)/shard_map/psum | solution.py:95
  31.7 39.2 %all-gather.2.cloned.1.call-done = bf16[2,512,4608]{2,1,0:T(8,128)(2,1)} async-done(((bf16[2,32,4608]{2,1,0:T(8,128)(2,1)}), bf16[2,512,4608]{2,1,0:T(8,128)(2,1)}) %all-gather.2.cloned.1.call-update) | async-done | bytes 9437200 | tf_op jit(solution)/shard_map/all_gather | solution.py:96
  70.9 12.1 %fusion.24 = f32[1024,768]{1,0:T(8,128)S(1)} fusion(bf16[1024,4608]{1,0:T(8,128)(2,1)} %bitcast.112, bf16[768,4608]{1,0:T(8,128)(2,1)} %param.14), kind=kOutput, calls=%fused_computation.49 | convolution fusion | flops 7247757312 | bytes 19660800 | tf_op jit(solution)/shard_map/dot_general | solution.py:100
  83.2 27.7 %all_to_all.55 = f32[8,64,768]{2,1,0:T(8,128)} all-to-all(f32[8,64,768]{2,1,0:T(8,128)S(1)} %bitcast.107), channel_id=1, replica_groups=mesh['line_outer'=8,'line_core'=2,'col'=8] {'col'}, dimensions={0} | all-to-all | bytes 3145728 | tf_op jit(solution)/shard_map/all_to_all | solution.py:16
  110.9 1.5 reduce_sum.64
  112.4 1.3 broadcast_in_dim.22
  113.7 4.4 all-to-all-start.1
  118.2 18.5 %all-to-all-done.1 = f32[8,64,768]{2,1,0:T(8,128)} async-done(((f32[8,64,768]{2,1,0:T(8,128)}), f32[8,64,768]{2,1,0:T(8,128)}, u32[]{:S(2)}, u32[]{:S(2)}) %all-to-all-start.1) | async-done | bytes 1572896 | tf_op jit(solution)/shard_map/all_to_all | solution.py:23
  136.7 5.4 %fusion.8 = bf16[512,1536]{1,0:T(8,128)(2,1)S(1)} fusion(f32[512,768]{1,0:T(8,128)} %bitcast.4, s32[1536]{0:T(1024)S(1)} %get-tuple-element.11, f32[1536]{0:T(1024)S(1)} %copy-done.7, pred[1536]{0:T(1024)(128)(4,1)S(1)} %get-tuple-element.10), kind=kOutput, calls=%fused_computation.12 | convolution fusion | flops 7251296256 | bytes 3159552 | tf_op jit(solution)/shard_map/dot_general | solution.py:111
  142.2 3.3 collective-permute-start
  145.5 1.9 collective-permute-done
  147.5 16.0 %all_to_all.56 = bf16[8,32,1536]{2,1,0:T(8,128)(2,1)S(1)} all-to-all(bf16[8,32,1536]{2,1,0:T(8,128)(2,1)S(1)} %fusion.18), channel_id=1, replica_groups=mesh['line_outer'=8,'line_core'=2,'col'=8] {'line_outer'}, dimensions={0} | all-to-all | bytes 1572864 | tf_op jit(solution)/shard_map/all_to_all | solution.py:49
  163.7 14.4 %all_to_all.57 = bf16[8,32,1536]{2,1,0:T(8,128)(2,1)S(1)} all-to-all(bf16[8,32,1536]{2,1,0:T(8,128)(2,1)S(1)} %broadcast_in_dim.25), channel_id=1, replica_groups=mesh['line_outer'=8,'line_core'=2,'col'=8] {'line_outer'}, dimensions={0} | all-to-all | bytes 1572864 | tf_op jit(solution)/shard_map/all_to_all | solution.py:57
  178.1 2.3 collective-permute-start.1
  180.4 1.9 collective-permute-done.1
  182.5 1.4 fusion.9
  183.9 25.8 %all_to_all.58 = f32[8,64,768]{2,1,0:T(8,128)} all-to-all(f32[8,64,768]{2,1,0:T(8,128)S(1)} %fusion.9), channel_id=1, replica_groups=mesh['line_outer'=8,'line_core'=2,'col'=8] {'col'}, dimensions={0} | all-to-all | bytes 3145728 | tf_op jit(solution)/shard_map/all_to_all | solution.py:16
  209.8 1.5 reduce_sum.66
  211.3 1.3 broadcast_in_dim.26
  212.6 4.4 all-to-all-start.5
  217.0 18.3 %all-to-all-done.5 = f32[8,64,768]{2,1,0:T(8,128)} async-done(((f32[8,64,768]{2,1,0:T(8,128)}), f32[8,64,768]{2,1,0:T(8,128)}, u32[]{:S(2)}, u32[]{:S(2)}) %all-to-all-start.5) | async-done | bytes 1572896 | tf_op jit(solution)/shard_map/all_to_all | solution.py:23
  235.4 2.8 multiply_subtract_fusion
  238.1 1.4 fusion.19
  239.7 3.5 collective-permute-start.2
  243.2 3.0 collective-permute-done.2
  246.2 0.4 bitcast_add_fusion.1
  246.6 23.5 %all_to_all.59 = f32[8,32,1536]{2,1,0:T(8,128)S(1)} all-to-all(f32[8,32,1536]{2,1,0:T(8,128)S(1)} %bitcast_add_fusion.1), channel_id=1, replica_groups=mesh['line_outer'=8,'line_core'=2,'col'=8] {'line_outer'}, dimensions={0} | all-to-all | bytes 3145728 | tf_op jit(solution)/shard_map/all_to_all | solution.py:49
  270.4 22.8 %all_to_all.60 = f32[8,32,1536]{2,1,0:T(8,128)S(1)} all-to-all(f32[8,32,1536]{2,1,0:T(8,128)S(1)} %broadcast_in_dim.27), channel_id=1, replica_groups=mesh['line_outer'=8,'line_core'=2,'col'=8] {'line_outer'}, dimensions={0} | all-to-all | bytes 3145728 | tf_op jit(solution)/shard_map/all_to_all | solution.py:57
  293.2 2.1 collective-permute-start.3
  295.3 3.0 collective-permute-done.3
  298.6 0.3 bitcast_multiply_fusion
  299.0 4.3 fusion.4
  303.3 25.3 %all_to_all.61 = f32[8,64,768]{2,1,0:T(8,128)S(1)} all-to-all(f32[8,64,768]{2,1,0:T(8,128)S(1)} %fusion.4), channel_id=1, replica_groups=mesh['line_outer'=8,'line_core'=2,'col'=8] {'col'}, dimensions={0} | all-to-all | bytes 3145728 | tf_op jit(solution)/shard_map/all_to_all | solution.py:16
  328.7 1.3 broadcast_in_dim.28
  330.0 4.4 all-to-all-start.9
  334.4 18.3 %all-to-all-done.9 = f32[8,64,768]{2,1,0:T(8,128)} async-done(((f32[8,64,768]{2,1,0:T(8,128)}), f32[8,64,768]{2,1,0:T(8,128)}, u32[]{:S(2)}, u32[]{:S(2)}) %all-to-all-start.9) | async-done | bytes 1572896 | tf_op jit(solution)/shard_map/all_to_all | solution.py:23
  352.8 4.0 fusion.13
  356.8 6.0 %fusion.25 = f32[512,4608]{1,0:T(8,128)S(1)} fusion(bf16[512,768]{1,0:T(8,128)(2,1)S(1)} %get-tuple-element.8, bf16[768,4608]{1,0:T(8,128)(2,1)} %param.14), kind=kOutput, calls=%fused_computation.50 | convolution fusion | flops 3623878656 | bytes 17301504 | tf_op jit(solution)/shard_map/dot_general | solution.py:129
  362.8 0.6 select_bitcast_fusion
  363.4 3.5 collective-permute-start.4
  366.9 7.5 %collective-permute-done.4 = f32[8,32,4608]{2,1,0:T(8,128)S(1)} collective-permute-done((f32[8,32,4608]{2,1,0:T(8,128)S(1)}, f32[8,32,4608]{2,1,0:T(8,128)S(1)}, u32[]{:S(2)}, u32[]{:S(2)}) %collective-permute-start.4) | collective-permute-done | bytes 4718624 | tf_op jit(solution)/shard_map/ppermute | solution.py:37
  374.4 3.3 fusion.1
  377.7 4.7 %all-to-all-start.10 = ((f32[8,32,4608]{2,1,0:T(8,128)}), f32[8,32,4608]{2,1,0:T(8,128)}, u32[]{:S(2)}, u32[]{:S(2)}) async-start(f32[8,32,4608]{2,1,0:T(8,128)} %fusion.1), calls=%async_computation.10 | async-start | bytes 9437184 | tf_op jit(solution)/shard_map/all_to_all | solution.py:49
  382.5 54.8 %all-to-all-done.10 = f32[8,32,4608]{2,1,0:T(8,128)} async-done(((f32[8,32,4608]{2,1,0:T(8,128)}), f32[8,32,4608]{2,1,0:T(8,128)}, u32[]{:S(2)}, u32[]{:S(2)}) %all-to-all-start.10) | async-done | bytes 4718624 | tf_op jit(solution)/shard_map/all_to_all | solution.py:49
  437.3 2.8 reduce_sum.69
  440.1 1.7 maximum_minimum_fusion
  (41 shorter events, 1.7 us)
Async XLA Ops:
  7.2 175.3 %copy-start = (bf16[768,1536]{1,0:T(8,128)(2,1)S(1)}, bf16[768,1536]{1,0:T(8,128)(2,1)}, u32[]{:S(2)}) copy-start(bf16[768,1536]{1,0:T(8,128)(2,1)} %param.15) | copy-start | bytes 7077892
  7.2 63.7 %all-gather.2.cloned.1.call-start = ((), (), s32[]{:S(2)}) async-start(), calls=%async_computation.11 | async-start | bytes 10027008 | tf_op jit(solution)/shard_map/all_gather | solution.py:96
  113.7 4.4 copy-start.8
  113.7 22.9 %copy-start.7 = (f32[1536]{0:T(1024)S(1)}, f32[1536]{0:T(1024)}, u32[]{:S(2)}) copy-start(f32[1536]{0:T(1024)} %param.27) | copy-start | bytes 18436
  113.7 22.9 %all-to-all-start.1 = ((f32[8,64,768]{2,1,0:T(8,128)}), f32[8,64,768]{2,1,0:T(8,128)}, u32[]{:S(2)}, u32[]{:S(2)}) async-start(f32[8,64,768]{2,1,0:T(8,128)} %broadcast_in_dim.22), calls=%async_computation.1 | async-start | bytes 3145728 | tf_op jit(solution)/shard_map/all_to_all | solution.py:23
  142.2 5.2 %collective-permute-start = (bf16[8,32,1536]{2,1,0:T(8,128)(2,1)S(1)}, bf16[8,32,1536]{2,1,0:T(8,128)(2,1)S(1)}, u32[]{:S(2)}, u32[]{:S(2)}) collective-permute-start(bf16[8,32,1536]{2,1,0:T(8,128)(2,1)S(1)} %fusion.16), channel_id=1, source_target_pairs={{0,8},{8,0},{1,9},{9,1},{2,10},{10,2},{3,11},{11,3},{4,12},{12,4},... | collective-permute-start | bytes 2359304 | tf_op jit(solution)/shard_map/ppermute | solution.py:37
  178.1 4.2 collective-permute-start.1
  212.6 4.4 copy-start.6
  212.6 22.8 %all-to-all-start.5 = ((f32[8,64,768]{2,1,0:T(8,128)}), f32[8,64,768]{2,1,0:T(8,128)}, u32[]{:S(2)}, u32[]{:S(2)}) async-start(f32[8,64,768]{2,1,0:T(8,128)} %broadcast_in_dim.26), calls=%async_computation.5 | async-start | bytes 3145728 | tf_op jit(solution)/shard_map/all_to_all | solution.py:23
  238.1 1.4 copy-start.2
  239.7 6.5 %collective-permute-start.2 = (f32[8,32,1536]{2,1,0:T(8,128)S(1)}, f32[8,32,1536]{2,1,0:T(8,128)S(1)}, u32[]{:S(2)}, u32[]{:S(2)}) collective-permute-start(f32[8,32,1536]{2,1,0:T(8,128)S(1)} %select_bitcast_fusion.1), channel_id=1, source_target_pairs={{0,8},{8,0},{1,9},{9,1},{2,10},{10,2},{3,11},{11,3},{4,12},{12,4},... | collective-permute-start | bytes 4718600 | tf_op jit(solution)/shard_map/ppermute | solution.py:37
  293.2 5.1 %collective-permute-start.3 = (f32[8,32,1536]{2,1,0:T(8,128)S(1)}, f32[8,32,1536]{2,1,0:T(8,128)S(1)}, u32[]{:S(2)}, u32[]{:S(2)}) collective-permute-start(f32[8,32,1536]{2,1,0:T(8,128)S(1)} %all_to_all.60), channel_id=1, source_target_pairs={{0,8},{8,0},{1,9},{9,1},{2,10},{10,2},{3,11},{11,3},{4,12},{12,4},... | collective-permute-start | bytes 4718600 | tf_op jit(solution)/shard_map/ppermute | solution.py:37
  330.0 4.5 copy-start.5
  330.0 22.8 %copy-start.3 = (f32[512,768]{1,0:T(8,128)S(1)}, f32[512,768]{1,0:T(8,128)}, u32[]{:S(2)}) copy-start(f32[512,768]{1,0:T(8,128)} %copy-done.2) | copy-start | bytes 4718596
  330.0 22.8 %all-to-all-start.9 = ((f32[8,64,768]{2,1,0:T(8,128)}), f32[8,64,768]{2,1,0:T(8,128)}, u32[]{:S(2)}, u32[]{:S(2)}) async-start(f32[8,64,768]{2,1,0:T(8,128)} %broadcast_in_dim.28), calls=%async_computation.9 | async-start | bytes 3145728 | tf_op jit(solution)/shard_map/all_to_all | solution.py:23
  363.4 11.0 %collective-permute-start.4 = (f32[8,32,4608]{2,1,0:T(8,128)S(1)}, f32[8,32,4608]{2,1,0:T(8,128)S(1)}, u32[]{:S(2)}, u32[]{:S(2)}) collective-permute-start(f32[8,32,4608]{2,1,0:T(8,128)S(1)} %select_bitcast_fusion), channel_id=1, source_target_pairs={{0,8},{8,0},{1,9},{9,1},{2,10},{10,2},{3,11},{11,3},{4,12},{12,4},... | collective-permute-start | bytes 14155784 | tf_op jit(solution)/shard_map/ppermute | solution.py:37
  377.7 4.7 %copy-start.10 = (f32[32]{0:T(128)S(1)}, f32[32]{0:T(128)}, u32[]{:S(2)}) copy-start(f32[32]{0:T(128)} %param.21) | copy-start | bytes 388
  377.7 4.7 %copy-start.11 = (f32[32]{0:T(128)S(1)}, f32[32]{0:T(128)}, u32[]{:S(2)}) copy-start(f32[32]{0:T(128)} %param.20) | copy-start | bytes 388
  377.7 59.5 %all-to-all-start.10 = ((f32[8,32,4608]{2,1,0:T(8,128)}), f32[8,32,4608]{2,1,0:T(8,128)}, u32[]{:S(2)}, u32[]{:S(2)}) async-start(f32[8,32,4608]{2,1,0:T(8,128)} %fusion.1), calls=%async_computation.10 | async-start | bytes 9437184 | tf_op jit(solution)/shard_map/all_to_all | solution.py:49
  382.5 57.6 %copy-start.9 = (f32[32]{0:T(128)}, f32[32]{0:T(128)S(1)}, u32[]{:S(2)}) copy-start(f32[32]{0:T(128)S(1)} %multiply_add_fusion) | copy-start | bytes 388
  382.5 57.6 %copy-start.4 = (f32[32,4608]{1,0:T(8,128)S(1)}, f32[32,4608]{1,0:T(8,128)}, u32[]{:S(2)}) copy-start(f32[32,4608]{1,0:T(8,128)} %param.16) | copy-start | bytes 1769476
  437.3 4.5 %copy-start.1 = (bf16[768,1536]{1,0:T(8,128)(2,1)S(1)}, bf16[768,1536]{1,0:T(8,128)(2,1)}, u32[]{:S(2)}) copy-start(bf16[768,1536]{1,0:T(8,128)(2,1)} %param.15) | copy-start | bytes 7077892
Sparse Core Ops, SparseCore 0:
  10.2 60.6 all-gather.1

commit v9 on v8

--- a/solution.py
+++ b/solution.py
@@ -93,12 +93,22 @@
     ptdf_turned = ptdf.T
     local_total = jnp.sum(extra_high.astype(jnp.float32) + extra_low.astype(jnp.float32), axis=1)
     bus_total = lax.psum(local_total, "col")
-    portion = lax.all_gather(stacked, LINE, axis=1, tiled=True)
-    portion, bus_total = lax.optimization_barrier((portion, bus_total))
-    count = portion.shape[1]
-    flat = portion.reshape(2 * count, portion.shape[2])
-    product = jnp.dot(flat, ptdf_turned, preferred_element_type=jnp.float32)
-    flow_part = product[:count] + product[count:]
+    mine = lax.all_gather(stacked, LINE_OUTER, axis=1, tiled=True)
+    mine, bus_total = lax.optimization_barrier((mine, bus_total))
+    other = swap_cores(mine)
+    outer = lax.axis_size(LINE_OUTER)
+    rows = injection.shape[0]
+
+    def flows(portion):
+        count = portion.shape[1]
+        product = jnp.dot(portion.reshape(2 * count, portion.shape[2]), ptdf_turned, preferred_element_type=jnp.float32)
+        return (product[:count] + product[count:]).reshape(outer, rows, lines_dev)
+
+    mine_flow, other_flow = flows(mine), flows(other)
+    core = lax.axis_index(LINE_CORE)
+    flow_part = jnp.where(
+        core == 0, jnp.stack([mine_flow, other_flow], axis=1), jnp.stack([other_flow, mine_flow], axis=1)
+    ).reshape(2 * outer * rows, lines_dev)
     base_flow = full_sum(flow_part, "col")
     balance_new = balance_dual + (bus_total - demand) / BUSES
     base_new = dual_update(base_dual, base_flow, flow_limit[None, :])

time: 450 us -> 496 us (1.10)
  waiting for transfers between devices: 167 us -> 209 us
    all_gather x1, waiting for transfers between devices: 39.2 us -> 82 us  [on_device(): mine = lax.all_gather(stacked, LINE_OUTER, axis=1, tiled=True)]
    dot_general x1 -> x2, matrix products: 12.1 us -> 15.6 us  [flows(): jnp.dot(portion.reshape(2 * count, portion.shape[2]), ptdf_turned, prefer...]
    ppermute x5 -> x6, starting transfers between devices: 14.6 us -> 16.2 us  [swap_cores(): return lax.ppermute(value, LINE_CORE, [(0, 1), (1, 0)])]
    ppermute x5 -> x6, waiting for transfers between devices: 17.4 us -> 17.4 us  [swap_cores(): return lax.ppermute(value, LINE_CORE, [(0, 1), (1, 0)])]
  transfers between devices with their start and end apart: 10 -> 11, of which waited for: 10 -> 10; matrix products, arithmetic and copies ran while one was open for 0% -> 2% of each run, Pallas kernels for 0% -> 0%
where the time goes in v9:
time: 496 us
  waiting for transfers between devices  209 us (42%)
  blocking collectives  176 us (35%)
  starting transfers between devices  34.3 us (7%)
  matrix products  34.2 us (7%)
  other arithmetic  22.9 us (5%)
  between operations  14.4 us (3%)
    all_gather x1, waiting for transfers between devices, on_device(): mine = lax.all_gather(stacked, LINE_OUTER, axis=1, tiled=True)  82 us
    all_to_all x3, blocking collectives, summed_block(): lax.all_to_all(value.reshape(n, rows, *value.shape[1:]), axis, 0, 0, tile...  78.6 us
    all_to_all x3, waiting for transfers between devices, gathered_rows(): whole = lax.all_to_all(copies, axis, 0, 0, tiled=True)  55 us
    all_to_all x1, waiting for transfers between devices, line_summed_block(): parts = lax.all_to_all(pair_sum, LINE_OUTER, 0, 0, tiled=True)  54.8 us
    all_to_all x2, blocking collectives, line_summed_block(): parts = lax.all_to_all(pair_sum, LINE_OUTER, 0, 0, tiled=True)  39.1 us
    all_to_all x2, blocking collectives, line_gathered_rows(): mine = lax.all_to_all(copies, LINE_OUTER, 0, 0, tiled=True)  36.9 us
    psum x1, blocking collectives, on_device(): bus_total = lax.psum(local_total, 'col')  21.9 us
    ppermute x6, waiting for transfers between devices, swap_cores(): return lax.ppermute(value, LINE_CORE, [(0, 1), (1, 0)])  17.4 us
  transfers between devices with their start and end apart: 11, of which 10 were waited for; matrix products, arithmetic and copies ran while one was open for 2% of the time, Pallas kernels for 0%

profile of v9, /device:TPU:1, one launch (start us, length us, event | category | flops | bytes accessed | tf_op | source)
XLA Modules:
  0.0 495.5 jit_solution(9141713949026965982)
XLA Ops:
  7.2 1.6 fusion.22
  8.8 0.9 pad_maximum_fusion
  9.7 21.9 %psum.7 = f32[32]{0:T(128)S(1)} all-reduce(f32[32]{0:T(128)S(1)} %get-tuple-element.12), channel_id=1, replica_groups=mesh['line_outer'=8,'line_core'=2,'col'=8] {'col'}, use_global_device_ids=true, to_apply=%region_1.0 | all-reduce | flops 32 | bytes 256 | tf_op jit(solution)/shard_map/psum | solution.py:95
  31.7 82.0 %all-gather.2.cloned.1.call-done = bf16[2,256,4608]{2,1,0:T(8,128)(2,1)} async-done(((bf16[2,32,4608]{2,1,0:T(8,128)(2,1)}), bf16[2,256,4608]{2,1,0:T(8,128)(2,1)}) %all-gather.2.cloned.1.call-update) | async-done | bytes 4718608 | tf_op jit(solution)/shard_map/all_gather | solution.py:96
  113.7 1.2 collective-permute-start
  114.8 7.8 %fusion.24 = f32[512,768]{1,0:T(8,128)S(1)} fusion(bf16[512,4608]{1,0:T(8,128)(2,1)} %bitcast.125, bf16[768,4608]{1,0:T(8,128)(2,1)} %param.14), kind=kOutput, calls=%fused_computation.51 | convolution fusion | flops 3623878656 | bytes 13369344 | tf_op jit(solution)/shard_map/dot_general | solution.py:104
  122.8 7.8 %fusion.25 = f32[512,768]{1,0:T(8,128)S(1)} fusion(bf16[512,4608]{1,0:T(8,128)(2,1)} %bitcast.5, bf16[768,4608]{1,0:T(8,128)(2,1)} %param.14), kind=kOutput, calls=%fused_computation.52 | convolution fusion | flops 3623878656 | bytes 13369344 | tf_op jit(solution)/shard_map/dot_general | solution.py:104
  130.8 27.3 %all_to_all.55 = f32[8,64,768]{2,1,0:T(8,128)} all-to-all(f32[8,64,768]{2,1,0:T(8,128)S(1)} %bitcast.118), channel_id=1, replica_groups=mesh['line_outer'=8,'line_core'=2,'col'=8] {'col'}, dimensions={0} | all-to-all | bytes 3145728 | tf_op jit(solution)/shard_map/all_to_all | solution.py:16
  158.0 1.5 reduce_sum.64
  159.5 1.3 broadcast_in_dim.22
  160.8 4.4 all-to-all-start.1
  165.3 18.4 %all-to-all-done.1 = f32[8,64,768]{2,1,0:T(8,128)} async-done(((f32[8,64,768]{2,1,0:T(8,128)}), f32[8,64,768]{2,1,0:T(8,128)}, u32[]{:S(2)}, u32[]{:S(2)}) %all-to-all-start.1) | async-done | bytes 1572896 | tf_op jit(solution)/shard_map/all_to_all | solution.py:23
  183.6 5.4 %fusion.8 = bf16[512,1536]{1,0:T(8,128)(2,1)S(1)} fusion(f32[512,768]{1,0:T(8,128)} %bitcast.11, s32[1536]{0:T(1024)S(1)} %get-tuple-element.11, f32[1536]{0:T(1024)S(1)} %copy-done.7, pred[1536]{0:T(1024)(128)(4,1)S(1)} %get-tuple-element.10), kind=kOutput, calls=%fused_computation.12 | convolution fusion | flops 7251296256 | bytes 3159552 | tf_op jit(solution)/shard_map/dot_general | solution.py:121
  189.2 3.4 collective-permute-start.1
  192.6 1.9 collective-permute-done.1
  194.6 15.6 %all_to_all.56 = bf16[8,32,1536]{2,1,0:T(8,128)(2,1)S(1)} all-to-all(bf16[8,32,1536]{2,1,0:T(8,128)(2,1)S(1)} %fusion.18), channel_id=1, replica_groups=mesh['line_outer'=8,'line_core'=2,'col'=8] {'line_outer'}, dimensions={0} | all-to-all | bytes 1572864 | tf_op jit(solution)/shard_map/all_to_all | solution.py:49
  210.4 14.4 %all_to_all.57 = bf16[8,32,1536]{2,1,0:T(8,128)(2,1)S(1)} all-to-all(bf16[8,32,1536]{2,1,0:T(8,128)(2,1)S(1)} %broadcast_in_dim.25), channel_id=1, replica_groups=mesh['line_outer'=8,'line_core'=2,'col'=8] {'line_outer'}, dimensions={0} | all-to-all | bytes 1572864 | tf_op jit(solution)/shard_map/all_to_all | solution.py:57
  224.8 2.3 collective-permute-start.2
  227.1 1.9 collective-permute-done.2
  229.2 1.4 fusion.9
  230.6 25.8 %all_to_all.58 = f32[8,64,768]{2,1,0:T(8,128)} all-to-all(f32[8,64,768]{2,1,0:T(8,128)S(1)} %fusion.9), channel_id=1, replica_groups=mesh['line_outer'=8,'line_core'=2,'col'=8] {'col'}, dimensions={0} | all-to-all | bytes 3145728 | tf_op jit(solution)/shard_map/all_to_all | solution.py:16
  256.5 1.5 reduce_sum.66
  258.0 1.3 broadcast_in_dim.26
  259.2 4.4 all-to-all-start.5
  263.7 18.3 %all-to-all-done.5 = f32[8,64,768]{2,1,0:T(8,128)} async-done(((f32[8,64,768]{2,1,0:T(8,128)}), f32[8,64,768]{2,1,0:T(8,128)}, u32[]{:S(2)}, u32[]{:S(2)}) %all-to-all-start.5) | async-done | bytes 1572896 | tf_op jit(solution)/shard_map/all_to_all | solution.py:23
  282.0 2.8 multiply_subtract_fusion
  284.8 1.4 fusion.19
  286.4 3.6 collective-permute-start.3
  290.1 3.0 collective-permute-done.3
  293.5 23.5 %all_to_all.59 = f32[8,32,1536]{2,1,0:T(8,128)S(1)} all-to-all(f32[8,32,1536]{2,1,0:T(8,128)S(1)} %bitcast_add_fusion.1), channel_id=1, replica_groups=mesh['line_outer'=8,'line_core'=2,'col'=8] {'line_outer'}, dimensions={0} | all-to-all | bytes 3145728 | tf_op jit(solution)/shard_map/all_to_all | solution.py:49
  317.2 22.5 %all_to_all.60 = f32[8,32,1536]{2,1,0:T(8,128)S(1)} all-to-all(f32[8,32,1536]{2,1,0:T(8,128)S(1)} %broadcast_in_dim.27), channel_id=1, replica_groups=mesh['line_outer'=8,'line_core'=2,'col'=8] {'line_outer'}, dimensions={0} | all-to-all | bytes 3145728 | tf_op jit(solution)/shard_map/all_to_all | solution.py:57
  339.7 2.2 collective-permute-start.4
  342.0 3.0 collective-permute-done.4
  345.7 4.3 fusion.4
  350.0 25.5 %all_to_all.61 = f32[8,64,768]{2,1,0:T(8,128)S(1)} all-to-all(f32[8,64,768]{2,1,0:T(8,128)S(1)} %fusion.4), channel_id=1, replica_groups=mesh['line_outer'=8,'line_core'=2,'col'=8] {'col'}, dimensions={0} | all-to-all | bytes 3145728 | tf_op jit(solution)/shard_map/all_to_all | solution.py:16
  375.6 1.3 broadcast_in_dim.28
  376.8 4.4 all-to-all-start.9
  381.3 18.3 %all-to-all-done.9 = f32[8,64,768]{2,1,0:T(8,128)} async-done(((f32[8,64,768]{2,1,0:T(8,128)}), f32[8,64,768]{2,1,0:T(8,128)}, u32[]{:S(2)}, u32[]{:S(2)}) %all-to-all-start.9) | async-done | bytes 1572896 | tf_op jit(solution)/shard_map/all_to_all | solution.py:23
  399.6 4.0 fusion.13
  403.6 6.0 %fusion.26 = f32[512,4608]{1,0:T(8,128)S(1)} fusion(bf16[512,768]{1,0:T(8,128)(2,1)S(1)} %get-tuple-element.8, bf16[768,4608]{1,0:T(8,128)(2,1)} %param.14), kind=kOutput, calls=%fused_computation.53 | convolution fusion | flops 3623878656 | bytes 17301504 | tf_op jit(solution)/shard_map/dot_general | solution.py:139
  409.7 0.6 select_bitcast_fusion
  410.3 3.5 collective-permute-start.5
  413.7 7.5 %collective-permute-done.5 = f32[8,32,4608]{2,1,0:T(8,128)S(1)} collective-permute-done((f32[8,32,4608]{2,1,0:T(8,128)S(1)}, f32[8,32,4608]{2,1,0:T(8,128)S(1)}, u32[]{:S(2)}, u32[]{:S(2)}) %collective-permute-start.5) | collective-permute-done | bytes 4718624 | tf_op jit(solution)/shard_map/ppermute | solution.py:37
  421.3 3.3 fusion.1
  424.6 4.7 all-to-all-start.10
  429.4 54.8 %all-to-all-done.10 = f32[8,32,4608]{2,1,0:T(8,128)} async-done(((f32[8,32,4608]{2,1,0:T(8,128)}), f32[8,32,4608]{2,1,0:T(8,128)}, u32[]{:S(2)}, u32[]{:S(2)}) %all-to-all-start.10) | async-done | bytes 4718624 | tf_op jit(solution)/shard_map/all_to_all | solution.py:49
  484.1 2.8 reduce_sum.69
  487.0 1.7 maximum_minimum_fusion
  (46 shorter events, 2.5 us)
Async XLA Ops:
  7.2 222.0 %copy-start = (bf16[768,1536]{1,0:T(8,128)(2,1)S(1)}, bf16[768,1536]{1,0:T(8,128)(2,1)}, u32[]{:S(2)}) copy-start(bf16[768,1536]{1,0:T(8,128)(2,1)} %param.15) | copy-start | bytes 7077892
  7.2 106.5 %all-gather.2.cloned.1.call-start = ((), (), s32[]{:S(2)}) async-start(), calls=%async_computation.11 | async-start | bytes 5308416 | tf_op jit(solution)/shard_map/all_gather | solution.py:96
  113.7 9.1 %collective-permute-start = (bf16[2,256,4608]{2,1,0:T(8,128)(2,1)}, bf16[2,256,4608]{2,1,0:T(8,128)(2,1)}, u32[]{:S(2)}, u32[]{:S(2)}) collective-permute-start(bf16[2,256,4608]{2,1,0:T(8,128)(2,1)} %all-gather.2.cloned.1.call-done), channel_id=1, source_target_pairs={{0,8},{8,0},{1,9},{9,1},{2,10},{10,2},{3,11},{11,3},{4,12},{12,4},... | collective-permute-start | bytes 14155784 | tf_op jit(solution)/shard_map/ppermute | solution.py:37
  160.8 4.4 copy-start.8
  160.8 22.8 %copy-start.7 = (f32[1536]{0:T(1024)S(1)}, f32[1536]{0:T(1024)}, u32[]{:S(2)}) copy-start(f32[1536]{0:T(1024)} %param.27) | copy-start | bytes 18436
  160.8 22.8 %all-to-all-start.1 = ((f32[8,64,768]{2,1,0:T(8,128)}), f32[8,64,768]{2,1,0:T(8,128)}, u32[]{:S(2)}, u32[]{:S(2)}) async-start(f32[8,64,768]{2,1,0:T(8,128)} %broadcast_in_dim.22), calls=%async_computation.1 | async-start | bytes 3145728 | tf_op jit(solution)/shard_map/all_to_all | solution.py:23
  189.2 5.3 %collective-permute-start.1 = (bf16[8,32,1536]{2,1,0:T(8,128)(2,1)S(1)}, bf16[8,32,1536]{2,1,0:T(8,128)(2,1)S(1)}, u32[]{:S(2)}, u32[]{:S(2)}) collective-permute-start(bf16[8,32,1536]{2,1,0:T(8,128)(2,1)S(1)} %fusion.16), channel_id=1, source_target_pairs={{0,8},{8,0},{1,9},{9,1},{2,10},{10,2},{3,11},{11,3},{4,12},{12,4},... | collective-permute-start | bytes 2359304 | tf_op jit(solution)/shard_map/ppermute | solution.py:37
  224.8 4.2 collective-permute-start.2
  259.2 4.4 copy-start.6
  259.2 22.8 %all-to-all-start.5 = ((f32[8,64,768]{2,1,0:T(8,128)}), f32[8,64,768]{2,1,0:T(8,128)}, u32[]{:S(2)}, u32[]{:S(2)}) async-start(f32[8,64,768]{2,1,0:T(8,128)} %broadcast_in_dim.26), calls=%async_computation.5 | async-start | bytes 3145728 | tf_op jit(solution)/shard_map/all_to_all | solution.py:23
  284.8 1.4 copy-start.2
  286.4 6.7 %collective-permute-start.3 = (f32[8,32,1536]{2,1,0:T(8,128)S(1)}, f32[8,32,1536]{2,1,0:T(8,128)S(1)}, u32[]{:S(2)}, u32[]{:S(2)}) collective-permute-start(f32[8,32,1536]{2,1,0:T(8,128)S(1)} %select_bitcast_fusion.1), channel_id=1, source_target_pairs={{0,8},{8,0},{1,9},{9,1},{2,10},{10,2},{3,11},{11,3},{4,12},{12,4},... | collective-permute-start | bytes 4718600 | tf_op jit(solution)/shard_map/ppermute | solution.py:37
  339.7 5.3 %collective-permute-start.4 = (f32[8,32,1536]{2,1,0:T(8,128)S(1)}, f32[8,32,1536]{2,1,0:T(8,128)S(1)}, u32[]{:S(2)}, u32[]{:S(2)}) collective-permute-start(f32[8,32,1536]{2,1,0:T(8,128)S(1)} %all_to_all.60), channel_id=1, source_target_pairs={{0,8},{8,0},{1,9},{9,1},{2,10},{10,2},{3,11},{11,3},{4,12},{12,4},... | collective-permute-start | bytes 4718600 | tf_op jit(solution)/shard_map/ppermute | solution.py:37
  376.8 4.4 copy-start.5
  376.8 22.8 %copy-start.3 = (f32[512,768]{1,0:T(8,128)S(1)}, f32[512,768]{1,0:T(8,128)}, u32[]{:S(2)}) copy-start(f32[512,768]{1,0:T(8,128)} %copy-done.2) | copy-start | bytes 4718596
  376.8 22.8 %all-to-all-start.9 = ((f32[8,64,768]{2,1,0:T(8,128)}), f32[8,64,768]{2,1,0:T(8,128)}, u32[]{:S(2)}, u32[]{:S(2)}) async-start(f32[8,64,768]{2,1,0:T(8,128)} %broadcast_in_dim.28), calls=%async_computation.9 | async-start | bytes 3145728 | tf_op jit(solution)/shard_map/all_to_all | solution.py:23
  410.3 11.0 %collective-permute-start.5 = (f32[8,32,4608]{2,1,0:T(8,128)S(1)}, f32[8,32,4608]{2,1,0:T(8,128)S(1)}, u32[]{:S(2)}, u32[]{:S(2)}) collective-permute-start(f32[8,32,4608]{2,1,0:T(8,128)S(1)} %select_bitcast_fusion), channel_id=1, source_target_pairs={{0,8},{8,0},{1,9},{9,1},{2,10},{10,2},{3,11},{11,3},{4,12},{12,4},... | collective-permute-start | bytes 14155784 | tf_op jit(solution)/shard_map/ppermute | solution.py:37
  424.6 4.7 copy-start.10
  424.6 4.8 copy-start.11
  424.6 59.5 %all-to-all-start.10 = ((f32[8,32,4608]{2,1,0:T(8,128)}), f32[8,32,4608]{2,1,0:T(8,128)}, u32[]{:S(2)}, u32[]{:S(2)}) async-start(f32[8,32,4608]{2,1,0:T(8,128)} %fusion.1), calls=%async_computation.10 | async-start | bytes 9437184 | tf_op jit(solution)/shard_map/all_to_all | solution.py:49
  429.4 57.6 %copy-start.9 = (f32[32]{0:T(128)}, f32[32]{0:T(128)S(1)}, u32[]{:S(2)}) copy-start(f32[32]{0:T(128)S(1)} %multiply_add_fusion) | copy-start | bytes 388
  429.4 57.6 %copy-start.4 = (f32[32,4608]{1,0:T(8,128)S(1)}, f32[32,4608]{1,0:T(8,128)}, u32[]{:S(2)}) copy-start(f32[32,4608]{1,0:T(8,128)} %param.16) | copy-start | bytes 1769476
  484.1 4.5 copy-start.1
Sparse Core Ops, SparseCore 0:
  10.2 103.4 all-gather.1

commit v10 on v8

--- a/solution.py
+++ b/solution.py
@@ -124,8 +124,12 @@
         precision=exact,
         preferred_element_type=jnp.float32,
     )
-    returned = full_sum(returned_part, "col")
-    line_total = (base_new + post_new + returned).astype(jnp.bfloat16)
+    returned = summed_block(returned_part, "col")
+    block_rows = returned.shape[0]
+    first_row = lax.axis_index("col") * block_rows
+    base_block = lax.dynamic_slice_in_dim(base_new, first_row, block_rows, axis=0)
+    post_block = lax.dynamic_slice_in_dim(post_new, first_row, block_rows, axis=0)
+    line_total = gathered_rows((base_block + post_block + returned).astype(jnp.bfloat16), "col")
     prices = line_summed_block(jnp.dot(line_total, ptdf, preferred_element_type=jnp.float32))
     moved = injection - primal_step * (bus_cost[None, :] + prices + balance_new[:, None])
     new_injection = jnp.clip(moved, 0.0, bus_cap[None, :])

time: 450 us -> 442 us (0.982)
  blocking collectives: 177 us -> 170 us
    all_to_all x3 -> x2, blocking collectives: 78.8 us -> 53.5 us  [summed_block(): lax.all_to_all(value.reshape(n, rows, *value.shape[1:]), axis, 0, 0, tile...]
    all_to_all x0 -> x1, waiting for transfers between devices: none -> 20.6 us  [summed_block(): lax.all_to_all(value.reshape(n, rows, *value.shape[1:]), axis, 0, 0, tile...]
    all_to_all x3 -> x2, waiting for transfers between devices: 55.1 us -> 36.8 us  [gathered_rows(): whole = lax.all_to_all(copies, axis, 0, 0, tiled=True)]
    all_to_all x0 -> x1, blocking collectives: none -> 17.8 us  [gathered_rows(): whole = lax.all_to_all(copies, axis, 0, 0, tiled=True)]
    all_to_all x3 -> x2, starting transfers between devices: 13.3 us -> 8.85 us  [gathered_rows(): whole = lax.all_to_all(copies, axis, 0, 0, tiled=True)]
where the time goes in v10:
time: 442 us; the launch traced here: 441 us
  blocking collectives  170 us (38%)
  waiting for transfers between devices  169 us (38%)
  starting transfers between devices  31.9 us (7%)
  matrix products  31.9 us (7%)
  other arithmetic  21.8 us (5%)
  between operations  14.3 us (3%)
    all_to_all x1, waiting for transfers between devices, line_summed_block(): parts = lax.all_to_all(pair_sum, LINE_OUTER, 0, 0, tiled=True)  54.8 us
    all_to_all x2, blocking collectives, summed_block(): lax.all_to_all(value.reshape(n, rows, *value.shape[1:]), axis, 0, 0, tile...  53.5 us
    all_to_all x2, blocking collectives, line_summed_block(): parts = lax.all_to_all(pair_sum, LINE_OUTER, 0, 0, tiled=True)  39.6 us
    all_gather x1, waiting for transfers between devices, on_device(): portion = lax.all_gather(stacked, LINE, axis=1, tiled=True)  39.2 us
    all_to_all x2, blocking collectives, line_gathered_rows(): mine = lax.all_to_all(copies, LINE_OUTER, 0, 0, tiled=True)  36.9 us
    all_to_all x2, waiting for transfers between devices, gathered_rows(): whole = lax.all_to_all(copies, axis, 0, 0, tiled=True)  36.8 us
    psum x1, blocking collectives, on_device(): bus_total = lax.psum(local_total, 'col')  21.9 us
    all_to_all x1, waiting for transfers between devices, summed_block(): lax.all_to_all(value.reshape(n, rows, *value.shape[1:]), axis, 0, 0, tile...  20.6 us
  transfers between devices with their start and end apart: 10, of which 10 were waited for; matrix products, arithmetic and copies ran while one was open for 0% of the time, Pallas kernels for 0%

profile of v10, /device:TPU:1, one launch (start us, length us, event | category | flops | bytes accessed | tf_op | source)
XLA Modules:
  0.0 441.4 jit_solution(6882399962998105725)
XLA Ops:
  7.2 1.6 fusion.23
  8.8 0.9 pad_maximum_fusion
  9.7 21.9 %psum.7 = f32[32]{0:T(128)S(1)} all-reduce(f32[32]{0:T(128)S(1)} %get-tuple-element.12), channel_id=1, replica_groups=mesh['line_outer'=8,'line_core'=2,'col'=8] {'col'}, use_global_device_ids=true, to_apply=%region_1.0 | all-reduce | flops 32 | bytes 256 | tf_op jit(solution)/shard_map/psum | solution.py:95
  31.7 39.2 %all-gather.2.cloned.1.call-done = bf16[2,512,4608]{2,1,0:T(8,128)(2,1)} async-done(((bf16[2,32,4608]{2,1,0:T(8,128)(2,1)}), bf16[2,512,4608]{2,1,0:T(8,128)(2,1)}) %all-gather.2.cloned.1.call-update) | async-done | bytes 9437200 | tf_op jit(solution)/shard_map/all_gather | solution.py:96
  70.9 12.1 %fusion.25 = f32[1024,768]{1,0:T(8,128)S(1)} fusion(bf16[1024,4608]{1,0:T(8,128)(2,1)} %bitcast.110, bf16[768,4608]{1,0:T(8,128)(2,1)} %param.14), kind=kOutput, calls=%fused_computation.50 | convolution fusion | flops 7247757312 | bytes 19660800 | tf_op jit(solution)/shard_map/dot_general | solution.py:100
  83.2 27.7 %all_to_all.55 = f32[8,64,768]{2,1,0:T(8,128)} all-to-all(f32[8,64,768]{2,1,0:T(8,128)S(1)} %bitcast.104), channel_id=1, replica_groups=mesh['line_outer'=8,'line_core'=2,'col'=8] {'col'}, dimensions={0} | all-to-all | bytes 3145728 | tf_op jit(solution)/shard_map/all_to_all | solution.py:16
  110.9 1.5 reduce_sum.64
  112.4 1.3 broadcast_in_dim.22
  113.7 4.4 %all-to-all-start.1 = ((f32[8,64,768]{2,1,0:T(8,128)}), f32[8,64,768]{2,1,0:T(8,128)}, u32[]{:S(2)}, u32[]{:S(2)}) async-start(f32[8,64,768]{2,1,0:T(8,128)} %broadcast_in_dim.22), calls=%async_computation.1 | async-start | bytes 3145728 | tf_op jit(solution)/shard_map/all_to_all | solution.py:23
  118.2 18.5 %all-to-all-done.1 = f32[8,64,768]{2,1,0:T(8,128)} async-done(((f32[8,64,768]{2,1,0:T(8,128)}), f32[8,64,768]{2,1,0:T(8,128)}, u32[]{:S(2)}, u32[]{:S(2)}) %all-to-all-start.1) | async-done | bytes 1572896 | tf_op jit(solution)/shard_map/all_to_all | solution.py:23
  136.7 5.4 %fusion.10 = bf16[512,1536]{1,0:T(8,128)(2,1)S(1)} fusion(f32[512,768]{1,0:T(8,128)} %bitcast.4, s32[1536]{0:T(1024)S(1)} %get-tuple-element.9, f32[1536]{0:T(1024)S(1)} %copy-done.6, pred[1536]{0:T(1024)(128)(4,1)S(1)} %get-tuple-element.8), kind=kOutput, calls=%fused_computation.14 | convolution fusion | flops 7251296256 | bytes 3159552 | tf_op jit(solution)/shard_map/dot_general | solution.py:111
  142.2 3.3 collective-permute-start
  145.5 1.9 collective-permute-done
  147.5 16.0 %all_to_all.56 = bf16[8,32,1536]{2,1,0:T(8,128)(2,1)S(1)} all-to-all(bf16[8,32,1536]{2,1,0:T(8,128)(2,1)S(1)} %fusion.19), channel_id=1, replica_groups=mesh['line_outer'=8,'line_core'=2,'col'=8] {'line_outer'}, dimensions={0} | all-to-all | bytes 1572864 | tf_op jit(solution)/shard_map/all_to_all | solution.py:49
  163.7 14.4 %all_to_all.57 = bf16[8,32,1536]{2,1,0:T(8,128)(2,1)S(1)} all-to-all(bf16[8,32,1536]{2,1,0:T(8,128)(2,1)S(1)} %broadcast_in_dim.25), channel_id=1, replica_groups=mesh['line_outer'=8,'line_core'=2,'col'=8] {'line_outer'}, dimensions={0} | all-to-all | bytes 1572864 | tf_op jit(solution)/shard_map/all_to_all | solution.py:57
  178.1 2.3 collective-permute-start.1
  180.4 1.9 collective-permute-done.1
  182.5 1.4 fusion.11
  183.9 25.8 %all_to_all.58 = f32[8,64,768]{2,1,0:T(8,128)} all-to-all(f32[8,64,768]{2,1,0:T(8,128)S(1)} %fusion.11), channel_id=1, replica_groups=mesh['line_outer'=8,'line_core'=2,'col'=8] {'col'}, dimensions={0} | all-to-all | bytes 3145728 | tf_op jit(solution)/shard_map/all_to_all | solution.py:16
  209.8 1.5 reduce_sum.66
  211.3 1.3 broadcast_in_dim.26
  212.6 4.4 %all-to-all-start.5 = ((f32[8,64,768]{2,1,0:T(8,128)}), f32[8,64,768]{2,1,0:T(8,128)}, u32[]{:S(2)}, u32[]{:S(2)}) async-start(f32[8,64,768]{2,1,0:T(8,128)} %broadcast_in_dim.26), calls=%async_computation.5 | async-start | bytes 3145728 | tf_op jit(solution)/shard_map/all_to_all | solution.py:23
  217.0 18.3 %all-to-all-done.5 = f32[8,64,768]{2,1,0:T(8,128)} async-done(((f32[8,64,768]{2,1,0:T(8,128)}), f32[8,64,768]{2,1,0:T(8,128)}, u32[]{:S(2)}, u32[]{:S(2)}) %all-to-all-start.5) | async-done | bytes 1572896 | tf_op jit(solution)/shard_map/all_to_all | solution.py:23
  235.3 4.7 %multiply_subtract_fusion.1 = (f32[512,768]{1,0:T(8,128)}, f32[512,768]{1,0:T(8,128)S(1)}) fusion(f32[512,768]{1,0:T(8,128)} %param.22, f32[768]{0:T(1024)S(1)} %neg.8, f32[768]{0:T(1024)S(1)} %copy-done.4, f32[8,64,768]{2,1,0:T(8,128)} %all-to-all-done.1, f32[768]{0:T(1024)S(1)} %neg.9, f32[768]{0:T(1024)S(1)} %copy-done.5, f32[512,768]{1,0:T(8,128)} %param.23, ...), kind=kLoop, calls=%fused_computation.29 | loop fusion | flops 5898240 | bytes 9449472 | tf_op jit(solution)/shard_map/sub | solution.py:69
  240.1 1.4 fusion.20
  241.7 3.5 collective-permute-start.2
  245.2 3.0 collective-permute-done.2
  248.2 0.4 bitcast_add_fusion
  248.6 23.7 %all_to_all.59 = f32[8,32,1536]{2,1,0:T(8,128)S(1)} all-to-all(f32[8,32,1536]{2,1,0:T(8,128)S(1)} %bitcast_add_fusion), channel_id=1, replica_groups=mesh['line_outer'=8,'line_core'=2,'col'=8] {'line_outer'}, dimensions={0} | all-to-all | bytes 3145728 | tf_op jit(solution)/shard_map/all_to_all | solution.py:49
  272.5 22.5 %all_to_all.60 = f32[8,32,1536]{2,1,0:T(8,128)S(1)} all-to-all(f32[8,32,1536]{2,1,0:T(8,128)S(1)} %broadcast_in_dim.27), channel_id=1, replica_groups=mesh['line_outer'=8,'line_core'=2,'col'=8] {'line_outer'}, dimensions={0} | all-to-all | bytes 3145728 | tf_op jit(solution)/shard_map/all_to_all | solution.py:57
  295.0 2.2 collective-permute-start.3
  297.2 3.0 collective-permute-done.3
  300.3 0.3 maximum_select_fusion
  300.6 0.3 bitcast_multiply_fusion
  300.9 5.4 %fusion.6 = f32[8,64,768]{2,1,0:T(8,128)} fusion(f32[8,64,1536]{2,1,0:T(8,128)S(1)} %bitcast_multiply_fusion, s32[1536]{0:T(1024)S(1)} %get-tuple-element.9), kind=kOutput, calls=%fused_computation.9 | convolution fusion | flops 7248936960 | bytes 4724736 | tf_op jit(solution)/shard_map/dot_general | solution.py:120
  306.4 4.5 %all-to-all-start.8 = ((f32[8,64,768]{2,1,0:T(8,128)}), f32[8,64,768]{2,1,0:T(8,128)S(1)}, u32[]{:S(2)}, u32[]{:S(2)}) async-start(f32[8,64,768]{2,1,0:T(8,128)} %fusion.6), calls=%async_computation.8 | async-start | bytes 3145728 | tf_op jit(solution)/shard_map/all_to_all | solution.py:16
  310.9 20.6 %all-to-all-done.8 = f32[8,64,768]{2,1,0:T(8,128)S(1)} async-done(((f32[8,64,768]{2,1,0:T(8,128)}), f32[8,64,768]{2,1,0:T(8,128)S(1)}, u32[]{:S(2)}, u32[]{:S(2)}) %all-to-all-start.8) | async-done | bytes 1572896 | tf_op jit(solution)/shard_map/all_to_all | solution.py:16
  331.5 1.1 add_convert_fusion
  332.7 17.8 %all_to_all.61 = bf16[8,64,768]{2,1,0:T(8,128)(2,1)S(1)} all-to-all(bf16[8,64,768]{2,1,0:T(8,128)(2,1)S(1)} %broadcast_in_dim.28), channel_id=1, replica_groups=mesh['line_outer'=8,'line_core'=2,'col'=8] {'col'}, dimensions={0} | all-to-all | bytes 1572864 | tf_op jit(solution)/shard_map/all_to_all | solution.py:23
  350.5 6.0 %fusion = f32[8,2,32,4608]{3,2,1,0:T(8,128)S(1)} fusion(bf16[8,2,32,768]{3,2,1,0:T(8,128)(2,1)S(1)} %bitcast.108, bf16[768,4608]{1,0:T(8,128)(2,1)} %param.14), kind=kOutput, calls=%fused_computation | convolution fusion | flops 3623878656 | bytes 17301504 | tf_op jit(solution)/shard_map/dot_general | solution.py:133
  356.5 0.6 select_bitcast_fusion
  357.1 2.5 collective-permute-start.4
  359.6 7.5 %collective-permute-done.4 = f32[8,32,4608]{2,1,0:T(8,128)S(1)} collective-permute-done((f32[8,32,4608]{2,1,0:T(8,128)S(1)}, f32[8,32,4608]{2,1,0:T(8,128)S(1)}, u32[]{:S(2)}, u32[]{:S(2)}) %collective-permute-start.4) | collective-permute-done | bytes 4718624 | tf_op jit(solution)/shard_map/ppermute | solution.py:37
  367.2 3.3 fusion.3
  370.5 4.7 %all-to-all-start.10 = ((f32[8,32,4608]{2,1,0:T(8,128)}), f32[8,32,4608]{2,1,0:T(8,128)}, u32[]{:S(2)}, u32[]{:S(2)}) async-start(f32[8,32,4608]{2,1,0:T(8,128)} %fusion.3), calls=%async_computation.10 | async-start | bytes 9437184 | tf_op jit(solution)/shard_map/all_to_all | solution.py:49
  375.3 54.8 %all-to-all-done.10 = f32[8,32,4608]{2,1,0:T(8,128)} async-done(((f32[8,32,4608]{2,1,0:T(8,128)}), f32[8,32,4608]{2,1,0:T(8,128)}, u32[]{:S(2)}, u32[]{:S(2)}) %all-to-all-start.10) | async-done | bytes 4718624 | tf_op jit(solution)/shard_map/all_to_all | solution.py:49
  430.1 2.8 reduce_sum.69
  432.9 1.7 maximum_minimum_fusion
  (39 shorter events, 1.4 us)
Async XLA Ops:
  7.2 175.3 %copy-start = (bf16[768,1536]{1,0:T(8,128)(2,1)S(1)}, bf16[768,1536]{1,0:T(8,128)(2,1)}, u32[]{:S(2)}) copy-start(bf16[768,1536]{1,0:T(8,128)(2,1)} %param.15) | copy-start | bytes 7077892
  7.2 63.7 %all-gather.2.cloned.1.call-start = ((), (), s32[]{:S(2)}) async-start(), calls=%async_computation.11 | async-start | bytes 10027008 | tf_op jit(solution)/shard_map/all_gather | solution.py:96
  113.7 4.4 %copy-start.7 = (s32[1536]{0:T(1024)S(1)}, s32[1536]{0:T(1024)}, u32[]{:S(2)}) copy-start(s32[1536]{0:T(1024)} %param.26) | copy-start | bytes 18436
  113.7 22.9 %copy-start.6 = (f32[1536]{0:T(1024)S(1)}, f32[1536]{0:T(1024)}, u32[]{:S(2)}) copy-start(f32[1536]{0:T(1024)} %param.27) | copy-start | bytes 18436
  113.7 22.9 %all-to-all-start.1 = ((f32[8,64,768]{2,1,0:T(8,128)}), f32[8,64,768]{2,1,0:T(8,128)}, u32[]{:S(2)}, u32[]{:S(2)}) async-start(f32[8,64,768]{2,1,0:T(8,128)} %broadcast_in_dim.22), calls=%async_computation.1 | async-start | bytes 3145728 | tf_op jit(solution)/shard_map/all_to_all | solution.py:23
  142.2 5.2 %collective-permute-start = (bf16[8,32,1536]{2,1,0:T(8,128)(2,1)S(1)}, bf16[8,32,1536]{2,1,0:T(8,128)(2,1)S(1)}, u32[]{:S(2)}, u32[]{:S(2)}) collective-permute-start(bf16[8,32,1536]{2,1,0:T(8,128)(2,1)S(1)} %fusion.17), channel_id=1, source_target_pairs={{0,8},{8,0},{1,9},{9,1},{2,10},{10,2},{3,11},{11,3},{4,12},{12,4},... | collective-permute-start | bytes 2359304 | tf_op jit(solution)/shard_map/ppermute | solution.py:37
  178.1 4.2 collective-permute-start.1
  212.5 4.4 %copy-start.4 = (f32[768]{0:T(1024)S(1)}, f32[768]{0:T(1024)}, u32[]{:S(2)}) copy-start(f32[768]{0:T(1024)} %param.24) | copy-start | bytes 9220
  212.6 4.5 %copy-start.5 = (f32[768]{0:T(1024)S(1)}, f32[768]{0:T(1024)}, u32[]{:S(2)}) copy-start(f32[768]{0:T(1024)} %param.25) | copy-start | bytes 9220
  212.6 22.8 %all-to-all-start.5 = ((f32[8,64,768]{2,1,0:T(8,128)}), f32[8,64,768]{2,1,0:T(8,128)}, u32[]{:S(2)}, u32[]{:S(2)}) async-start(f32[8,64,768]{2,1,0:T(8,128)} %broadcast_in_dim.26), calls=%async_computation.5 | async-start | bytes 3145728 | tf_op jit(solution)/shard_map/all_to_all | solution.py:23
  240.1 1.4 copy-start.3
  241.7 6.5 %collective-permute-start.2 = (f32[8,32,1536]{2,1,0:T(8,128)S(1)}, f32[8,32,1536]{2,1,0:T(8,128)S(1)}, u32[]{:S(2)}, u32[]{:S(2)}) collective-permute-start(f32[8,32,1536]{2,1,0:T(8,128)S(1)} %select_bitcast_fusion.1), channel_id=1, source_target_pairs={{0,8},{8,0},{1,9},{9,1},{2,10},{10,2},{3,11},{11,3},{4,12},{12,4},... | collective-permute-start | bytes 4718600 | tf_op jit(solution)/shard_map/ppermute | solution.py:37
  295.0 5.3 %collective-permute-start.3 = (f32[8,32,1536]{2,1,0:T(8,128)S(1)}, f32[8,32,1536]{2,1,0:T(8,128)S(1)}, u32[]{:S(2)}, u32[]{:S(2)}) collective-permute-start(f32[8,32,1536]{2,1,0:T(8,128)S(1)} %all_to_all.60), channel_id=1, source_target_pairs={{0,8},{8,0},{1,9},{9,1},{2,10},{10,2},{3,11},{11,3},{4,12},{12,4},... | collective-permute-start | bytes 4718600 | tf_op jit(solution)/shard_map/ppermute | solution.py:37
  306.4 25.1 %all-to-all-start.8 = ((f32[8,64,768]{2,1,0:T(8,128)}), f32[8,64,768]{2,1,0:T(8,128)S(1)}, u32[]{:S(2)}, u32[]{:S(2)}) async-start(f32[8,64,768]{2,1,0:T(8,128)} %fusion.6), calls=%async_computation.8 | async-start | bytes 3145728 | tf_op jit(solution)/shard_map/all_to_all | solution.py:16
  357.1 10.1 %collective-permute-start.4 = (f32[8,32,4608]{2,1,0:T(8,128)S(1)}, f32[8,32,4608]{2,1,0:T(8,128)S(1)}, u32[]{:S(2)}, u32[]{:S(2)}) collective-permute-start(f32[8,32,4608]{2,1,0:T(8,128)S(1)} %select_bitcast_fusion), channel_id=1, source_target_pairs={{0,8},{8,0},{1,9},{9,1},{2,10},{10,2},{3,11},{11,3},{4,12},{12,4},... | collective-permute-start | bytes 14155784 | tf_op jit(solution)/shard_map/ppermute | solution.py:37
  370.5 4.7 %copy-start.9 = (f32[32]{0:T(128)S(1)}, f32[32]{0:T(128)}, u32[]{:S(2)}) copy-start(f32[32]{0:T(128)} %param.21) | copy-start | bytes 388
  370.5 4.8 %copy-start.10 = (f32[32]{0:T(128)S(1)}, f32[32]{0:T(128)}, u32[]{:S(2)}) copy-start(f32[32]{0:T(128)} %param.20) | copy-start | bytes 388
  370.5 59.5 %all-to-all-start.10 = ((f32[8,32,4608]{2,1,0:T(8,128)}), f32[8,32,4608]{2,1,0:T(8,128)}, u32[]{:S(2)}, u32[]{:S(2)}) async-start(f32[8,32,4608]{2,1,0:T(8,128)} %fusion.3), calls=%async_computation.10 | async-start | bytes 9437184 | tf_op jit(solution)/shard_map/all_to_all | solution.py:49
  375.3 57.6 %copy-start.8 = (f32[32]{0:T(128)}, f32[32]{0:T(128)S(1)}, u32[]{:S(2)}) copy-start(f32[32]{0:T(128)S(1)} %multiply_add_fusion) | copy-start | bytes 388
  375.3 57.6 %copy-start.2 = (f32[32,4608]{1,0:T(8,128)S(1)}, f32[32,4608]{1,0:T(8,128)}, u32[]{:S(2)}) copy-start(f32[32,4608]{1,0:T(8,128)} %param.16) | copy-start | bytes 1769476
  430.1 4.5 %copy-start.1 = (bf16[768,1536]{1,0:T(8,128)(2,1)S(1)}, bf16[768,1536]{1,0:T(8,128)(2,1)}, u32[]{:S(2)}) copy-start(bf16[768,1536]{1,0:T(8,128)(2,1)} %param.15) | copy-start | bytes 7077892
Sparse Core Ops, SparseCore 0:
  10.2 60.6 all-gather.1

commit v11 on v10

--- a/solution.py
+++ b/solution.py
@@ -91,15 +91,40 @@
     stacked = jnp.stack([extra_high, extra_low], axis=0)
     lines_dev = ptdf.shape[0]
     ptdf_turned = ptdf.T
+    outer = lax.axis_size(LINE_OUTER)
+    line_devs = 2 * outer
+    rows = injection.shape[0]
+    half = rows // 2
+
+    def flows(portion):
+        lead = portion.shape[:-3]
+        count = portion.shape[-2]
+        flat = portion.reshape(-1, portion.shape[-1])
+        product = jnp.dot(flat, ptdf_turned, preferred_element_type=jnp.float32)
+        product = product.reshape(*lead, 2, count, lines_dev)
+        return product[..., 0, :, :] + product[..., 1, :, :]
+
+    by_gather = lax.all_gather(stacked[:, :half], LINE, axis=1, tiled=True)
+    copies = jnp.broadcast_to(stacked[None, :, half:], (outer, *stacked[:, half:].shape))
+    mine = lax.all_to_all(copies, LINE_OUTER, 0, 0, tiled=True)
+    other = swap_cores(mine)
+    core = lax.axis_index(LINE_CORE)
+    gather_flow = flows(by_gather).reshape(line_devs, half, lines_dev)
+    mine_flow, other_flow = flows(mine), flows(other)
+    swap_flow = jnp.where(
+        core == 0, jnp.stack([mine_flow, other_flow], axis=1), jnp.stack([other_flow, mine_flow], axis=1)
+    ).reshape(line_devs, rows - half, lines_dev)
+    flow_part = jnp.concatenate([gather_flow, swap_flow], axis=1).reshape(line_devs * rows, lines_dev)
     local_total = jnp.sum(extra_high.astype(jnp.float32) + extra_low.astype(jnp.float32), axis=1)
-    bus_total = lax.psum(local_total, "col")
-    portion = lax.all_gather(stacked, LINE, axis=1, tiled=True)
-    portion, bus_total = lax.optimization_barrier((portion, bus_total))
-    count = portion.shape[1]
-    flat = portion.reshape(2 * count, portion.shape[2])
-    product = jnp.dot(flat, ptdf_turned, preferred_element_type=jnp.float32)
-    flow_part = product[:count] + product[count:]
-    base_flow = full_sum(flow_part, "col")
+    first_snapshot = lax.axis_index(LINE) * rows
+    totals = lax.dynamic_update_slice(
+        jnp.zeros((line_devs * rows, 128), jnp.float32),
+        jnp.broadcast_to(local_total[:, None], (rows, 128)),
+        (first_snapshot, 0),
+    )
+    summed = full_sum(jnp.concatenate([flow_part, totals], axis=1), "col")
+    base_flow = summed[:, :lines_dev]
+    bus_total = lax.dynamic_slice_in_dim(summed[:, lines_dev], first_snapshot, rows)
     balance_new = balance_dual + (bus_total - demand) / BUSES
     base_new = dual_update(base_dual, base_flow, flow_limit[None, :])
     first_line = lax.axis_index(LINE) * lines_dev

time: 442 us -> 447 us (1.011)
  blocking collectives: 170 us -> 150 us
  starting transfers between devices: 31.9 us -> 41.2 us
  matrix products: 31.9 us -> 39.3 us
    all_to_all x0 -> x1, waiting for transfers between devices: none -> 39 us  [on_device(): mine = lax.all_to_all(copies, LINE_OUTER, 0, 0, tiled=True)]
    all_gather x1, waiting for transfers between devices: 39.2 us -> 1.77 us  [on_device(): by_gather = lax.all_gather(stacked[:, :half], LINE, axis=1, tiled=True)]
    psum x1 -> x0, blocking collectives: 21.9 us -> none  [on_device(): bus_total = lax.psum(local_total, 'col')]
    dot_general x1 -> x3, matrix products: 12.1 us -> 19.5 us  [flows(): product = jnp.dot(flat, ptdf_turned, preferred_element_type=jnp.float32)]
    all_to_all x0 -> x1, starting transfers between devices: none -> 6.78 us  [on_device(): mine = lax.all_to_all(copies, LINE_OUTER, 0, 0, tiled=True)]
    ppermute x5 -> x6, starting transfers between devices: 13.8 us -> 16.1 us  [swap_cores(): return lax.ppermute(value, LINE_CORE, [(0, 1), (1, 0)])]
    ppermute x5 -> x6, waiting for transfers between devices: 17.4 us -> 17.4 us  [swap_cores(): return lax.ppermute(value, LINE_CORE, [(0, 1), (1, 0)])]
  transfers between devices with their start and end apart: 10 -> 12, of which waited for: 10 -> 11; matrix products, arithmetic and copies ran while one was open for 0% -> 3% of each run, Pallas kernels for 0% -> 0%
where the time goes in v11:
time: 447 us; the launch traced here: 446 us
  waiting for transfers between devices  173 us (39%)
  blocking collectives  150 us (34%)
  starting transfers between devices  41.2 us (9%)
  matrix products  39.3 us (9%)
  other arithmetic  22.1 us (5%)
  between operations  14.4 us (3%)
  local copies, waits for them, and re-layouts  5.89 us (1%)
    all_to_all x2, blocking collectives, summed_block(): lax.all_to_all(value.reshape(n, rows, *value.shape[1:]), axis, 0, 0, tile...  56.5 us
    all_to_all x1, waiting for transfers between devices, line_summed_block(): parts = lax.all_to_all(pair_sum, LINE_OUTER, 0, 0, tiled=True)  53.7 us
    all_to_all x2, waiting for transfers between devices, gathered_rows(): whole = lax.all_to_all(copies, axis, 0, 0, tiled=True)  40.7 us
    all_to_all x1, waiting for transfers between devices, on_device(): mine = lax.all_to_all(copies, LINE_OUTER, 0, 0, tiled=True)  39 us
    all_to_all x2, blocking collectives, line_summed_block(): parts = lax.all_to_all(pair_sum, LINE_OUTER, 0, 0, tiled=True)  38.6 us
    all_to_all x2, blocking collectives, line_gathered_rows(): mine = lax.all_to_all(copies, LINE_OUTER, 0, 0, tiled=True)  36.9 us
    all_to_all x1, waiting for transfers between devices, summed_block(): lax.all_to_all(value.reshape(n, rows, *value.shape[1:]), axis, 0, 0, tile...  20.6 us
    dot_general x3, matrix products, flows(): product = jnp.dot(flat, ptdf_turned, preferred_element_type=jnp.float32)  19.5 us
  transfers between devices with their start and end apart: 12, of which 11 were waited for; matrix products, arithmetic and copies ran while one was open for 3% of the time, Pallas kernels for 0%

profile of v11, /device:TPU:1, one launch (start us, length us, event | category | flops | bytes accessed | tf_op | source)
XLA Modules:
  0.0 445.8 jit_solution(9685070701207135233)
XLA Ops:
  7.2 1.6 convert_bitcast_fusion
  9.6 1.7 broadcast_in_dim.28
  11.3 6.8 %all-to-all-start = ((bf16[8,2,16,4608]{3,2,1,0:T(8,128)(2,1)}), bf16[8,2,16,4608]{3,2,1,0:T(8,128)(2,1)}, u32[]{:S(2)}, u32[]{:S(2)}) async-start(bf16[8,2,16,4608]{3,2,1,0:T(8,128)(2,1)} %broadcast_in_dim.28), calls=%async_computation | async-start | bytes 4718592 | tf_op jit(solution)/shard_map/all_to_all | solution.py:109
  18.1 39.0 %all-to-all-done = bf16[8,2,16,4608]{3,2,1,0:T(8,128)(2,1)} async-done(((bf16[8,2,16,4608]{3,2,1,0:T(8,128)(2,1)}), bf16[8,2,16,4608]{3,2,1,0:T(8,128)(2,1)}, u32[]{:S(2)}, u32[]{:S(2)}) %all-to-all-start) | async-done | bytes 2359328 | tf_op jit(solution)/shard_map/all_to_all | solution.py:109
  57.1 3.6 collective-permute-start
  60.9 5.9 %fusion.4 = f32[8,2,16,768]{3,2,1,0:T(8,128)S(1)} fusion(bf16[8,2,16,4608]{3,2,1,0:T(8,128)(2,1)} %all-to-all-done, bf16[768,4608]{1,0:T(8,128)(2,1)} %param.14), kind=kOutput, calls=%fused_computation.4 | convolution fusion | flops 1811939328 | bytes 10223616 | tf_op jit(solution)/shard_map/dot_general | solution.py:103
  66.8 5.9 %fusion.2 = f32[8,2,16,768]{3,2,1,0:T(8,128)S(1)} fusion(bf16[8,2,16,4608]{3,2,1,0:T(8,128)(2,1)} %collective-permute-done, bf16[768,4608]{1,0:T(8,128)(2,1)} %param.14), kind=kOutput, calls=%fused_computation.2 | convolution fusion | flops 1811939328 | bytes 10223616 | tf_op jit(solution)/shard_map/dot_general | solution.py:103
  72.8 1.8 all-gather.2.cloned.1.call-done
  74.6 7.8 %fusion.31 = f32[512,768]{1,0:T(8,128)S(1)} fusion(bf16[512,4608]{1,0:T(8,128)(2,1)} %bitcast.119, bf16[768,4608]{1,0:T(8,128)(2,1)} %param.14), kind=kOutput, calls=%fused_computation.65 | convolution fusion | flops 3623878656 | bytes 13369344 | tf_op jit(solution)/shard_map/dot_general | solution.py:103
  82.7 30.3 %all_to_all.60 = f32[8,64,896]{2,1,0:T(8,128)} all-to-all(f32[8,64,896]{2,1,0:T(8,128)S(1)} %pad_maximum_fusion), channel_id=1, replica_groups=mesh['line_outer'=8,'line_core'=2,'col'=8] {'col'}, dimensions={0} | all-to-all | bytes 3670016 | tf_op jit(solution)/shard_map/all_to_all | solution.py:16
  113.0 1.6 reduce_sum.64
  114.6 1.4 broadcast_in_dim.31
  116.0 4.4 all-to-all-start.2
  120.5 22.6 %all-to-all-done.2 = f32[8,64,896]{2,1,0:T(8,128)} async-done(((f32[8,64,896]{2,1,0:T(8,128)}), f32[8,64,896]{2,1,0:T(8,128)}, u32[]{:S(2)}, u32[]{:S(2)}) %all-to-all-start.2) | async-done | bytes 1835040 | tf_op jit(solution)/shard_map/all_to_all | solution.py:23
  143.1 5.4 %fusion.14 = bf16[512,1536]{1,0:T(8,128)(2,1)S(1)} fusion(s32[1536]{0:T(1024)S(1)} %get-tuple-element.5, f32[1536]{0:T(1024)S(1)} %copy-done.6, pred[1536]{0:T(1024)(128)(4,1)S(1)} %get-tuple-element.4, f32[512,896]{1,0:T(8,128)} %bitcast.10), kind=kOutput, calls=%fused_computation.18 | convolution fusion | flops 7251296256 | bytes 3159552 | tf_op jit(solution)/shard_map/dot_general | solution.py:136
  148.6 2.0 collective-permute-start.1
  150.6 1.9 collective-permute-done.1
  152.6 15.1 %all_to_all.61 = bf16[8,32,1536]{2,1,0:T(8,128)(2,1)S(1)} all-to-all(bf16[8,32,1536]{2,1,0:T(8,128)(2,1)S(1)} %fusion.24), channel_id=1, replica_groups=mesh['line_outer'=8,'line_core'=2,'col'=8] {'line_outer'}, dimensions={0} | all-to-all | bytes 1572864 | tf_op jit(solution)/shard_map/all_to_all | solution.py:49
  167.9 14.4 %all_to_all.62 = bf16[8,32,1536]{2,1,0:T(8,128)(2,1)S(1)} all-to-all(bf16[8,32,1536]{2,1,0:T(8,128)(2,1)S(1)} %broadcast_in_dim.34), channel_id=1, replica_groups=mesh['line_outer'=8,'line_core'=2,'col'=8] {'line_outer'}, dimensions={0} | all-to-all | bytes 1572864 | tf_op jit(solution)/shard_map/all_to_all | solution.py:57
  182.4 2.3 collective-permute-start.2
  184.7 1.9 collective-permute-done.2
  186.8 1.4 fusion.15
  188.2 26.2 %all_to_all.63 = f32[8,64,768]{2,1,0:T(8,128)} all-to-all(f32[8,64,768]{2,1,0:T(8,128)S(1)} %fusion.15), channel_id=1, replica_groups=mesh['line_outer'=8,'line_core'=2,'col'=8] {'col'}, dimensions={0} | all-to-all | bytes 3145728 | tf_op jit(solution)/shard_map/all_to_all | solution.py:16
  214.4 1.5 reduce_sum.66
  215.9 1.3 broadcast_in_dim.35
  217.2 4.6 %all-to-all-start.6 = ((f32[8,64,768]{2,1,0:T(8,128)}), f32[8,64,768]{2,1,0:T(8,128)}, u32[]{:S(2)}, u32[]{:S(2)}) async-start(f32[8,64,768]{2,1,0:T(8,128)} %broadcast_in_dim.35), calls=%async_computation.6 | async-start | bytes 3145728 | tf_op jit(solution)/shard_map/all_to_all | solution.py:23
  221.8 18.1 %all-to-all-done.6 = f32[8,64,768]{2,1,0:T(8,128)} async-done(((f32[8,64,768]{2,1,0:T(8,128)}), f32[8,64,768]{2,1,0:T(8,128)}, u32[]{:S(2)}, u32[]{:S(2)}) %all-to-all-start.6) | async-done | bytes 1572896 | tf_op jit(solution)/shard_map/all_to_all | solution.py:23
  239.9 4.7 %multiply_subtract_fusion.1 = (f32[512,768]{1,0:T(8,128)}, f32[512,768]{1,0:T(8,128)S(1)}) fusion(f32[512,768]{1,0:T(8,128)} %param.22, f32[512,896]{1,0:T(8,128)} %bitcast.10, f32[768]{0:T(1024)S(1)} %neg.8, f32[768]{0:T(1024)S(1)} %copy-done.4, f32[768]{0:T(1024)S(1)} %neg.9, f32[768]{0:T(1024)S(1)} %copy-done.5, f32[512,768]{1,0:T(8,128)} %param.23, ...), kind=kLoop, calls=%fused_computation.34 | loop fusion | flops 5898240 | bytes 9449472 | tf_op jit(solution)/shard_map/sub | solution.py:69
  244.7 1.4 fusion.25
  246.3 3.5 collective-permute-start.3
  249.8 3.0 collective-permute-done.3
  253.2 23.5 %all_to_all.64 = f32[8,32,1536]{2,1,0:T(8,128)S(1)} all-to-all(f32[8,32,1536]{2,1,0:T(8,128)S(1)} %bitcast_add_fusion), channel_id=1, replica_groups=mesh['line_outer'=8,'line_core'=2,'col'=8] {'line_outer'}, dimensions={0} | all-to-all | bytes 3145728 | tf_op jit(solution)/shard_map/all_to_all | solution.py:49
  276.9 22.5 %all_to_all.65 = f32[8,32,1536]{2,1,0:T(8,128)S(1)} all-to-all(f32[8,32,1536]{2,1,0:T(8,128)S(1)} %broadcast_in_dim.36), channel_id=1, replica_groups=mesh['line_outer'=8,'line_core'=2,'col'=8] {'line_outer'}, dimensions={0} | all-to-all | bytes 3145728 | tf_op jit(solution)/shard_map/all_to_all | solution.py:57
  299.4 2.2 collective-permute-start.4
  301.6 3.0 collective-permute-done.4
  305.4 5.4 %fusion.10 = f32[8,64,768]{2,1,0:T(8,128)} fusion(f32[8,64,1536]{2,1,0:T(8,128)S(1)} %bitcast_multiply_fusion, s32[1536]{0:T(1024)S(1)} %get-tuple-element.5), kind=kOutput, calls=%fused_computation.13 | convolution fusion | flops 7248936960 | bytes 4724736 | tf_op jit(solution)/shard_map/dot_general | solution.py:145
  310.8 4.4 all-to-all-start.9
  315.2 20.6 %all-to-all-done.9 = f32[8,64,768]{2,1,0:T(8,128)S(1)} async-done(((f32[8,64,768]{2,1,0:T(8,128)}), f32[8,64,768]{2,1,0:T(8,128)S(1)}, u32[]{:S(2)}, u32[]{:S(2)}) %all-to-all-start.9) | async-done | bytes 1572896 | tf_op jit(solution)/shard_map/all_to_all | solution.py:16
  335.9 1.1 add_convert_fusion
  337.0 17.8 %all_to_all.66 = bf16[8,64,768]{2,1,0:T(8,128)(2,1)S(1)} all-to-all(bf16[8,64,768]{2,1,0:T(8,128)(2,1)S(1)} %broadcast_in_dim.37), channel_id=1, replica_groups=mesh['line_outer'=8,'line_core'=2,'col'=8] {'col'}, dimensions={0} | all-to-all | bytes 1572864 | tf_op jit(solution)/shard_map/all_to_all | solution.py:23
  354.8 6.0 %fusion = f32[8,2,32,4608]{3,2,1,0:T(8,128)S(1)} fusion(bf16[8,2,32,768]{3,2,1,0:T(8,128)(2,1)S(1)} %bitcast.117, bf16[768,4608]{1,0:T(8,128)(2,1)} %param.14), kind=kOutput, calls=%fused_computation | convolution fusion | flops 3623878656 | bytes 17301504 | tf_op jit(solution)/shard_map/dot_general | solution.py:158
  361.5 2.5 collective-permute-start.5
  364.0 7.5 %collective-permute-done.5 = f32[8,32,4608]{2,1,0:T(8,128)S(1)} collective-permute-done((f32[8,32,4608]{2,1,0:T(8,128)S(1)}, f32[8,32,4608]{2,1,0:T(8,128)S(1)}, u32[]{:S(2)}, u32[]{:S(2)}) %collective-permute-start.5) | collective-permute-done | bytes 4718624 | tf_op jit(solution)/shard_map/ppermute | solution.py:37
  371.5 3.3 fusion.7
  374.9 4.7 %all-to-all-start.11 = ((f32[8,32,4608]{2,1,0:T(8,128)}), f32[8,32,4608]{2,1,0:T(8,128)}, u32[]{:S(2)}, u32[]{:S(2)}) async-start(f32[8,32,4608]{2,1,0:T(8,128)} %fusion.7), calls=%async_computation.11 | async-start | bytes 9437184 | tf_op jit(solution)/shard_map/all_to_all | solution.py:49
  380.8 53.7 %all-to-all-done.11 = f32[8,32,4608]{2,1,0:T(8,128)} async-done(((f32[8,32,4608]{2,1,0:T(8,128)}), f32[8,32,4608]{2,1,0:T(8,128)}, u32[]{:S(2)}, u32[]{:S(2)}) %all-to-all-start.11) | async-done | bytes 4718624 | tf_op jit(solution)/shard_map/all_to_all | solution.py:49
  434.4 2.8 reduce_sum.69
  437.2 1.7 maximum_minimum_fusion
  (54 shorter events, 5.3 us)
Async XLA Ops:
  7.2 179.6 %copy-start = (bf16[768,1536]{1,0:T(8,128)(2,1)S(1)}, bf16[768,1536]{1,0:T(8,128)(2,1)}, u32[]{:S(2)}) copy-start(bf16[768,1536]{1,0:T(8,128)(2,1)} %param.15) | copy-start | bytes 7077892
  7.2 67.4 %all-gather.2.cloned.1.call-start = ((), (), s32[]{:S(2)}) async-start(), calls=%async_computation.12 | async-start | bytes 5013504 | tf_op jit(solution)/shard_map/all_gather | solution.py:107
  11.3 45.8 %all-to-all-start = ((bf16[8,2,16,4608]{3,2,1,0:T(8,128)(2,1)}), bf16[8,2,16,4608]{3,2,1,0:T(8,128)(2,1)}, u32[]{:S(2)}, u32[]{:S(2)}) async-start(bf16[8,2,16,4608]{3,2,1,0:T(8,128)(2,1)} %broadcast_in_dim.28), calls=%async_computation | async-start | bytes 4718592 | tf_op jit(solution)/shard_map/all_to_all | solution.py:109
  57.1 9.7 %collective-permute-start = (bf16[8,2,16,4608]{3,2,1,0:T(8,128)(2,1)}, bf16[8,2,16,4608]{3,2,1,0:T(8,128)(2,1)}, u32[]{:S(2)}, u32[]{:S(2)}) collective-permute-start(bf16[8,2,16,4608]{3,2,1,0:T(8,128)(2,1)} %all-to-all-done), channel_id=1, source_target_pairs={{0,8},{8,0},{1,9},{9,1},{2,10},{10,2},{3,11},{11,3},{4,12},{12,4},... | collective-permute-start | bytes 7077896 | tf_op jit(solution)/shard_map/ppermute | solution.py:37
  116.0 4.5 %copy-start.7 = (s32[1536]{0:T(1024)S(1)}, s32[1536]{0:T(1024)}, u32[]{:S(2)}) copy-start(s32[1536]{0:T(1024)} %param.26) | copy-start | bytes 18436
  116.0 27.1 %copy-start.6 = (f32[1536]{0:T(1024)S(1)}, f32[1536]{0:T(1024)}, u32[]{:S(2)}) copy-start(f32[1536]{0:T(1024)} %param.27) | copy-start | bytes 18436
  116.0 27.1 %all-to-all-start.2 = ((f32[8,64,896]{2,1,0:T(8,128)}), f32[8,64,896]{2,1,0:T(8,128)}, u32[]{:S(2)}, u32[]{:S(2)}) async-start(f32[8,64,896]{2,1,0:T(8,128)} %broadcast_in_dim.31), calls=%async_computation.2 | async-start | bytes 3670016 | tf_op jit(solution)/shard_map/all_to_all | solution.py:23
  148.6 3.9 collective-permute-start.1
  182.4 4.2 collective-permute-start.2
  217.2 4.6 %copy-start.4 = (f32[768]{0:T(1024)S(1)}, f32[768]{0:T(1024)}, u32[]{:S(2)}) copy-start(f32[768]{0:T(1024)} %param.24) | copy-start | bytes 9220
  217.2 4.6 %copy-start.5 = (f32[768]{0:T(1024)S(1)}, f32[768]{0:T(1024)}, u32[]{:S(2)}) copy-start(f32[768]{0:T(1024)} %param.25) | copy-start | bytes 9220
  217.2 22.8 %all-to-all-start.6 = ((f32[8,64,768]{2,1,0:T(8,128)}), f32[8,64,768]{2,1,0:T(8,128)}, u32[]{:S(2)}, u32[]{:S(2)}) async-start(f32[8,64,768]{2,1,0:T(8,128)} %broadcast_in_dim.35), calls=%async_computation.6 | async-start | bytes 3145728 | tf_op jit(solution)/shard_map/all_to_all | solution.py:23
  244.7 1.4 copy-start.3
  246.3 6.5 %collective-permute-start.3 = (f32[8,32,1536]{2,1,0:T(8,128)S(1)}, f32[8,32,1536]{2,1,0:T(8,128)S(1)}, u32[]{:S(2)}, u32[]{:S(2)}) collective-permute-start(f32[8,32,1536]{2,1,0:T(8,128)S(1)} %select_bitcast_fusion.1), channel_id=1, source_target_pairs={{0,8},{8,0},{1,9},{9,1},{2,10},{10,2},{3,11},{11,3},{4,12},{12,4},... | collective-permute-start | bytes 4718600 | tf_op jit(solution)/shard_map/ppermute | solution.py:37
  299.4 5.3 %collective-permute-start.4 = (f32[8,32,1536]{2,1,0:T(8,128)S(1)}, f32[8,32,1536]{2,1,0:T(8,128)S(1)}, u32[]{:S(2)}, u32[]{:S(2)}) collective-permute-start(f32[8,32,1536]{2,1,0:T(8,128)S(1)} %all_to_all.65), channel_id=1, source_target_pairs={{0,8},{8,0},{1,9},{9,1},{2,10},{10,2},{3,11},{11,3},{4,12},{12,4},... | collective-permute-start | bytes 4718600 | tf_op jit(solution)/shard_map/ppermute | solution.py:37
  310.8 25.0 %all-to-all-start.9 = ((f32[8,64,768]{2,1,0:T(8,128)}), f32[8,64,768]{2,1,0:T(8,128)S(1)}, u32[]{:S(2)}, u32[]{:S(2)}) async-start(f32[8,64,768]{2,1,0:T(8,128)} %fusion.10), calls=%async_computation.9 | async-start | bytes 3145728 | tf_op jit(solution)/shard_map/all_to_all | solution.py:16
  361.5 10.1 %collective-permute-start.5 = (f32[8,32,4608]{2,1,0:T(8,128)S(1)}, f32[8,32,4608]{2,1,0:T(8,128)S(1)}, u32[]{:S(2)}, u32[]{:S(2)}) collective-permute-start(f32[8,32,4608]{2,1,0:T(8,128)S(1)} %select_bitcast_fusion), channel_id=1, source_target_pairs={{0,8},{8,0},{1,9},{9,1},{2,10},{10,2},{3,11},{11,3},{4,12},{12,4},... | collective-permute-start | bytes 14155784 | tf_op jit(solution)/shard_map/ppermute | solution.py:37
  374.9 5.8 %copy-start.9 = (f32[32]{0:T(128)S(1)}, f32[32]{0:T(128)}, u32[]{:S(2)}) copy-start(f32[32]{0:T(128)} %param.21) | copy-start | bytes 388
  374.9 5.8 %copy-start.10 = (f32[32]{0:T(128)S(1)}, f32[32]{0:T(128)}, u32[]{:S(2)}) copy-start(f32[32]{0:T(128)} %param.20) | copy-start | bytes 388
  374.9 59.5 %all-to-all-start.11 = ((f32[8,32,4608]{2,1,0:T(8,128)}), f32[8,32,4608]{2,1,0:T(8,128)}, u32[]{:S(2)}, u32[]{:S(2)}) async-start(f32[8,32,4608]{2,1,0:T(8,128)} %fusion.7), calls=%async_computation.11 | async-start | bytes 9437184 | tf_op jit(solution)/shard_map/all_to_all | solution.py:49
  380.7 56.5 %copy-start.8 = (f32[32]{0:T(128)}, f32[32]{0:T(128)S(1)}, u32[]{:S(2)}) copy-start(f32[32]{0:T(128)S(1)} %multiply_add_fusion) | copy-start | bytes 388
  380.7 56.5 %copy-start.2 = (f32[32,4608]{1,0:T(8,128)S(1)}, f32[32,4608]{1,0:T(8,128)}, u32[]{:S(2)}) copy-start(f32[32,4608]{1,0:T(8,128)} %param.16) | copy-start | bytes 1769476
  434.4 4.5 %copy-start.1 = (bf16[768,1536]{1,0:T(8,128)(2,1)S(1)}, bf16[768,1536]{1,0:T(8,128)(2,1)}, u32[]{:S(2)}) copy-start(bf16[768,1536]{1,0:T(8,128)(2,1)} %param.15) | copy-start | bytes 7077892
Sparse Core Ops, SparseCore 0:
  10.2 64.3 all-gather.1

commit v12 on v11

--- a/solution.py
+++ b/solution.py
@@ -94,7 +94,7 @@
     outer = lax.axis_size(LINE_OUTER)
     line_devs = 2 * outer
     rows = injection.shape[0]
-    half = rows // 2
+    half = rows - rows // 4
 
     def flows(portion):
         lead = portion.shape[:-3]
@@ -104,7 +104,10 @@
         product = product.reshape(*lead, 2, count, lines_dev)
         return product[..., 0, :, :] + product[..., 1, :, :]
 
+    local_total = jnp.sum(extra_high.astype(jnp.float32) + extra_low.astype(jnp.float32), axis=1)
+    bus_total = lax.psum(local_total, "col")
     by_gather = lax.all_gather(stacked[:, :half], LINE, axis=1, tiled=True)
+    by_gather, bus_total = lax.optimization_barrier((by_gather, bus_total))
     copies = jnp.broadcast_to(stacked[None, :, half:], (outer, *stacked[:, half:].shape))
     mine = lax.all_to_all(copies, LINE_OUTER, 0, 0, tiled=True)
     other = swap_cores(mine)
@@ -115,16 +118,7 @@
         core == 0, jnp.stack([mine_flow, other_flow], axis=1), jnp.stack([other_flow, mine_flow], axis=1)
     ).reshape(line_devs, rows - half, lines_dev)
     flow_part = jnp.concatenate([gather_flow, swap_flow], axis=1).reshape(line_devs * rows, lines_dev)
-    local_total = jnp.sum(extra_high.astype(jnp.float32) + extra_low.astype(jnp.float32), axis=1)
-    first_snapshot = lax.axis_index(LINE) * rows
-    totals = lax.dynamic_update_slice(
-        jnp.zeros((line_devs * rows, 128), jnp.float32),
-        jnp.broadcast_to(local_total[:, None], (rows, 128)),
-        (first_snapshot, 0),
-    )
-    summed = full_sum(jnp.concatenate([flow_part, totals], axis=1), "col")
-    base_flow = summed[:, :lines_dev]
-    bus_total = lax.dynamic_slice_in_dim(summed[:, lines_dev], first_snapshot, rows)
+    base_flow = full_sum(flow_part, "col")
     balance_new = balance_dual + (bus_total - demand) / BUSES
     base_new = dual_update(base_dual, base_flow, flow_limit[None, :])
     first_line = lax.axis_index(LINE) * lines_dev

time: 447 us -> 438 us (0.980)
  waiting for transfers between devices: 173 us -> 130 us
  blocking collectives: 150 us -> 180 us
  starting transfers between devices: 41.2 us -> 45.7 us
    all_to_all x1, waiting for transfers between devices: 39 us -> 0.01 us  [on_device(): mine = lax.all_to_all(copies, LINE_OUTER, 0, 0, tiled=True)]
    psum x0 -> x1, blocking collectives: none -> 32.3 us  [on_device(): bus_total = lax.psum(local_total, 'col')]
    ppermute x6, starting transfers between devices: 16.1 us -> 20.7 us  [swap_cores(): return lax.ppermute(value, LINE_CORE, [(0, 1), (1, 0)])]
  transfers between devices with their start and end apart: 12 -> 12, of which waited for: 11 -> 10; matrix products, arithmetic and copies ran while one was open for 3% -> 3% of each run, Pallas kernels for 0% -> 0%
where the time goes in v12:
time: 438 us; the launch traced here: 437 us
  blocking collectives  180 us (41%)
  waiting for transfers between devices  130 us (30%)
  starting transfers between devices  45.7 us (10%)
  matrix products  40.7 us (9%)
  other arithmetic  21.9 us (5%)
  between operations  14.4 us (3%)
    all_to_all x1, waiting for transfers between devices, line_summed_block(): parts = lax.all_to_all(pair_sum, LINE_OUTER, 0, 0, tiled=True)  54.8 us
    all_to_all x2, blocking collectives, summed_block(): lax.all_to_all(value.reshape(n, rows, *value.shape[1:]), axis, 0, 0, tile...  53.4 us
    all_to_all x2, blocking collectives, line_summed_block(): parts = lax.all_to_all(pair_sum, LINE_OUTER, 0, 0, tiled=True)  39.5 us
    all_to_all x2, blocking collectives, line_gathered_rows(): mine = lax.all_to_all(copies, LINE_OUTER, 0, 0, tiled=True)  36.9 us
    all_to_all x2, waiting for transfers between devices, gathered_rows(): whole = lax.all_to_all(copies, axis, 0, 0, tiled=True)  36.7 us
    psum x1, blocking collectives, on_device(): bus_total = lax.psum(local_total, 'col')  32.3 us
    dot_general x3, matrix products, flows(): product = jnp.dot(flat, ptdf_turned, preferred_element_type=jnp.float32)  21 us
    ppermute x6, starting transfers between devices, swap_cores(): return lax.ppermute(value, LINE_CORE, [(0, 1), (1, 0)])  20.7 us
  transfers between devices with their start and end apart: 12, of which 10 were waited for; matrix products, arithmetic and copies ran while one was open for 3% of the time, Pallas kernels for 0%

profile of v12, /device:TPU:1, one launch (start us, length us, event | category | flops | bytes accessed | tf_op | source)
XLA Modules:
  0.0 436.5 jit_solution(11201866246346206107)
XLA Ops:
  7.2 1.6 fusion.27
  8.8 0.8 fusion.28
  9.7 1.1 broadcast_in_dim.24
  10.8 6.8 %all-to-all-start = ((bf16[8,2,8,4608]{3,2,1,0:T(8,128)(2,1)}), bf16[8,2,8,4608]{3,2,1,0:T(8,128)(2,1)S(1)}, u32[]{:S(2)}, u32[]{:S(2)}) async-start(bf16[8,2,8,4608]{3,2,1,0:T(8,128)(2,1)} %broadcast_in_dim.24), calls=%async_computation | async-start | bytes 2359296 | tf_op jit(solution)/shard_map/all_to_all | solution.py:112
  17.6 32.3 %psum.7 = f32[32]{0:T(128)S(1)} all-reduce(f32[32]{0:T(128)S(1)} %get-tuple-element.12), channel_id=1, replica_groups=mesh['line_outer'=8,'line_core'=2,'col'=8] {'col'}, use_global_device_ids=true, to_apply=%region_1.0 | all-reduce | flops 32 | bytes 256 | tf_op jit(solution)/shard_map/psum | solution.py:108
  49.9 6.9 %collective-permute-start = (bf16[8,2,8,4608]{3,2,1,0:T(8,128)(2,1)S(1)}, bf16[8,2,8,4608]{3,2,1,0:T(8,128)(2,1)S(1)}, u32[]{:S(2)}, u32[]{:S(2)}) collective-permute-start(bf16[8,2,8,4608]{3,2,1,0:T(8,128)(2,1)S(1)} %all-to-all-done), channel_id=1, source_target_pairs={{0,8},{8,0},{1,9},{9,1},{2,10},{10,2},{3,11},{11,3},{4,12},{12,4},... | collective-permute-start | bytes 3538952 | tf_op jit(solution)/shard_map/ppermute | solution.py:37
  56.7 5.6 %fusion.4 = f32[8,2,8,768]{3,2,1,0:T(8,128)S(1)} fusion(bf16[8,2,8,4608]{3,2,1,0:T(8,128)(2,1)S(1)} %all-to-all-done, bf16[768,4608]{1,0:T(8,128)(2,1)} %param.14), kind=kOutput, calls=%fused_computation.4 | convolution fusion | flops 905969664 | bytes 8650752 | tf_op jit(solution)/shard_map/dot_general | solution.py:103
  62.3 5.5 %fusion.2 = f32[8,2,8,768]{3,2,1,0:T(8,128)S(1)} fusion(bf16[8,2,8,4608]{3,2,1,0:T(8,128)(2,1)S(1)} %collective-permute-done, bf16[768,4608]{1,0:T(8,128)(2,1)} %param.14), kind=kOutput, calls=%fused_computation.2 | convolution fusion | flops 905969664 | bytes 8650752 | tf_op jit(solution)/shard_map/dot_general | solution.py:103
  68.3 10.0 %fusion.30 = f32[768,768]{1,0:T(8,128)S(1)} fusion(bf16[768,4608]{1,0:T(8,128)(2,1)} %bitcast.120, bf16[768,4608]{1,0:T(8,128)(2,1)} %param.14), kind=kOutput, calls=%fused_computation.61 | convolution fusion | flops 5435817984 | bytes 16515072 | tf_op jit(solution)/shard_map/dot_general | solution.py:103
  78.5 27.5 %all_to_all.60 = f32[8,64,768]{2,1,0:T(8,128)} all-to-all(f32[8,64,768]{2,1,0:T(8,128)S(1)} %bitcast.109), channel_id=1, replica_groups=mesh['line_outer'=8,'line_core'=2,'col'=8] {'col'}, dimensions={0} | all-to-all | bytes 3145728 | tf_op jit(solution)/shard_map/all_to_all | solution.py:16
  106.1 1.5 reduce_sum.64
  107.6 1.3 broadcast_in_dim.25
  108.8 4.4 %all-to-all-start.2 = ((f32[8,64,768]{2,1,0:T(8,128)}), f32[8,64,768]{2,1,0:T(8,128)}, u32[]{:S(2)}, u32[]{:S(2)}) async-start(f32[8,64,768]{2,1,0:T(8,128)} %broadcast_in_dim.25), calls=%async_computation.2 | async-start | bytes 3145728 | tf_op jit(solution)/shard_map/all_to_all | solution.py:23
  113.3 18.4 %all-to-all-done.2 = f32[8,64,768]{2,1,0:T(8,128)} async-done(((f32[8,64,768]{2,1,0:T(8,128)}), f32[8,64,768]{2,1,0:T(8,128)}, u32[]{:S(2)}, u32[]{:S(2)}) %all-to-all-start.2) | async-done | bytes 1572896 | tf_op jit(solution)/shard_map/all_to_all | solution.py:23
  131.8 5.5 %fusion.14 = bf16[512,1536]{1,0:T(8,128)(2,1)S(1)} fusion(f32[512,768]{1,0:T(8,128)} %bitcast.9, s32[1536]{0:T(1024)S(1)} %get-tuple-element.9, f32[1536]{0:T(1024)S(1)} %copy-done.6, pred[1536]{0:T(1024)(128)(4,1)S(1)} %get-tuple-element.8), kind=kOutput, calls=%fused_computation.18 | convolution fusion | flops 7251296256 | bytes 3159552 | tf_op jit(solution)/shard_map/dot_general | solution.py:130
  137.3 3.3 collective-permute-start.1
  140.6 1.9 collective-permute-done.1
  142.7 16.0 %all_to_all.61 = bf16[8,32,1536]{2,1,0:T(8,128)(2,1)S(1)} all-to-all(bf16[8,32,1536]{2,1,0:T(8,128)(2,1)S(1)} %fusion.23), channel_id=1, replica_groups=mesh['line_outer'=8,'line_core'=2,'col'=8] {'line_outer'}, dimensions={0} | all-to-all | bytes 1572864 | tf_op jit(solution)/shard_map/all_to_all | solution.py:49
  158.8 14.4 %all_to_all.62 = bf16[8,32,1536]{2,1,0:T(8,128)(2,1)S(1)} all-to-all(bf16[8,32,1536]{2,1,0:T(8,128)(2,1)S(1)} %broadcast_in_dim.28), channel_id=1, replica_groups=mesh['line_outer'=8,'line_core'=2,'col'=8] {'line_outer'}, dimensions={0} | all-to-all | bytes 1572864 | tf_op jit(solution)/shard_map/all_to_all | solution.py:57
  173.3 2.3 collective-permute-start.2
  175.6 1.9 collective-permute-done.2
  177.7 1.4 fusion.15
  179.1 25.8 %all_to_all.63 = f32[8,64,768]{2,1,0:T(8,128)} all-to-all(f32[8,64,768]{2,1,0:T(8,128)S(1)} %fusion.15), channel_id=1, replica_groups=mesh['line_outer'=8,'line_core'=2,'col'=8] {'col'}, dimensions={0} | all-to-all | bytes 3145728 | tf_op jit(solution)/shard_map/all_to_all | solution.py:16
  204.9 1.5 reduce_sum.66
  206.4 1.3 broadcast_in_dim.29
  207.7 4.6 %all-to-all-start.6 = ((f32[8,64,768]{2,1,0:T(8,128)}), f32[8,64,768]{2,1,0:T(8,128)}, u32[]{:S(2)}, u32[]{:S(2)}) async-start(f32[8,64,768]{2,1,0:T(8,128)} %broadcast_in_dim.29), calls=%async_computation.6 | async-start | bytes 3145728 | tf_op jit(solution)/shard_map/all_to_all | solution.py:23
  212.3 18.3 %all-to-all-done.6 = f32[8,64,768]{2,1,0:T(8,128)} async-done(((f32[8,64,768]{2,1,0:T(8,128)}), f32[8,64,768]{2,1,0:T(8,128)}, u32[]{:S(2)}, u32[]{:S(2)}) %all-to-all-start.6) | async-done | bytes 1572896 | tf_op jit(solution)/shard_map/all_to_all | solution.py:23
  230.6 4.7 %multiply_subtract_fusion.1 = (f32[512,768]{1,0:T(8,128)}, f32[512,768]{1,0:T(8,128)S(1)}) fusion(f32[512,768]{1,0:T(8,128)} %param.22, f32[768]{0:T(1024)S(1)} %neg.8, f32[768]{0:T(1024)S(1)} %copy-done.4, f32[8,64,768]{2,1,0:T(8,128)} %all-to-all-done.2, f32[768]{0:T(1024)S(1)} %neg.9, f32[768]{0:T(1024)S(1)} %copy-done.5, f32[512,768]{1,0:T(8,128)} %param.23, ...), kind=kLoop, calls=%fused_computation.33 | loop fusion | flops 5898240 | bytes 9449472 | tf_op jit(solution)/shard_map/sub | solution.py:69
  235.4 1.4 fusion.24
  237.0 3.5 collective-permute-start.3
  240.5 3.0 collective-permute-done.3
  243.9 23.5 %all_to_all.64 = f32[8,32,1536]{2,1,0:T(8,128)S(1)} all-to-all(f32[8,32,1536]{2,1,0:T(8,128)S(1)} %bitcast_add_fusion), channel_id=1, replica_groups=mesh['line_outer'=8,'line_core'=2,'col'=8] {'line_outer'}, dimensions={0} | all-to-all | bytes 3145728 | tf_op jit(solution)/shard_map/all_to_all | solution.py:49
  267.6 22.5 %all_to_all.65 = f32[8,32,1536]{2,1,0:T(8,128)S(1)} all-to-all(f32[8,32,1536]{2,1,0:T(8,128)S(1)} %broadcast_in_dim.30), channel_id=1, replica_groups=mesh['line_outer'=8,'line_core'=2,'col'=8] {'line_outer'}, dimensions={0} | all-to-all | bytes 3145728 | tf_op jit(solution)/shard_map/all_to_all | solution.py:57
  290.1 2.2 collective-permute-start.4
  292.4 3.0 collective-permute-done.4
  296.1 5.4 %fusion.10 = f32[8,64,768]{2,1,0:T(8,128)} fusion(f32[8,64,1536]{2,1,0:T(8,128)S(1)} %bitcast_multiply_fusion, s32[1536]{0:T(1024)S(1)} %get-tuple-element.9), kind=kOutput, calls=%fused_computation.13 | convolution fusion | flops 7248936960 | bytes 4724736 | tf_op jit(solution)/shard_map/dot_general | solution.py:139
  301.5 4.4 %all-to-all-start.9 = ((f32[8,64,768]{2,1,0:T(8,128)}), f32[8,64,768]{2,1,0:T(8,128)S(1)}, u32[]{:S(2)}, u32[]{:S(2)}) async-start(f32[8,64,768]{2,1,0:T(8,128)} %fusion.10), calls=%async_computation.9 | async-start | bytes 3145728 | tf_op jit(solution)/shard_map/all_to_all | solution.py:16
  305.9 20.6 %all-to-all-done.9 = f32[8,64,768]{2,1,0:T(8,128)S(1)} async-done(((f32[8,64,768]{2,1,0:T(8,128)}), f32[8,64,768]{2,1,0:T(8,128)S(1)}, u32[]{:S(2)}, u32[]{:S(2)}) %all-to-all-start.9) | async-done | bytes 1572896 | tf_op jit(solution)/shard_map/all_to_all | solution.py:16
  326.6 1.1 add_convert_fusion
  327.7 17.8 %all_to_all.66 = bf16[8,64,768]{2,1,0:T(8,128)(2,1)S(1)} all-to-all(bf16[8,64,768]{2,1,0:T(8,128)(2,1)S(1)} %broadcast_in_dim.31), channel_id=1, replica_groups=mesh['line_outer'=8,'line_core'=2,'col'=8] {'col'}, dimensions={0} | all-to-all | bytes 1572864 | tf_op jit(solution)/shard_map/all_to_all | solution.py:23
  345.5 6.0 %fusion = f32[8,2,32,4608]{3,2,1,0:T(8,128)S(1)} fusion(bf16[8,2,32,768]{3,2,1,0:T(8,128)(2,1)S(1)} %bitcast.118, bf16[768,4608]{1,0:T(8,128)(2,1)} %param.14), kind=kOutput, calls=%fused_computation | convolution fusion | flops 3623878656 | bytes 17301504 | tf_op jit(solution)/shard_map/dot_general | solution.py:152
  352.2 2.5 collective-permute-start.5
  354.7 7.5 %collective-permute-done.5 = f32[8,32,4608]{2,1,0:T(8,128)S(1)} collective-permute-done((f32[8,32,4608]{2,1,0:T(8,128)S(1)}, f32[8,32,4608]{2,1,0:T(8,128)S(1)}, u32[]{:S(2)}, u32[]{:S(2)}) %collective-permute-start.5) | collective-permute-done | bytes 4718624 | tf_op jit(solution)/shard_map/ppermute | solution.py:37
  362.2 3.3 fusion.7
  365.6 4.7 %all-to-all-start.11 = ((f32[8,32,4608]{2,1,0:T(8,128)}), f32[8,32,4608]{2,1,0:T(8,128)}, u32[]{:S(2)}, u32[]{:S(2)}) async-start(f32[8,32,4608]{2,1,0:T(8,128)} %fusion.7), calls=%async_computation.11 | async-start | bytes 9437184 | tf_op jit(solution)/shard_map/all_to_all | solution.py:49
  370.4 54.8 %all-to-all-done.11 = f32[8,32,4608]{2,1,0:T(8,128)} async-done(((f32[8,32,4608]{2,1,0:T(8,128)}), f32[8,32,4608]{2,1,0:T(8,128)}, u32[]{:S(2)}, u32[]{:S(2)}) %all-to-all-start.11) | async-done | bytes 4718624 | tf_op jit(solution)/shard_map/all_to_all | solution.py:49
  425.1 2.8 reduce_sum.69
  427.9 1.7 maximum_minimum_fusion
  (51 shorter events, 3.6 us)
Async XLA Ops:
  7.2 170.5 %copy-start = (bf16[768,1536]{1,0:T(8,128)(2,1)S(1)}, bf16[768,1536]{1,0:T(8,128)(2,1)}, u32[]{:S(2)}) copy-start(bf16[768,1536]{1,0:T(8,128)(2,1)} %param.15) | copy-start | bytes 7077892
  7.2 61.1 %all-gather.2.cloned.1.call-start = ((), (), s32[]{:S(2)}) async-start(), calls=%async_computation.12 | async-start | bytes 7520256 | tf_op jit(solution)/shard_map/all_gather | solution.py:109
  10.8 39.1 %all-to-all-start = ((bf16[8,2,8,4608]{3,2,1,0:T(8,128)(2,1)}), bf16[8,2,8,4608]{3,2,1,0:T(8,128)(2,1)S(1)}, u32[]{:S(2)}, u32[]{:S(2)}) async-start(bf16[8,2,8,4608]{3,2,1,0:T(8,128)(2,1)} %broadcast_in_dim.24), calls=%async_computation | async-start | bytes 2359296 | tf_op jit(solution)/shard_map/all_to_all | solution.py:112
  49.9 12.5 %collective-permute-start = (bf16[8,2,8,4608]{3,2,1,0:T(8,128)(2,1)S(1)}, bf16[8,2,8,4608]{3,2,1,0:T(8,128)(2,1)S(1)}, u32[]{:S(2)}, u32[]{:S(2)}) collective-permute-start(bf16[8,2,8,4608]{3,2,1,0:T(8,128)(2,1)S(1)} %all-to-all-done), channel_id=1, source_target_pairs={{0,8},{8,0},{1,9},{9,1},{2,10},{10,2},{3,11},{11,3},{4,12},{12,4},... | collective-permute-start | bytes 3538952 | tf_op jit(solution)/shard_map/ppermute | solution.py:37
  108.8 4.4 %copy-start.7 = (s32[1536]{0:T(1024)S(1)}, s32[1536]{0:T(1024)}, u32[]{:S(2)}) copy-start(s32[1536]{0:T(1024)} %param.26) | copy-start | bytes 18436
  108.8 22.9 %copy-start.6 = (f32[1536]{0:T(1024)S(1)}, f32[1536]{0:T(1024)}, u32[]{:S(2)}) copy-start(f32[1536]{0:T(1024)} %param.27) | copy-start | bytes 18436
  108.8 22.9 %all-to-all-start.2 = ((f32[8,64,768]{2,1,0:T(8,128)}), f32[8,64,768]{2,1,0:T(8,128)}, u32[]{:S(2)}, u32[]{:S(2)}) async-start(f32[8,64,768]{2,1,0:T(8,128)} %broadcast_in_dim.25), calls=%async_computation.2 | async-start | bytes 3145728 | tf_op jit(solution)/shard_map/all_to_all | solution.py:23
  137.3 5.3 %collective-permute-start.1 = (bf16[8,32,1536]{2,1,0:T(8,128)(2,1)S(1)}, bf16[8,32,1536]{2,1,0:T(8,128)(2,1)S(1)}, u32[]{:S(2)}, u32[]{:S(2)}) collective-permute-start(bf16[8,32,1536]{2,1,0:T(8,128)(2,1)S(1)} %fusion.21), channel_id=1, source_target_pairs={{0,8},{8,0},{1,9},{9,1},{2,10},{10,2},{3,11},{11,3},{4,12},{12,4},... | collective-permute-start | bytes 2359304 | tf_op jit(solution)/shard_map/ppermute | solution.py:37
  173.3 4.2 collective-permute-start.2
  207.7 4.6 %copy-start.4 = (f32[768]{0:T(1024)S(1)}, f32[768]{0:T(1024)}, u32[]{:S(2)}) copy-start(f32[768]{0:T(1024)} %param.24) | copy-start | bytes 9220
  207.7 4.6 %copy-start.5 = (f32[768]{0:T(1024)S(1)}, f32[768]{0:T(1024)}, u32[]{:S(2)}) copy-start(f32[768]{0:T(1024)} %param.25) | copy-start | bytes 9220
  207.7 23.0 %all-to-all-start.6 = ((f32[8,64,768]{2,1,0:T(8,128)}), f32[8,64,768]{2,1,0:T(8,128)}, u32[]{:S(2)}, u32[]{:S(2)}) async-start(f32[8,64,768]{2,1,0:T(8,128)} %broadcast_in_dim.29), calls=%async_computation.6 | async-start | bytes 3145728 | tf_op jit(solution)/shard_map/all_to_all | solution.py:23
  235.4 1.4 copy-start.3
  237.0 6.5 %collective-permute-start.3 = (f32[8,32,1536]{2,1,0:T(8,128)S(1)}, f32[8,32,1536]{2,1,0:T(8,128)S(1)}, u32[]{:S(2)}, u32[]{:S(2)}) collective-permute-start(f32[8,32,1536]{2,1,0:T(8,128)S(1)} %select_bitcast_fusion.1), channel_id=1, source_target_pairs={{0,8},{8,0},{1,9},{9,1},{2,10},{10,2},{3,11},{11,3},{4,12},{12,4},... | collective-permute-start | bytes 4718600 | tf_op jit(solution)/shard_map/ppermute | solution.py:37
  290.1 5.3 %collective-permute-start.4 = (f32[8,32,1536]{2,1,0:T(8,128)S(1)}, f32[8,32,1536]{2,1,0:T(8,128)S(1)}, u32[]{:S(2)}, u32[]{:S(2)}) collective-permute-start(f32[8,32,1536]{2,1,0:T(8,128)S(1)} %all_to_all.65), channel_id=1, source_target_pairs={{0,8},{8,0},{1,9},{9,1},{2,10},{10,2},{3,11},{11,3},{4,12},{12,4},... | collective-permute-start | bytes 4718600 | tf_op jit(solution)/shard_map/ppermute | solution.py:37
  301.5 25.0 %all-to-all-start.9 = ((f32[8,64,768]{2,1,0:T(8,128)}), f32[8,64,768]{2,1,0:T(8,128)S(1)}, u32[]{:S(2)}, u32[]{:S(2)}) async-start(f32[8,64,768]{2,1,0:T(8,128)} %fusion.10), calls=%async_computation.9 | async-start | bytes 3145728 | tf_op jit(solution)/shard_map/all_to_all | solution.py:16
  352.2 10.1 %collective-permute-start.5 = (f32[8,32,4608]{2,1,0:T(8,128)S(1)}, f32[8,32,4608]{2,1,0:T(8,128)S(1)}, u32[]{:S(2)}, u32[]{:S(2)}) collective-permute-start(f32[8,32,4608]{2,1,0:T(8,128)S(1)} %select_bitcast_fusion), channel_id=1, source_target_pairs={{0,8},{8,0},{1,9},{9,1},{2,10},{10,2},{3,11},{11,3},{4,12},{12,4},... | collective-permute-start | bytes 14155784 | tf_op jit(solution)/shard_map/ppermute | solution.py:37
  365.6 4.7 %copy-start.9 = (f32[32]{0:T(128)S(1)}, f32[32]{0:T(128)}, u32[]{:S(2)}) copy-start(f32[32]{0:T(128)} %param.21) | copy-start | bytes 388
  365.6 4.8 %copy-start.10 = (f32[32]{0:T(128)S(1)}, f32[32]{0:T(128)}, u32[]{:S(2)}) copy-start(f32[32]{0:T(128)} %param.20) | copy-start | bytes 388
  365.6 59.5 %all-to-all-start.11 = ((f32[8,32,4608]{2,1,0:T(8,128)}), f32[8,32,4608]{2,1,0:T(8,128)}, u32[]{:S(2)}, u32[]{:S(2)}) async-start(f32[8,32,4608]{2,1,0:T(8,128)} %fusion.7), calls=%async_computation.11 | async-start | bytes 9437184 | tf_op jit(solution)/shard_map/all_to_all | solution.py:49
  370.3 57.6 %copy-start.8 = (f32[32]{0:T(128)}, f32[32]{0:T(128)S(1)}, u32[]{:S(2)}) copy-start(f32[32]{0:T(128)S(1)} %multiply_add_fusion) | copy-start | bytes 388
  370.4 57.6 %copy-start.2 = (f32[32,4608]{1,0:T(8,128)S(1)}, f32[32,4608]{1,0:T(8,128)}, u32[]{:S(2)}) copy-start(f32[32,4608]{1,0:T(8,128)} %param.16) | copy-start | bytes 1769476
  425.1 4.5 %copy-start.1 = (bf16[768,1536]{1,0:T(8,128)(2,1)S(1)}, bf16[768,1536]{1,0:T(8,128)(2,1)}, u32[]{:S(2)}) copy-start(bf16[768,1536]{1,0:T(8,128)(2,1)} %param.15) | copy-start | bytes 7077892
Sparse Core Ops, SparseCore 0:
  10.2 57.9 all-gather.1

commit v13 on v12

--- a/solution.py
+++ b/solution.py
@@ -149,7 +149,15 @@
     base_block = lax.dynamic_slice_in_dim(base_new, first_row, block_rows, axis=0)
     post_block = lax.dynamic_slice_in_dim(post_new, first_row, block_rows, axis=0)
     line_total = gathered_rows((base_block + post_block + returned).astype(jnp.bfloat16), "col")
-    prices = line_summed_block(jnp.dot(line_total, ptdf, preferred_element_type=jnp.float32))
+    outer_devs = lax.axis_size(LINE_OUTER)
+    core_now = lax.axis_index(LINE_CORE)
+    by_core = line_total.reshape(outer_devs, 2, line_total.shape[0] // (2 * outer_devs), line_total.shape[1])
+    keep_rows = jnp.where(core_now == 0, by_core[:, 0], by_core[:, 1])
+    give_rows = jnp.where(core_now == 0, by_core[:, 1], by_core[:, 0])
+    given = swap_cores(jnp.dot(give_rows, ptdf, preferred_element_type=jnp.float32))
+    kept = lax.optimization_barrier(jnp.dot(keep_rows, ptdf, preferred_element_type=jnp.float32))
+    pair_sum = kept + given
+    prices = lax.all_to_all(pair_sum, LINE_OUTER, 0, 0, tiled=True).sum(axis=0, dtype=jnp.float32)
     moved = injection - primal_step * (bus_cost[None, :] + prices + balance_new[:, None])
     new_injection = jnp.clip(moved, 0.0, bus_cap[None, :])
     return (new_injection, balance_new, base_new, post_new)
@@ -177,6 +185,5 @@
         P("col"),
     )
     out_specs = (P(LINE, "col"), P(LINE), P(None, LINE), P(None, LINE))
-    return jax.shard_map(
-        on_device, mesh=fine, in_specs=in_specs, out_specs=out_specs, check_vma=False
-    )
+
+    return jax.shard_map(on_device, mesh=fine, in_specs=in_specs, out_specs=out_specs, check_vma=False)

time: 438 us -> 436 us (level)
  no operation moved by 1% of the time
where the time goes in v13:
time: 436 us; the launch traced here: 435 us
  blocking collectives  180 us (41%)
  waiting for transfers between devices  128 us (29%)
  starting transfers between devices  45.7 us (10%)
  matrix products  41.9 us (10%)
  other arithmetic  20.8 us (5%)
  between operations  14.4 us (3%)
    all_to_all x1, waiting for transfers between devices, on_device(): lax.all_to_all(pair_sum, LINE_OUTER, 0, 0, tiled=True)  54.8 us
    all_to_all x2, blocking collectives, summed_block(): lax.all_to_all(value.reshape(n, rows, *value.shape[1:]), axis, 0, 0, tile...  53.4 us
    all_to_all x2, blocking collectives, line_summed_block(): parts = lax.all_to_all(pair_sum, LINE_OUTER, 0, 0, tiled=True)  39.5 us
    all_to_all x2, blocking collectives, line_gathered_rows(): mine = lax.all_to_all(copies, LINE_OUTER, 0, 0, tiled=True)  36.9 us
    all_to_all x2, waiting for transfers between devices, gathered_rows(): whole = lax.all_to_all(copies, axis, 0, 0, tiled=True)  36.8 us
    psum x1, blocking collectives, on_device(): bus_total = lax.psum(local_total, 'col')  32.3 us
    dot_general x3, matrix products, flows(): product = jnp.dot(flat, ptdf_turned, preferred_element_type=jnp.float32)  21 us
    ppermute x6, starting transfers between devices, swap_cores(): return lax.ppermute(value, LINE_CORE, [(0, 1), (1, 0)])  20.7 us
  transfers between devices with their start and end apart: 12, of which 10 were waited for; matrix products, arithmetic and copies ran while one was open for 3% of the time, Pallas kernels for 0%

profile of v13, /device:TPU:1, one launch (start us, length us, event | category | flops | bytes accessed | tf_op | source)
XLA Modules:
  0.0 434.8 jit_solution(6765569381494954391)
XLA Ops:
  7.2 1.6 fusion.27
  9.7 1.1 broadcast_in_dim.24
  10.8 6.8 %all-to-all-start = ((bf16[8,2,8,4608]{3,2,1,0:T(8,128)(2,1)}), bf16[8,2,8,4608]{3,2,1,0:T(8,128)(2,1)S(1)}, u32[]{:S(2)}, u32[]{:S(2)}) async-start(bf16[8,2,8,4608]{3,2,1,0:T(8,128)(2,1)} %broadcast_in_dim.24), calls=%async_computation | async-start | bytes 2359296 | tf_op jit(solution)/shard_map/all_to_all | solution.py:112
  17.6 32.3 %psum.7 = f32[32]{0:T(128)S(1)} all-reduce(f32[32]{0:T(128)S(1)} %get-tuple-element.12), channel_id=1, replica_groups=mesh['line_outer'=8,'line_core'=2,'col'=8] {'col'}, use_global_device_ids=true, to_apply=%region_1.0 | all-reduce | flops 32 | bytes 256 | tf_op jit(solution)/shard_map/psum | solution.py:108
  49.9 6.9 %collective-permute-start = (bf16[8,2,8,4608]{3,2,1,0:T(8,128)(2,1)S(1)}, bf16[8,2,8,4608]{3,2,1,0:T(8,128)(2,1)S(1)}, u32[]{:S(2)}, u32[]{:S(2)}) collective-permute-start(bf16[8,2,8,4608]{3,2,1,0:T(8,128)(2,1)S(1)} %all-to-all-done), channel_id=1, source_target_pairs={{0,8},{8,0},{1,9},{9,1},{2,10},{10,2},{3,11},{11,3},{4,12},{12,4},... | collective-permute-start | bytes 3538952 | tf_op jit(solution)/shard_map/ppermute | solution.py:37
  56.7 5.6 %fusion.6 = f32[8,2,8,768]{3,2,1,0:T(8,128)S(1)} fusion(bf16[8,2,8,4608]{3,2,1,0:T(8,128)(2,1)S(1)} %all-to-all-done, bf16[768,4608]{1,0:T(8,128)(2,1)} %param.14), kind=kOutput, calls=%fused_computation.6 | convolution fusion | flops 905969664 | bytes 8650752 | tf_op jit(solution)/shard_map/dot_general | solution.py:103
  62.3 5.5 %fusion.4 = f32[8,2,8,768]{3,2,1,0:T(8,128)S(1)} fusion(bf16[8,2,8,4608]{3,2,1,0:T(8,128)(2,1)S(1)} %collective-permute-done, bf16[768,4608]{1,0:T(8,128)(2,1)} %param.14), kind=kOutput, calls=%fused_computation.4 | convolution fusion | flops 905969664 | bytes 8650752 | tf_op jit(solution)/shard_map/dot_general | solution.py:103
  68.3 10.0 %fusion.40 = f32[768,768]{1,0:T(8,128)S(1)} fusion(bf16[768,4608]{1,0:T(8,128)(2,1)} %bitcast.113, bf16[768,4608]{1,0:T(8,128)(2,1)} %param.14), kind=kOutput, calls=%fused_computation.69 | convolution fusion | flops 5435817984 | bytes 16515072 | tf_op jit(solution)/shard_map/dot_general | solution.py:103
  78.5 27.5 %all_to_all.60 = f32[8,64,768]{2,1,0:T(8,128)} all-to-all(f32[8,64,768]{2,1,0:T(8,128)S(1)} %bitcast.101), channel_id=1, replica_groups=mesh['line_outer'=8,'line_core'=2,'col'=8] {'col'}, dimensions={0} | all-to-all | bytes 3145728 | tf_op jit(solution)/shard_map/all_to_all | solution.py:16
  106.1 1.5 reduce_sum.64
  107.6 1.3 broadcast_in_dim.25
  108.8 4.4 %all-to-all-start.2 = ((f32[8,64,768]{2,1,0:T(8,128)}), f32[8,64,768]{2,1,0:T(8,128)}, u32[]{:S(2)}, u32[]{:S(2)}) async-start(f32[8,64,768]{2,1,0:T(8,128)} %broadcast_in_dim.25), calls=%async_computation.2 | async-start | bytes 3145728 | tf_op jit(solution)/shard_map/all_to_all | solution.py:23
  113.3 18.4 %all-to-all-done.2 = f32[8,64,768]{2,1,0:T(8,128)} async-done(((f32[8,64,768]{2,1,0:T(8,128)}), f32[8,64,768]{2,1,0:T(8,128)}, u32[]{:S(2)}, u32[]{:S(2)}) %all-to-all-start.2) | async-done | bytes 1572896 | tf_op jit(solution)/shard_map/all_to_all | solution.py:23
  131.8 5.4 %fusion.14 = bf16[512,1536]{1,0:T(8,128)(2,1)S(1)} fusion(f32[512,768]{1,0:T(8,128)} %bitcast.9, s32[1536]{0:T(1024)S(1)} %get-tuple-element.9, f32[1536]{0:T(1024)S(1)} %copy-done.6, pred[1536]{0:T(1024)(128)(4,1)S(1)} %get-tuple-element.8), kind=kOutput, calls=%fused_computation.16 | convolution fusion | flops 7251296256 | bytes 3159552 | tf_op jit(solution)/shard_map/dot_general | solution.py:130
  137.3 3.3 collective-permute-start.1
  140.6 1.9 collective-permute-done.1
  142.7 16.0 %all_to_all.61 = bf16[8,32,1536]{2,1,0:T(8,128)(2,1)S(1)} all-to-all(bf16[8,32,1536]{2,1,0:T(8,128)(2,1)S(1)} %fusion.23), channel_id=1, replica_groups=mesh['line_outer'=8,'line_core'=2,'col'=8] {'line_outer'}, dimensions={0} | all-to-all | bytes 1572864 | tf_op jit(solution)/shard_map/all_to_all | solution.py:49
  158.9 14.4 %all_to_all.62 = bf16[8,32,1536]{2,1,0:T(8,128)(2,1)S(1)} all-to-all(bf16[8,32,1536]{2,1,0:T(8,128)(2,1)S(1)} %broadcast_in_dim.28), channel_id=1, replica_groups=mesh['line_outer'=8,'line_core'=2,'col'=8] {'line_outer'}, dimensions={0} | all-to-all | bytes 1572864 | tf_op jit(solution)/shard_map/all_to_all | solution.py:57
  173.3 2.3 collective-permute-start.2
  175.6 1.9 collective-permute-done.2
  177.7 1.4 fusion.15
  179.1 25.8 %all_to_all.63 = f32[8,64,768]{2,1,0:T(8,128)} all-to-all(f32[8,64,768]{2,1,0:T(8,128)S(1)} %fusion.15), channel_id=1, replica_groups=mesh['line_outer'=8,'line_core'=2,'col'=8] {'col'}, dimensions={0} | all-to-all | bytes 3145728 | tf_op jit(solution)/shard_map/all_to_all | solution.py:16
  204.9 1.5 reduce_sum.66
  206.4 1.3 broadcast_in_dim.29
  207.7 4.6 %all-to-all-start.6 = ((f32[8,64,768]{2,1,0:T(8,128)}), f32[8,64,768]{2,1,0:T(8,128)}, u32[]{:S(2)}, u32[]{:S(2)}) async-start(f32[8,64,768]{2,1,0:T(8,128)} %broadcast_in_dim.29), calls=%async_computation.6 | async-start | bytes 3145728 | tf_op jit(solution)/shard_map/all_to_all | solution.py:23
  212.4 18.3 %all-to-all-done.6 = f32[8,64,768]{2,1,0:T(8,128)} async-done(((f32[8,64,768]{2,1,0:T(8,128)}), f32[8,64,768]{2,1,0:T(8,128)}, u32[]{:S(2)}, u32[]{:S(2)}) %all-to-all-start.6) | async-done | bytes 1572896 | tf_op jit(solution)/shard_map/all_to_all | solution.py:23
  230.7 4.7 %multiply_subtract_fusion.1 = (f32[512,768]{1,0:T(8,128)}, f32[512,768]{1,0:T(8,128)S(1)}) fusion(f32[512,768]{1,0:T(8,128)} %param.22, f32[768]{0:T(1024)S(1)} %neg.8, f32[768]{0:T(1024)S(1)} %copy-done.4, f32[8,64,768]{2,1,0:T(8,128)} %all-to-all-done.2, f32[768]{0:T(1024)S(1)} %neg.9, f32[768]{0:T(1024)S(1)} %copy-done.5, f32[512,768]{1,0:T(8,128)} %param.23, ...), kind=kLoop, calls=%fused_computation.31 | loop fusion | flops 5898240 | bytes 9449472 | tf_op jit(solution)/shard_map/sub | solution.py:69
  235.4 1.4 fusion.24
  237.0 3.4 collective-permute-start.3
  240.5 3.0 collective-permute-done.3
  243.9 23.5 %all_to_all.64 = f32[8,32,1536]{2,1,0:T(8,128)S(1)} all-to-all(f32[8,32,1536]{2,1,0:T(8,128)S(1)} %bitcast_add_fusion), channel_id=1, replica_groups=mesh['line_outer'=8,'line_core'=2,'col'=8] {'line_outer'}, dimensions={0} | all-to-all | bytes 3145728 | tf_op jit(solution)/shard_map/all_to_all | solution.py:49
  267.7 22.5 %all_to_all.65 = f32[8,32,1536]{2,1,0:T(8,128)S(1)} all-to-all(f32[8,32,1536]{2,1,0:T(8,128)S(1)} %broadcast_in_dim.30), channel_id=1, replica_groups=mesh['line_outer'=8,'line_core'=2,'col'=8] {'line_outer'}, dimensions={0} | all-to-all | bytes 3145728 | tf_op jit(solution)/shard_map/all_to_all | solution.py:57
  290.1 2.2 collective-permute-start.4
  292.4 3.0 collective-permute-done.4
  296.1 5.5 %fusion.10 = f32[8,64,768]{2,1,0:T(8,128)} fusion(f32[8,64,1536]{2,1,0:T(8,128)S(1)} %bitcast_multiply_fusion, s32[1536]{0:T(1024)S(1)} %get-tuple-element.9), kind=kOutput, calls=%fused_computation.11 | convolution fusion | flops 7248936960 | bytes 4724736 | tf_op jit(solution)/shard_map/dot_general | solution.py:139
  301.6 4.4 %all-to-all-start.9 = ((f32[8,64,768]{2,1,0:T(8,128)}), f32[8,64,768]{2,1,0:T(8,128)S(1)}, u32[]{:S(2)}, u32[]{:S(2)}) async-start(f32[8,64,768]{2,1,0:T(8,128)} %fusion.10), calls=%async_computation.9 | async-start | bytes 3145728 | tf_op jit(solution)/shard_map/all_to_all | solution.py:16
  306.0 20.6 %all-to-all-done.9 = f32[8,64,768]{2,1,0:T(8,128)S(1)} async-done(((f32[8,64,768]{2,1,0:T(8,128)}), f32[8,64,768]{2,1,0:T(8,128)S(1)}, u32[]{:S(2)}, u32[]{:S(2)}) %all-to-all-start.9) | async-done | bytes 1572896 | tf_op jit(solution)/shard_map/all_to_all | solution.py:16
  326.6 1.1 add_convert_fusion
  327.8 18.1 %all_to_all.66 = bf16[8,64,768]{2,1,0:T(8,128)(2,1)S(1)} all-to-all(bf16[8,64,768]{2,1,0:T(8,128)(2,1)S(1)} %broadcast_in_dim.31), channel_id=1, replica_groups=mesh['line_outer'=8,'line_core'=2,'col'=8] {'col'}, dimensions={0} | all-to-all | bytes 1572864 | tf_op jit(solution)/shard_map/all_to_all | solution.py:23
  345.8 5.2 %fusion = f32[8,32,4608]{2,1,0:T(8,128)S(1)} fusion(bf16[768,4608]{1,0:T(8,128)(2,1)} %param.14, pred[]{:T(512)S(6)} %eq.6, bf16[8,2,32,768]{3,2,1,0:T(8,128)(2,1)S(1)} %bitcast.106), kind=kOutput, calls=%fused_computation | convolution fusion | flops 1812135936 | bytes 12582913 | tf_op jit(solution)/shard_map/dot_general | solution.py:157
  351.0 2.5 collective-permute-start.5
  353.5 2.0 fusion.2
  355.6 5.5 %collective-permute-done.5 = f32[8,32,4608]{2,1,0:T(8,128)S(1)} collective-permute-done((f32[8,32,4608]{2,1,0:T(8,128)S(1)}, f32[8,32,4608]{2,1,0:T(8,128)S(1)}, u32[]{:S(2)}, u32[]{:S(2)}) %collective-permute-start.5) | collective-permute-done | bytes 4718624 | tf_op jit(solution)/shard_map/ppermute | solution.py:37
  361.1 2.8 add.85
  363.9 4.7 %all-to-all-start.11 = ((f32[8,32,4608]{2,1,0:T(8,128)}), f32[8,32,4608]{2,1,0:T(8,128)}, u32[]{:S(2)}, u32[]{:S(2)}) async-start(f32[8,32,4608]{2,1,0:T(8,128)} %add.85), calls=%async_computation.11 | async-start | bytes 9437184 | tf_op jit(solution)/shard_map/all_to_all | solution.py:160
  368.6 54.8 %all-to-all-done.11 = f32[8,32,4608]{2,1,0:T(8,128)} async-done(((f32[8,32,4608]{2,1,0:T(8,128)}), f32[8,32,4608]{2,1,0:T(8,128)}, u32[]{:S(2)}, u32[]{:S(2)}) %all-to-all-start.11) | async-done | bytes 4718624 | tf_op jit(solution)/shard_map/all_to_all | solution.py:160
  423.4 2.8 reduce_sum.69
  426.2 1.7 maximum_minimum_fusion
  (56 shorter events, 3.9 us)
Async XLA Ops:
  7.2 170.5 %copy-start = (bf16[768,1536]{1,0:T(8,128)(2,1)S(1)}, bf16[768,1536]{1,0:T(8,128)(2,1)}, u32[]{:S(2)}) copy-start(bf16[768,1536]{1,0:T(8,128)(2,1)} %param.15) | copy-start | bytes 7077892
  7.2 61.1 %all-gather.2.cloned.1.call-start = ((), (), s32[]{:S(2)}) async-start(), calls=%async_computation.12 | async-start | bytes 7520256 | tf_op jit(solution)/shard_map/all_gather | solution.py:109
  10.8 39.1 %all-to-all-start = ((bf16[8,2,8,4608]{3,2,1,0:T(8,128)(2,1)}), bf16[8,2,8,4608]{3,2,1,0:T(8,128)(2,1)S(1)}, u32[]{:S(2)}, u32[]{:S(2)}) async-start(bf16[8,2,8,4608]{3,2,1,0:T(8,128)(2,1)} %broadcast_in_dim.24), calls=%async_computation | async-start | bytes 2359296 | tf_op jit(solution)/shard_map/all_to_all | solution.py:112
  49.9 12.5 %collective-permute-start = (bf16[8,2,8,4608]{3,2,1,0:T(8,128)(2,1)S(1)}, bf16[8,2,8,4608]{3,2,1,0:T(8,128)(2,1)S(1)}, u32[]{:S(2)}, u32[]{:S(2)}) collective-permute-start(bf16[8,2,8,4608]{3,2,1,0:T(8,128)(2,1)S(1)} %all-to-all-done), channel_id=1, source_target_pairs={{0,8},{8,0},{1,9},{9,1},{2,10},{10,2},{3,11},{11,3},{4,12},{12,4},... | collective-permute-start | bytes 3538952 | tf_op jit(solution)/shard_map/ppermute | solution.py:37
  108.8 4.5 %copy-start.7 = (s32[1536]{0:T(1024)S(1)}, s32[1536]{0:T(1024)}, u32[]{:S(2)}) copy-start(s32[1536]{0:T(1024)} %param.26) | copy-start | bytes 18436
  108.8 22.9 %copy-start.6 = (f32[1536]{0:T(1024)S(1)}, f32[1536]{0:T(1024)}, u32[]{:S(2)}) copy-start(f32[1536]{0:T(1024)} %param.27) | copy-start | bytes 18436
  108.8 22.9 %all-to-all-start.2 = ((f32[8,64,768]{2,1,0:T(8,128)}), f32[8,64,768]{2,1,0:T(8,128)}, u32[]{:S(2)}, u32[]{:S(2)}) async-start(f32[8,64,768]{2,1,0:T(8,128)} %broadcast_in_dim.25), calls=%async_computation.2 | async-start | bytes 3145728 | tf_op jit(solution)/shard_map/all_to_all | solution.py:23
  137.3 5.3 %collective-permute-start.1 = (bf16[8,32,1536]{2,1,0:T(8,128)(2,1)S(1)}, bf16[8,32,1536]{2,1,0:T(8,128)(2,1)S(1)}, u32[]{:S(2)}, u32[]{:S(2)}) collective-permute-start(bf16[8,32,1536]{2,1,0:T(8,128)(2,1)S(1)} %fusion.21), channel_id=1, source_target_pairs={{0,8},{8,0},{1,9},{9,1},{2,10},{10,2},{3,11},{11,3},{4,12},{12,4},... | collective-permute-start | bytes 2359304 | tf_op jit(solution)/shard_map/ppermute | solution.py:37
  173.3 4.2 collective-permute-start.2
  207.7 4.6 %copy-start.4 = (f32[768]{0:T(1024)S(1)}, f32[768]{0:T(1024)}, u32[]{:S(2)}) copy-start(f32[768]{0:T(1024)} %param.24) | copy-start | bytes 9220
  207.7 4.6 %copy-start.5 = (f32[768]{0:T(1024)S(1)}, f32[768]{0:T(1024)}, u32[]{:S(2)}) copy-start(f32[768]{0:T(1024)} %param.25) | copy-start | bytes 9220
  207.7 23.0 %all-to-all-start.6 = ((f32[8,64,768]{2,1,0:T(8,128)}), f32[8,64,768]{2,1,0:T(8,128)}, u32[]{:S(2)}, u32[]{:S(2)}) async-start(f32[8,64,768]{2,1,0:T(8,128)} %broadcast_in_dim.29), calls=%async_computation.6 | async-start | bytes 3145728 | tf_op jit(solution)/shard_map/all_to_all | solution.py:23
  235.4 1.4 copy-start.3
  237.0 6.5 %collective-permute-start.3 = (f32[8,32,1536]{2,1,0:T(8,128)S(1)}, f32[8,32,1536]{2,1,0:T(8,128)S(1)}, u32[]{:S(2)}, u32[]{:S(2)}) collective-permute-start(f32[8,32,1536]{2,1,0:T(8,128)S(1)} %select_bitcast_fusion), channel_id=1, source_target_pairs={{0,8},{8,0},{1,9},{9,1},{2,10},{10,2},{3,11},{11,3},{4,12},{12,4},... | collective-permute-start | bytes 4718600 | tf_op jit(solution)/shard_map/ppermute | solution.py:37
  290.1 5.3 %collective-permute-start.4 = (f32[8,32,1536]{2,1,0:T(8,128)S(1)}, f32[8,32,1536]{2,1,0:T(8,128)S(1)}, u32[]{:S(2)}, u32[]{:S(2)}) collective-permute-start(f32[8,32,1536]{2,1,0:T(8,128)S(1)} %all_to_all.65), channel_id=1, source_target_pairs={{0,8},{8,0},{1,9},{9,1},{2,10},{10,2},{3,11},{11,3},{4,12},{12,4},... | collective-permute-start | bytes 4718600 | tf_op jit(solution)/shard_map/ppermute | solution.py:37
  301.6 25.0 %all-to-all-start.9 = ((f32[8,64,768]{2,1,0:T(8,128)}), f32[8,64,768]{2,1,0:T(8,128)S(1)}, u32[]{:S(2)}, u32[]{:S(2)}) async-start(f32[8,64,768]{2,1,0:T(8,128)} %fusion.10), calls=%async_computation.9 | async-start | bytes 3145728 | tf_op jit(solution)/shard_map/all_to_all | solution.py:16
  327.7 25.8 %slice-start = ((s8[7077888]{0:T(1024)(128)(4,1)}), s8[4194304]{0:T(1024)(128)(4,1)S(1)}, s32[]{:S(2)}) async-start(s8[7077888]{0:T(1024)(128)(4,1)} %bitcast.97), calls=%async_computation.13 | async-start | bytes 8388608
  345.8 7.7 %slice-start.1 = ((s8[7077888]{0:T(1024)(128)(4,1)}), s8[2883584]{0:T(1024)(128)(4,1)S(1)}, s32[]{:S(2)}) async-start(s8[7077888]{0:T(1024)(128)(4,1)} %bitcast.97), calls=%async_computation.14 | async-start | bytes 5767168
  351.0 10.1 %collective-permute-start.5 = (f32[8,32,4608]{2,1,0:T(8,128)S(1)}, f32[8,32,4608]{2,1,0:T(8,128)S(1)}, u32[]{:S(2)}, u32[]{:S(2)}) collective-permute-start(f32[8,32,4608]{2,1,0:T(8,128)S(1)} %fusion), channel_id=1, source_target_pairs={{0,8},{8,0},{1,9},{9,1},{2,10},{10,2},{3,11},{11,3},{4,12},{12,4},... | collective-permute-start | bytes 14155784 | tf_op jit(solution)/shard_map/ppermute | solution.py:37
  363.9 4.7 %copy-start.9 = (f32[32]{0:T(128)S(1)}, f32[32]{0:T(128)}, u32[]{:S(2)}) copy-start(f32[32]{0:T(128)} %param.21) | copy-start | bytes 388
  363.9 4.7 %copy-start.10 = (f32[32]{0:T(128)S(1)}, f32[32]{0:T(128)}, u32[]{:S(2)}) copy-start(f32[32]{0:T(128)} %param.20) | copy-start | bytes 388
  363.9 59.5 %all-to-all-start.11 = ((f32[8,32,4608]{2,1,0:T(8,128)}), f32[8,32,4608]{2,1,0:T(8,128)}, u32[]{:S(2)}, u32[]{:S(2)}) async-start(f32[8,32,4608]{2,1,0:T(8,128)} %add.85), calls=%async_computation.11 | async-start | bytes 9437184 | tf_op jit(solution)/shard_map/all_to_all | solution.py:160
  368.6 57.6 %copy-start.8 = (f32[32]{0:T(128)}, f32[32]{0:T(128)S(1)}, u32[]{:S(2)}) copy-start(f32[32]{0:T(128)S(1)} %multiply_add_fusion) | copy-start | bytes 388
  368.6 57.6 %copy-start.2 = (f32[32,4608]{1,0:T(8,128)S(1)}, f32[32,4608]{1,0:T(8,128)}, u32[]{:S(2)}) copy-start(f32[32,4608]{1,0:T(8,128)} %param.16) | copy-start | bytes 1769476
  423.4 4.5 %copy-start.1 = (bf16[768,1536]{1,0:T(8,128)(2,1)S(1)}, bf16[768,1536]{1,0:T(8,128)(2,1)}, u32[]{:S(2)}) copy-start(bf16[768,1536]{1,0:T(8,128)(2,1)} %param.15) | copy-start | bytes 7077892
Sparse Core Ops, SparseCore 0:
  10.2 57.9 all-gather.1

commit v14 on v13

--- a/solution.py
+++ b/solution.py
@@ -127,9 +127,20 @@
     lines_seen = lax.broadcasted_iota(jnp.int32, (lines_dev, outage_line.shape[0]), 0)
     chosen = (lines_seen == local_line[None, :]).astype(jnp.float32)
     exact = lax.Precision.HIGHEST
-    picked = jnp.dot(base_flow, chosen, precision=exact, preferred_element_type=jnp.float32)
-    weighted = jnp.where(inside[None, :], picked * outage_weight[None, :], 0.0)
-    outage_flow = line_full_sum(weighted.astype(jnp.bfloat16))
+    outer_devs = lax.axis_size(LINE_OUTER)
+    core_now = lax.axis_index(LINE_CORE)
+    flow_by_core = base_flow.reshape(outer_devs, 2, base_flow.shape[0] // (2 * outer_devs), lines_dev)
+
+    def weighted(flow_rows):
+        picked = jnp.dot(flow_rows, chosen, precision=exact, preferred_element_type=jnp.float32)
+        return jnp.where(inside, picked * outage_weight, 0.0).astype(jnp.bfloat16)
+
+    given_out = swap_cores(weighted(jnp.where(core_now == 0, flow_by_core[:, 1], flow_by_core[:, 0])))
+    kept_out = lax.optimization_barrier(
+        weighted(jnp.where(core_now == 0, flow_by_core[:, 0], flow_by_core[:, 1]))
+    )
+    outage_parts = lax.all_to_all(kept_out + given_out, LINE_OUTER, 0, 0, tiled=True)
+    outage_flow = line_gathered_rows(outage_parts.sum(axis=0, dtype=jnp.bfloat16))
     shift_part = jnp.dot(outage_flow, lodf.T, preferred_element_type=jnp.float32)
     post_shift = full_sum(shift_part, "col")
     post_flow = base_flow + post_shift

time: 436 us -> 435 us (level)
  waiting for transfers between devices: 128 us -> 123 us
    all_to_all x0 -> x1, blocking collectives: none -> 16.7 us  [on_device(): lax.all_to_all(kept_out + given_out, LINE_OUTER, 0, 0, tiled=True)]
    all_to_all x2 -> x1, blocking collectives: 39.5 us -> 23.5 us  [line_summed_block(): parts = lax.all_to_all(pair_sum, LINE_OUTER, 0, 0, tiled=True)]
  transfers between devices with their start and end apart: 12 -> 12, of which waited for: 10 -> 9; matrix products, arithmetic and copies ran while one was open for 3% -> 5% of each run, Pallas kernels for 0% -> 0%
where the time goes in v14:
time: 435 us; the launch traced here: 434 us
  blocking collectives  180 us (41%)
  waiting for transfers between devices  123 us (28%)
  starting transfers between devices  45.7 us (11%)
  matrix products  43.9 us (10%)
  other arithmetic  23.1 us (5%)
  between operations  14.4 us (3%)
    all_to_all x1, waiting for transfers between devices, on_device(): lax.all_to_all(pair_sum, LINE_OUTER, 0, 0, tiled=True)  54.8 us
    all_to_all x2, blocking collectives, summed_block(): lax.all_to_all(value.reshape(n, rows, *value.shape[1:]), axis, 0, 0, tile...  53.4 us
    all_to_all x2, waiting for transfers between devices, gathered_rows(): whole = lax.all_to_all(copies, axis, 0, 0, tiled=True)  36.8 us
    all_to_all x2, blocking collectives, line_gathered_rows(): mine = lax.all_to_all(copies, LINE_OUTER, 0, 0, tiled=True)  36.6 us
    psum x1, blocking collectives, on_device(): bus_total = lax.psum(local_total, 'col')  32.3 us
    all_to_all x1, blocking collectives, line_summed_block(): parts = lax.all_to_all(pair_sum, LINE_OUTER, 0, 0, tiled=True)  23.5 us
    dot_general x3, matrix products, flows(): product = jnp.dot(flat, ptdf_turned, preferred_element_type=jnp.float32)  21 us
    ppermute x6, starting transfers between devices, swap_cores(): return lax.ppermute(value, LINE_CORE, [(0, 1), (1, 0)])  20.8 us
  transfers between devices with their start and end apart: 12, of which 9 were waited for; matrix products, arithmetic and copies ran while one was open for 5% of the time, Pallas kernels for 0%

profile of v14, /device:TPU:1, one launch (start us, length us, event | category | flops | bytes accessed | tf_op | source)
XLA Modules:
  0.0 434.3 jit_solution(16260017325776919500)
XLA Ops:
  7.2 1.6 fusion.51
  9.7 1.1 broadcast_in_dim.22
  10.8 6.8 %all-to-all-start = ((bf16[8,2,8,4608]{3,2,1,0:T(8,128)(2,1)}), bf16[8,2,8,4608]{3,2,1,0:T(8,128)(2,1)S(1)}, u32[]{:S(2)}, u32[]{:S(2)}) async-start(bf16[8,2,8,4608]{3,2,1,0:T(8,128)(2,1)} %broadcast_in_dim.22), calls=%async_computation | async-start | bytes 2359296 | tf_op jit(solution)/shard_map/all_to_all | solution.py:112
  17.6 32.3 %psum.7 = f32[32]{0:T(128)S(1)} all-reduce(f32[32]{0:T(128)S(1)} %get-tuple-element.12), channel_id=1, replica_groups=mesh['line_outer'=8,'line_core'=2,'col'=8] {'col'}, use_global_device_ids=true, to_apply=%region_1.0 | all-reduce | flops 32 | bytes 256 | tf_op jit(solution)/shard_map/psum | solution.py:108
  49.9 6.9 %collective-permute-start = (bf16[8,2,8,4608]{3,2,1,0:T(8,128)(2,1)S(1)}, bf16[8,2,8,4608]{3,2,1,0:T(8,128)(2,1)S(1)}, u32[]{:S(2)}, u32[]{:S(2)}) collective-permute-start(bf16[8,2,8,4608]{3,2,1,0:T(8,128)(2,1)S(1)} %all-to-all-done), channel_id=1, source_target_pairs={{0,8},{8,0},{1,9},{9,1},{2,10},{10,2},{3,11},{11,3},{4,12},{12,4},... | collective-permute-start | bytes 3538952 | tf_op jit(solution)/shard_map/ppermute | solution.py:37
  56.7 5.6 %fusion.6 = f32[8,2,8,768]{3,2,1,0:T(8,128)S(1)} fusion(bf16[8,2,8,4608]{3,2,1,0:T(8,128)(2,1)S(1)} %all-to-all-done, bf16[768,4608]{1,0:T(8,128)(2,1)} %param.14), kind=kOutput, calls=%fused_computation.6 | convolution fusion | flops 905969664 | bytes 8650752 | tf_op jit(solution)/shard_map/dot_general | solution.py:103
  62.3 5.5 %fusion.4 = f32[8,2,8,768]{3,2,1,0:T(8,128)S(1)} fusion(bf16[8,2,8,4608]{3,2,1,0:T(8,128)(2,1)S(1)} %collective-permute-done, bf16[768,4608]{1,0:T(8,128)(2,1)} %param.14), kind=kOutput, calls=%fused_computation.4 | convolution fusion | flops 905969664 | bytes 8650752 | tf_op jit(solution)/shard_map/dot_general | solution.py:103
  68.3 10.0 %fusion.66 = f32[768,768]{1,0:T(8,128)S(1)} fusion(bf16[768,4608]{1,0:T(8,128)(2,1)} %bitcast.109, bf16[768,4608]{1,0:T(8,128)(2,1)} %param.14), kind=kOutput, calls=%fused_computation.80 | convolution fusion | flops 5435817984 | bytes 16515072 | tf_op jit(solution)/shard_map/dot_general | solution.py:103
  78.5 27.5 %all_to_all.60 = f32[8,64,768]{2,1,0:T(8,128)} all-to-all(f32[8,64,768]{2,1,0:T(8,128)S(1)} %bitcast.99), channel_id=1, replica_groups=mesh['line_outer'=8,'line_core'=2,'col'=8] {'col'}, dimensions={0} | all-to-all | bytes 3145728 | tf_op jit(solution)/shard_map/all_to_all | solution.py:16
  106.1 1.5 reduce_sum.64
  107.6 1.3 broadcast_in_dim.23
  108.8 4.4 %all-to-all-start.2 = ((f32[8,64,768]{2,1,0:T(8,128)}), f32[8,64,768]{2,1,0:T(8,128)}, u32[]{:S(2)}, u32[]{:S(2)}) async-start(f32[8,64,768]{2,1,0:T(8,128)} %broadcast_in_dim.23), calls=%async_computation.2 | async-start | bytes 3145728 | tf_op jit(solution)/shard_map/all_to_all | solution.py:23
  113.3 18.4 %all-to-all-done.2 = f32[8,64,768]{2,1,0:T(8,128)} async-done(((f32[8,64,768]{2,1,0:T(8,128)}), f32[8,64,768]{2,1,0:T(8,128)}, u32[]{:S(2)}, u32[]{:S(2)}) %all-to-all-start.2) | async-done | bytes 1572896 | tf_op jit(solution)/shard_map/all_to_all | solution.py:23
  131.8 3.7 fusion.27
  135.5 3.3 collective-permute-start.1
  138.9 3.7 fusion.30
  142.8 16.7 %all_to_all.61 = bf16[8,32,1536]{2,1,0:T(8,128)(2,1)S(1)} all-to-all(bf16[8,32,1536]{2,1,0:T(8,128)(2,1)S(1)} %add.80), channel_id=1, replica_groups=mesh['line_outer'=8,'line_core'=2,'col'=8] {'line_outer'}, dimensions={0} | all-to-all | bytes 1572864 | tf_op jit(solution)/shard_map/all_to_all | solution.py:142
  159.7 14.1 %all_to_all.62 = bf16[8,32,1536]{2,1,0:T(8,128)(2,1)S(1)} all-to-all(bf16[8,32,1536]{2,1,0:T(8,128)(2,1)S(1)} %broadcast_in_dim.26), channel_id=1, replica_groups=mesh['line_outer'=8,'line_core'=2,'col'=8] {'line_outer'}, dimensions={0} | all-to-all | bytes 1572864 | tf_op jit(solution)/shard_map/all_to_all | solution.py:57
  173.8 2.1 collective-permute-start.2
  175.9 1.9 collective-permute-done.2
  178.0 1.4 fusion.33
  179.4 25.8 %all_to_all.63 = f32[8,64,768]{2,1,0:T(8,128)} all-to-all(f32[8,64,768]{2,1,0:T(8,128)S(1)} %fusion.33), channel_id=1, replica_groups=mesh['line_outer'=8,'line_core'=2,'col'=8] {'col'}, dimensions={0} | all-to-all | bytes 3145728 | tf_op jit(solution)/shard_map/all_to_all | solution.py:16
  205.2 1.5 reduce_sum.66
  206.8 1.3 broadcast_in_dim.27
  208.0 4.4 %all-to-all-start.6 = ((f32[8,64,768]{2,1,0:T(8,128)}), f32[8,64,768]{2,1,0:T(8,128)}, u32[]{:S(2)}, u32[]{:S(2)}) async-start(f32[8,64,768]{2,1,0:T(8,128)} %broadcast_in_dim.27), calls=%async_computation.6 | async-start | bytes 3145728 | tf_op jit(solution)/shard_map/all_to_all | solution.py:23
  212.5 18.3 %all-to-all-done.6 = f32[8,64,768]{2,1,0:T(8,128)} async-done(((f32[8,64,768]{2,1,0:T(8,128)}), f32[8,64,768]{2,1,0:T(8,128)}, u32[]{:S(2)}, u32[]{:S(2)}) %all-to-all-start.6) | async-done | bytes 1572896 | tf_op jit(solution)/shard_map/all_to_all | solution.py:23
  230.8 3.4 broadcast_multiply_fusion
  234.6 1.4 fusion.42
  236.2 3.5 collective-permute-start.3
  239.7 3.0 collective-permute-done.3
  243.1 23.5 %all_to_all.64 = f32[8,32,1536]{2,1,0:T(8,128)S(1)} all-to-all(f32[8,32,1536]{2,1,0:T(8,128)S(1)} %fusion.39), channel_id=1, replica_groups=mesh['line_outer'=8,'line_core'=2,'col'=8] {'line_outer'}, dimensions={0} | all-to-all | bytes 3145728 | tf_op jit(solution)/shard_map/all_to_all | solution.py:49
  266.8 22.5 %all_to_all.65 = f32[8,32,1536]{2,1,0:T(8,128)S(1)} all-to-all(f32[8,32,1536]{2,1,0:T(8,128)S(1)} %broadcast_in_dim.28), channel_id=1, replica_groups=mesh['line_outer'=8,'line_core'=2,'col'=8] {'line_outer'}, dimensions={0} | all-to-all | bytes 3145728 | tf_op jit(solution)/shard_map/all_to_all | solution.py:57
  289.3 2.2 collective-permute-start.4
  291.5 3.0 collective-permute-done.4
  295.3 5.5 %fusion.9 = f32[8,64,768]{2,1,0:T(8,128)} fusion(f32[8,64,1536]{2,1,0:T(8,128)S(1)} %bitcast_multiply_fusion, s32[1536]{0:T(1024)S(1)} %get-tuple-element.9), kind=kOutput, calls=%fused_computation.10 | convolution fusion | flops 7248936960 | bytes 4724736 | tf_op jit(solution)/shard_map/dot_general | solution.py:150
  300.7 4.5 %all-to-all-start.9 = ((f32[8,64,768]{2,1,0:T(8,128)}), f32[8,64,768]{2,1,0:T(8,128)S(1)}, u32[]{:S(2)}, u32[]{:S(2)}) async-start(f32[8,64,768]{2,1,0:T(8,128)} %fusion.9), calls=%async_computation.9 | async-start | bytes 3145728 | tf_op jit(solution)/shard_map/all_to_all | solution.py:16
  305.3 3.3 multiply_subtract_fusion.1
  308.6 17.2 %all-to-all-done.9 = f32[8,64,768]{2,1,0:T(8,128)S(1)} async-done(((f32[8,64,768]{2,1,0:T(8,128)}), f32[8,64,768]{2,1,0:T(8,128)S(1)}, u32[]{:S(2)}, u32[]{:S(2)}) %all-to-all-start.9) | async-done | bytes 1572896 | tf_op jit(solution)/shard_map/all_to_all | solution.py:16
  327.1 18.1 %all_to_all.66 = bf16[8,64,768]{2,1,0:T(8,128)(2,1)S(1)} all-to-all(bf16[8,64,768]{2,1,0:T(8,128)(2,1)S(1)} %broadcast_in_dim.29), channel_id=1, replica_groups=mesh['line_outer'=8,'line_core'=2,'col'=8] {'col'}, dimensions={0} | all-to-all | bytes 1572864 | tf_op jit(solution)/shard_map/all_to_all | solution.py:23
  345.1 5.2 %fusion = f32[8,32,4608]{2,1,0:T(8,128)S(1)} fusion(bf16[768,4608]{1,0:T(8,128)(2,1)} %param.14, pred[]{:T(512)S(6)} %eq.6, bf16[8,2,32,768]{3,2,1,0:T(8,128)(2,1)S(1)} %bitcast.102), kind=kOutput, calls=%fused_computation | convolution fusion | flops 1812135936 | bytes 12582913 | tf_op jit(solution)/shard_map/dot_general | solution.py:168
  350.3 2.7 collective-permute-start.5
  353.1 2.0 fusion.2
  355.1 5.5 %collective-permute-done.5 = f32[8,32,4608]{2,1,0:T(8,128)S(1)} collective-permute-done((f32[8,32,4608]{2,1,0:T(8,128)S(1)}, f32[8,32,4608]{2,1,0:T(8,128)S(1)}, u32[]{:S(2)}, u32[]{:S(2)}) %collective-permute-start.5) | collective-permute-done | bytes 4718624 | tf_op jit(solution)/shard_map/ppermute | solution.py:37
  360.6 2.8 add.86
  363.4 4.7 %all-to-all-start.11 = ((f32[8,32,4608]{2,1,0:T(8,128)}), f32[8,32,4608]{2,1,0:T(8,128)}, u32[]{:S(2)}, u32[]{:S(2)}) async-start(f32[8,32,4608]{2,1,0:T(8,128)} %add.86), calls=%async_computation.11 | async-start | bytes 9437184 | tf_op jit(solution)/shard_map/all_to_all | solution.py:171
  368.2 54.8 %all-to-all-done.11 = f32[8,32,4608]{2,1,0:T(8,128)} async-done(((f32[8,32,4608]{2,1,0:T(8,128)}), f32[8,32,4608]{2,1,0:T(8,128)}, u32[]{:S(2)}, u32[]{:S(2)}) %all-to-all-start.11) | async-done | bytes 4718624 | tf_op jit(solution)/shard_map/all_to_all | solution.py:171
  422.9 2.8 reduce_sum.69
  425.7 1.7 maximum_minimum_fusion
  (60 shorter events, 5.3 us)
Async XLA Ops:
  7.2 170.8 %copy-start = (bf16[768,1536]{1,0:T(8,128)(2,1)S(1)}, bf16[768,1536]{1,0:T(8,128)(2,1)}, u32[]{:S(2)}) copy-start(bf16[768,1536]{1,0:T(8,128)(2,1)} %param.15) | copy-start | bytes 7077892
  7.2 61.1 %all-gather.2.cloned.1.call-start = ((), (), s32[]{:S(2)}) async-start(), calls=%async_computation.12 | async-start | bytes 7520256 | tf_op jit(solution)/shard_map/all_gather | solution.py:109
  10.8 39.1 %all-to-all-start = ((bf16[8,2,8,4608]{3,2,1,0:T(8,128)(2,1)}), bf16[8,2,8,4608]{3,2,1,0:T(8,128)(2,1)S(1)}, u32[]{:S(2)}, u32[]{:S(2)}) async-start(bf16[8,2,8,4608]{3,2,1,0:T(8,128)(2,1)} %broadcast_in_dim.22), calls=%async_computation | async-start | bytes 2359296 | tf_op jit(solution)/shard_map/all_to_all | solution.py:112
  49.9 12.5 %collective-permute-start = (bf16[8,2,8,4608]{3,2,1,0:T(8,128)(2,1)S(1)}, bf16[8,2,8,4608]{3,2,1,0:T(8,128)(2,1)S(1)}, u32[]{:S(2)}, u32[]{:S(2)}) collective-permute-start(bf16[8,2,8,4608]{3,2,1,0:T(8,128)(2,1)S(1)} %all-to-all-done), channel_id=1, source_target_pairs={{0,8},{8,0},{1,9},{9,1},{2,10},{10,2},{3,11},{11,3},{4,12},{12,4},... | collective-permute-start | bytes 3538952 | tf_op jit(solution)/shard_map/ppermute | solution.py:37
  108.8 4.5 %copy-start.8 = (s32[1536]{0:T(1024)S(1)}, s32[1536]{0:T(1024)}, u32[]{:S(2)}) copy-start(s32[1536]{0:T(1024)} %param.26) | copy-start | bytes 18436
  108.8 22.9 %copy-start.7 = (f32[1536]{0:T(1024)S(1)}, f32[1536]{0:T(1024)}, u32[]{:S(2)}) copy-start(f32[1536]{0:T(1024)} %param.27) | copy-start | bytes 18436
  108.8 22.9 %all-to-all-start.2 = ((f32[8,64,768]{2,1,0:T(8,128)}), f32[8,64,768]{2,1,0:T(8,128)}, u32[]{:S(2)}, u32[]{:S(2)}) async-start(f32[8,64,768]{2,1,0:T(8,128)} %broadcast_in_dim.23), calls=%async_computation.2 | async-start | bytes 3145728 | tf_op jit(solution)/shard_map/all_to_all | solution.py:23
  135.5 7.1 %collective-permute-start.1 = (bf16[8,32,1536]{2,1,0:T(8,128)(2,1)S(1)}, bf16[8,32,1536]{2,1,0:T(8,128)(2,1)S(1)}, u32[]{:S(2)}, u32[]{:S(2)}) collective-permute-start(bf16[8,32,1536]{2,1,0:T(8,128)(2,1)S(1)} %fusion.27), channel_id=1, source_target_pairs={{0,8},{8,0},{1,9},{9,1},{2,10},{10,2},{3,11},{11,3},{4,12},{12,4},... | collective-permute-start | bytes 2359304 | tf_op jit(solution)/shard_map/ppermute | solution.py:37
  173.8 4.0 collective-permute-start.2
  208.0 4.4 %copy-start.5 = (f32[768]{0:T(1024)S(1)}, f32[768]{0:T(1024)}, u32[]{:S(2)}) copy-start(f32[768]{0:T(1024)} %param.25) | copy-start | bytes 9220
  208.0 22.8 %all-to-all-start.6 = ((f32[8,64,768]{2,1,0:T(8,128)}), f32[8,64,768]{2,1,0:T(8,128)}, u32[]{:S(2)}, u32[]{:S(2)}) async-start(f32[8,64,768]{2,1,0:T(8,128)} %broadcast_in_dim.27), calls=%async_computation.6 | async-start | bytes 3145728 | tf_op jit(solution)/shard_map/all_to_all | solution.py:23
  230.8 3.4 copy-start.4
  234.6 1.4 copy-start.3
  236.2 6.5 %collective-permute-start.3 = (f32[8,32,1536]{2,1,0:T(8,128)S(1)}, f32[8,32,1536]{2,1,0:T(8,128)S(1)}, u32[]{:S(2)}, u32[]{:S(2)}) collective-permute-start(f32[8,32,1536]{2,1,0:T(8,128)S(1)} %select_bitcast_fusion), channel_id=1, source_target_pairs={{0,8},{8,0},{1,9},{9,1},{2,10},{10,2},{3,11},{11,3},{4,12},{12,4},... | collective-permute-start | bytes 4718600 | tf_op jit(solution)/shard_map/ppermute | solution.py:37
  289.3 5.3 %collective-permute-start.4 = (f32[8,32,1536]{2,1,0:T(8,128)S(1)}, f32[8,32,1536]{2,1,0:T(8,128)S(1)}, u32[]{:S(2)}, u32[]{:S(2)}) collective-permute-start(f32[8,32,1536]{2,1,0:T(8,128)S(1)} %all_to_all.65), channel_id=1, source_target_pairs={{0,8},{8,0},{1,9},{9,1},{2,10},{10,2},{3,11},{11,3},{4,12},{12,4},... | collective-permute-start | bytes 4718600 | tf_op jit(solution)/shard_map/ppermute | solution.py:37
  300.7 4.5 %copy-start.6 = (f32[768]{0:T(1024)S(1)}, f32[768]{0:T(1024)}, u32[]{:S(2)}) copy-start(f32[768]{0:T(1024)} %param.24) | copy-start | bytes 9220
  300.7 25.1 %all-to-all-start.9 = ((f32[8,64,768]{2,1,0:T(8,128)}), f32[8,64,768]{2,1,0:T(8,128)S(1)}, u32[]{:S(2)}, u32[]{:S(2)}) async-start(f32[8,64,768]{2,1,0:T(8,128)} %fusion.9), calls=%async_computation.9 | async-start | bytes 3145728 | tf_op jit(solution)/shard_map/all_to_all | solution.py:16
  327.0 26.1 %slice-start = ((s8[7077888]{0:T(1024)(128)(4,1)}), s8[4194304]{0:T(1024)(128)(4,1)S(1)}, s32[]{:S(2)}) async-start(s8[7077888]{0:T(1024)(128)(4,1)} %bitcast.95), calls=%async_computation.13 | async-start | bytes 8388608
  345.1 7.9 %slice-start.1 = ((s8[7077888]{0:T(1024)(128)(4,1)}), s8[2883584]{0:T(1024)(128)(4,1)S(1)}, s32[]{:S(2)}) async-start(s8[7077888]{0:T(1024)(128)(4,1)} %bitcast.95), calls=%async_computation.14 | async-start | bytes 5767168
  350.3 10.3 %collective-permute-start.5 = (f32[8,32,4608]{2,1,0:T(8,128)S(1)}, f32[8,32,4608]{2,1,0:T(8,128)S(1)}, u32[]{:S(2)}, u32[]{:S(2)}) collective-permute-start(f32[8,32,4608]{2,1,0:T(8,128)S(1)} %fusion), channel_id=1, source_target_pairs={{0,8},{8,0},{1,9},{9,1},{2,10},{10,2},{3,11},{11,3},{4,12},{12,4},... | collective-permute-start | bytes 14155784 | tf_op jit(solution)/shard_map/ppermute | solution.py:37
  363.4 4.7 %copy-start.10 = (f32[32]{0:T(128)S(1)}, f32[32]{0:T(128)}, u32[]{:S(2)}) copy-start(f32[32]{0:T(128)} %param.21) | copy-start | bytes 388
  363.4 4.8 %copy-start.11 = (f32[32]{0:T(128)S(1)}, f32[32]{0:T(128)}, u32[]{:S(2)}) copy-start(f32[32]{0:T(128)} %param.20) | copy-start | bytes 388
  363.4 59.6 %all-to-all-start.11 = ((f32[8,32,4608]{2,1,0:T(8,128)}), f32[8,32,4608]{2,1,0:T(8,128)}, u32[]{:S(2)}, u32[]{:S(2)}) async-start(f32[8,32,4608]{2,1,0:T(8,128)} %add.86), calls=%async_computation.11 | async-start | bytes 9437184 | tf_op jit(solution)/shard_map/all_to_all | solution.py:171
  368.1 57.6 %copy-start.9 = (f32[32]{0:T(128)}, f32[32]{0:T(128)S(1)}, u32[]{:S(2)}) copy-start(f32[32]{0:T(128)S(1)} %multiply_add_fusion) | copy-start | bytes 388
  368.2 57.6 %copy-start.2 = (f32[32,4608]{1,0:T(8,128)S(1)}, f32[32,4608]{1,0:T(8,128)}, u32[]{:S(2)}) copy-start(f32[32,4608]{1,0:T(8,128)} %param.16) | copy-start | bytes 1769476
  422.9 4.5 %copy-start.1 = (bf16[768,1536]{1,0:T(8,128)(2,1)S(1)}, bf16[768,1536]{1,0:T(8,128)(2,1)}, u32[]{:S(2)}) copy-start(bf16[768,1536]{1,0:T(8,128)(2,1)} %param.15) | copy-start | bytes 7077892
Sparse Core Ops, SparseCore 0:
  10.2 57.9 all-gather.1
